TPU v7x, 128 devices: a whole 4x4x4 slice. The times are simulated.
128 devices in a mesh: grp: 4 (over x), tok: 32 (over z, y, core).
Axes of the slice: x: 4, y: 4, z: 4, core: 2. Of those that a mesh axis runs over, the one named last changes fastest.
Arguments:
- tokens: bfloat16 [16384, 2560], P(('grp', 'tok')), may hold values from -6 to 6
- input_gain: bfloat16 [2560], replicated, may hold values from 0.25 to 1.75
- query_down: bfloat16 [2560, 768], replicated, may hold values from -0.125 to 0.125
- query_gain: bfloat16 [768], replicated, may hold values from 0.25 to 1.75
- query_up: bfloat16 [768, 1920], replicated, may hold values from -0.21875 to 0.21875
- latent_down: bfloat16 [2560, 288], replicated, may hold values from -0.125 to 0.125
- latent_gain: bfloat16 [256], replicated, may hold values from 0.25 to 1.75
- key_up: bfloat16 [256, 1280], replicated, may hold values from -0.375 to 0.375
- value_up: bfloat16 [256, 1280], replicated, may hold values from -0.375 to 0.375
- output_weight: bfloat16 [1280, 2560], replicated, may hold values from -0.15625 to 0.15625
- post_gain: bfloat16 [2560], replicated, may hold values from 0.25 to 1.75
- gate_weight: bfloat16 [2560, 3200], P('tok', 'grp'), may hold values from -0.125 to 0.125
- up_weight: bfloat16 [2560, 3200], P('tok', 'grp'), may hold values from -0.125 to 0.125
- down_weight: bfloat16 [3200, 2560], P('grp', 'tok'), may hold values from -0.109375 to 0.109375
- cache_latents: bfloat16 [16, 4096, 288], P('grp', 'tok'), as said below
- prompt_latents: bfloat16 [8, 1024, 288], P(None, 'tok'), as said below
- cache_len: int32 [16], replicated, may hold values from 1 to 4096, 32768 in all
- prompt_len: int32 [8], replicated, may hold values from 1 to 1024, 4096 in all
- prompt_of: int32 [16], replicated, may hold values from 0 to 7
Outputs:
- layer_out: bfloat16 [16384, 2560], P(('grp', 'tok'))
- new_latents: bfloat16 [16384, 288], P(('grp', 'tok'))
Inputs may be any that keep to these rules, and one draw needn't show every extreme that they name: `cache_len`: some request has exactly 4096 live cached rows. `prompt_len`: some stored prompt has exactly 1024 live rows. `cache_latents`: rows past a request's live length are stored but never read. `prompt_latents`: rows past a prompt's live length are stored but never read.
All inputs are finite; a program needn't handle non-finite values.
Results may differ from a plain program's by a relative error of at most 0.02.
Values may be sent and summed in bfloat16 or wider, within the bound.
No kernel may reach another device: no remote copies, remote signals or barrier semaphores. Data moves between devices by JAX's collectives and lax.ppermute only.
A program may use at most 128 MiB of HBM per device.

v0:
```python
import jax
import jax.numpy as jnp
from jax import lax
from jax.sharding import PartitionSpec as P

KVR = 256
HEADS = 20
NOPE = 64
ROPE = 32
VDIM = 64
SPAN = 1024


EPSILON = 1e-06


def passed_along(block, axis, distance):
    devices = range(lax.axis_size(axis))
    route = [(i - distance, i) for i in devices if i - distance in devices]
    return lax.ppermute(block, axis, route)


def norm_rows(values, gain_vector):
    mean_square = jnp.mean(values * values, axis=-1, keepdims=True)
    return values * lax.rsqrt(mean_square + EPSILON) * gain_vector.astype(jnp.float32)


def rotate(values, positions):
    half_width = values.shape[-1] // 2
    frequency = 10000.0 ** (-jnp.arange(half_width, dtype=jnp.float32) / half_width)
    angles = positions.astype(jnp.float32)[:, None] * frequency[None, :]
    if values.ndim == 3:
        angles = angles[:, None, :]
    cosine = jnp.cos(angles)
    sine_part = jnp.sin(angles)
    leading = values[..., :half_width]
    trailing = values[..., half_width:]
    return jnp.concatenate(
        [leading * cosine - trailing * sine_part, trailing * cosine + leading * sine_part], axis=-1
    )


def attend_segment(
    softmax_state, queries, key_rows, lowers, limits, block_count, key_block, score_scale
):

    def fold_block(step_index, carried):
        running_max, running_sum, running_out = carried
        first_key = step_index * key_block
        key_piece = lax.dynamic_slice_in_dim(key_rows, first_key, key_block, 0)
        scores = (
            jnp.einsum("rw,kw->rk", queries, key_piece, preferred_element_type=jnp.float32)
            * score_scale
        )
        key_place = (first_key + jnp.arange(key_block, dtype=jnp.int32))[None, :]
        live_keys = jnp.logical_and(key_place >= lowers[:, None], key_place < limits[:, None])
        next_max = jnp.maximum(running_max, jnp.max(jnp.where(live_keys, scores, -1e30), axis=1))
        weights = jnp.where(live_keys, jnp.exp(scores - next_max[:, None]), 0.0)
        factor = jnp.exp(running_max - next_max)
        running_sum = running_sum * factor + jnp.sum(weights, axis=1)
        running_out = running_out * factor[:, None] + jnp.dot(
            weights.astype(jnp.bfloat16), key_piece[:, :KVR], preferred_element_type=jnp.float32
        )
        return (next_max, running_sum, running_out)

    return lax.fori_loop(0, block_count, fold_block, softmax_state)


def body(
    tokens,
    input_gain,
    query_down,
    query_gain,
    query_up,
    latent_down,
    latent_gain,
    key_up,
    value_up,
    output_weight,
    post_gain,
    gate_weight,
    up_weight,
    down_weight,
    cache_latents,
    prompt_latents,
    cache_len,
    prompt_len,
    prompt_of,
):
    group_index = lax.axis_index("grp")
    shard_index = lax.axis_index("tok")
    tok_dev = tokens.shape[0]
    tok_count = lax.axis_size("tok")
    group_requests = tok_dev * tok_count // SPAN
    local_request = shard_index % group_requests
    owner = group_index * group_requests + local_request
    offset = shard_index // group_requests * tok_dev
    within = offset + jnp.arange(tok_dev, dtype=jnp.int32)
    own_prompt = prompt_of[owner]
    prompt_live = prompt_len[own_prompt]
    cache_live = cache_len[owner]
    positions = prompt_live + cache_live + within
    normed = norm_rows(tokens.astype(jnp.float32), input_gain).astype(jnp.bfloat16)
    query_latent = norm_rows(
        jnp.dot(normed, query_down, preferred_element_type=jnp.float32), query_gain
    ).astype(jnp.bfloat16)
    query_full = jnp.dot(query_latent, query_up, preferred_element_type=jnp.float32).astype(
        jnp.bfloat16
    )
    query_full = lax.optimization_barrier(query_full).reshape(tok_dev, HEADS, NOPE + ROPE)
    absorbed = jnp.einsum(
        "thd,khd->thk",
        query_full[..., :NOPE],
        key_up.reshape(KVR, HEADS, NOPE),
        preferred_element_type=jnp.float32,
    )
    turned = rotate(query_full[..., NOPE:].astype(jnp.float32), positions)
    queries = jnp.concatenate([absorbed, turned], axis=-1).astype(jnp.bfloat16)
    latent_raw = jnp.dot(normed, latent_down, preferred_element_type=jnp.float32)
    new_latents = jnp.concatenate(
        [norm_rows(latent_raw[:, :KVR], latent_gain), rotate(latent_raw[:, KVR:], positions)],
        axis=-1,
    ).astype(jnp.bfloat16)
    latent_width = new_latents.shape[1]
    shards_back = SPAN // tok_dev
    earlier_pieces = []
    passing = new_latents
    for back in range(1, shards_back):
        passing = passed_along(passing, "tok", group_requests)
        earlier_pieces.insert(0, passing)
    span_rows = jnp.concatenate(earlier_pieces + [new_latents], axis=0)
    lead_rows = (shards_back - 1) * tok_dev
    span_lower = jnp.broadcast_to(lead_rows - offset, (tok_dev,))
    span_limit = lead_rows + 1 + jnp.arange(tok_dev, dtype=jnp.int32)
    cache_all, prompt_all = (
        lax.all_gather(cache_latents, "tok", axis=1, tiled=True),
        lax.all_gather(prompt_latents, "tok", axis=1, tiled=True),
    )
    cache_rows = lax.dynamic_index_in_dim(cache_all, local_request, 0, keepdims=False)
    prompt_rows = lax.dynamic_index_in_dim(prompt_all, own_prompt, 0, keepdims=False)
    query_rows = queries.reshape(tok_dev * HEADS, latent_width)
    row_count = tok_dev * HEADS
    score_scale = 1.0 / (NOPE + ROPE) ** 0.5
    softmax_state = (
        jnp.full((row_count,), -1e30, jnp.float32),
        jnp.zeros((row_count,), jnp.float32),
        jnp.zeros((row_count, KVR), jnp.float32),
    )
    no_lower = jnp.zeros((tok_dev,), jnp.int32)
    segments = (
        (prompt_rows, no_lower, jnp.broadcast_to(prompt_live, (tok_dev,))),
        (cache_rows, no_lower, jnp.broadcast_to(cache_live, (tok_dev,))),
        (span_rows, span_lower, span_limit),
    )
    for key_rows, token_lower, token_limit in segments:
        lowers = jnp.repeat(token_lower, HEADS)
        limits = jnp.repeat(token_limit, HEADS)
        key_block = min(512, key_rows.shape[0])
        block_count = key_rows.shape[0] // key_block
        softmax_state = attend_segment(
            softmax_state, query_rows, key_rows, lowers, limits, block_count, key_block, score_scale
        )
    running_max, running_sum, running_out = softmax_state
    latent_out = (
        (running_out / running_sum[:, None]).astype(jnp.bfloat16).reshape(tok_dev, HEADS, KVR)
    )
    heads_out = (
        jnp.einsum(
            "thk,khv->thv",
            latent_out,
            value_up.reshape(KVR, HEADS, VDIM),
            preferred_element_type=jnp.float32,
        )
        .astype(jnp.bfloat16)
        .reshape(tok_dev, HEADS * VDIM)
    )
    attended = jnp.dot(heads_out, output_weight, preferred_element_type=jnp.float32)
    residual = lax.optimization_barrier(
        (tokens.astype(jnp.float32) + attended).astype(jnp.bfloat16)
    )
    post_norm = norm_rows(residual.astype(jnp.float32), post_gain).astype(jnp.bfloat16)
    rows_all = lax.all_gather(post_norm, "grp", axis=0, tiled=True)
    gate_values = jnp.dot(
        rows_all,
        lax.all_gather(gate_weight, "tok", axis=0, tiled=True),
        preferred_element_type=jnp.float32,
    )
    up_values = jnp.dot(
        rows_all,
        lax.all_gather(up_weight, "tok", axis=0, tiled=True),
        preferred_element_type=jnp.float32,
    )
    hidden = (jax.nn.silu(gate_values) * up_values).astype(jnp.bfloat16)
    partial_out = jnp.dot(
        hidden,
        lax.all_gather(down_weight, "tok", axis=1, tiled=True),
        preferred_element_type=jnp.float32,
    )
    down_values = lax.psum_scatter(
        partial_out.astype(jnp.bfloat16), "grp", scatter_dimension=0, tiled=True
    ).astype(jnp.float32)
    layer_out = (residual.astype(jnp.float32) + down_values).astype(jnp.bfloat16)
    return (layer_out, new_latents)


def solution(mesh):
    in_specs = (
        P(("grp", "tok"), None),
        P(),
        P(),
        P(),
        P(),
        P(),
        P(),
        P(),
        P(),
        P(),
        P(),
        P("tok", "grp"),
        P("tok", "grp"),
        P("grp", "tok"),
        P("grp", "tok", None),
        P(None, "tok", None),
        P(),
        P(),
        P(),
    )
    out_specs = (P(("grp", "tok"), None), P(("grp", "tok"), None))
    return jax.shard_map(body, mesh=mesh, in_specs=in_specs, out_specs=out_specs, check_vma=False)
```

profile of v0, /device:TPU:8, one launch (start us, length us, event | category | flops | bytes accessed | tf_op | source)
XLA Modules:
  0.0 411.9 jit_solution(16430526760427926107)
XLA Ops:
  20.9 4.8 %collective-permute-start = (bf16[128,288]{0,1:T(8,128)(2,1)S(1)}, bf16[128,288]{0,1:T(8,128)(2,1)}, u32[]{:S(2)}, u32[]{:S(2)}) collective-permute-start(bf16[128,288]{0,1:T(8,128)(2,1)S(1)} %pad_maximum_fusion.1), channel_id=1, source_target_pairs={{0,4},{1,5},{2,6},{3,7},{4,8},{5,9},{6,10},{7,11},{8,12},{9,13},{1... | collective-permute-start | bytes 221192 | tf_op jit(solution)/shard_map/ppermute | solution.py:20
  28.9 4.7 %collective-permute-start.1 = (bf16[128,288]{0,1:T(8,128)(2,1)}, bf16[128,288]{0,1:T(8,128)(2,1)}, u32[]{:S(2)}, u32[]{:S(2)}) collective-permute-start(bf16[128,288]{0,1:T(8,128)(2,1)} %collective-permute-done), channel_id=1, source_target_pairs={{0,4},{1,5},{2,6},{3,7},{4,8},{5,9},{6,10},{7,11},{8,12},{9,13},{1... | collective-permute-start | bytes 221192 | tf_op jit(solution)/shard_map/ppermute | solution.py:20
  35.9 5.2 %collective-permute-start.2 = (bf16[128,288]{0,1:T(8,128)(2,1)}, bf16[128,288]{0,1:T(8,128)(2,1)S(1)}, u32[]{:S(2)}, u32[]{:S(2)}) collective-permute-start(bf16[128,288]{0,1:T(8,128)(2,1)} %collective-permute-done.1), channel_id=1, source_target_pairs={{0,4},{1,5},{2,6},{3,7},{4,8},{5,9},{6,10},{7,11},{8,12},{9,13},{1... | collective-permute-start | bytes 221192 | tf_op jit(solution)/shard_map/ppermute | solution.py:20
  43.3 7.5 %collective-permute-start.3 = (bf16[128,288]{0,1:T(8,128)(2,1)S(1)}, bf16[128,288]{0,1:T(8,128)(2,1)S(1)}, u32[]{:S(2)}, u32[]{:S(2)}) collective-permute-start(bf16[128,288]{0,1:T(8,128)(2,1)S(1)} %collective-permute-done.2), channel_id=1, source_target_pairs={{0,4},{1,5},{2,6},{3,7},{4,8},{5,9},{6,10},{7,11},{8,12},{9,13},{1... | collective-permute-start | bytes 221192 | tf_op jit(solution)/shard_map/ppermute | solution.py:20
  54.1 7.0 %collective-permute-start.4 = (bf16[128,288]{0,1:T(8,128)(2,1)S(1)}, bf16[128,288]{0,1:T(8,128)(2,1)S(1)}, u32[]{:S(2)}, u32[]{:S(2)}) collective-permute-start(bf16[128,288]{0,1:T(8,128)(2,1)S(1)} %collective-permute-done.3), channel_id=1, source_target_pairs={{0,4},{1,5},{2,6},{3,7},{4,8},{5,9},{6,10},{7,11},{8,12},{9,13},{1... | collective-permute-start | bytes 221192 | tf_op jit(solution)/shard_map/ppermute | solution.py:20
  66.8 6.8 %collective-permute-start.5 = (bf16[128,288]{0,1:T(8,128)(2,1)S(1)}, bf16[128,288]{0,1:T(8,128)(2,1)S(1)}, u32[]{:S(2)}, u32[]{:S(2)}) collective-permute-start(bf16[128,288]{0,1:T(8,128)(2,1)S(1)} %collective-permute-done.4), channel_id=1, source_target_pairs={{0,4},{1,5},{2,6},{3,7},{4,8},{5,9},{6,10},{7,11},{8,12},{9,13},{1... | collective-permute-start | bytes 221192 | tf_op jit(solution)/shard_map/ppermute | solution.py:20
  92.8 26.4 %while.56 = (s32[]{:T(128)}, f32[2560]{0:T(1024)S(1)}, f32[2560]{0:T(1024)S(1)}, f32[2560,256]{1,0:T(8,128)S(1)}, bf16[1024,288]{1,0:T(8,128)(2,1)}, /*index=5*/...) while((s32[]{:T(128)}, f32[2560]{0:T(1024)S(1)}, ...), condition=%wide.region_5.6_spmd.clone, body=%wide.region_2.5_spmd.clone.sunk | while | flops 1439840768 | bytes 44730576 | solution.py:66
  93.3 5.7 %fusion.130 = (f32[2560]{0:T(1024)S(1)}, f32[512,2560]{1,0:T(8,128)}) fusion(pred[512]{0:T(512)(128)(4,1)S(1)} %fusion.129, bf16[2560,288]{1,0:T(8,128)(2,1)} %get-tuple-element.733, bf16[1024,288]{1,0:T(8,128)(2,1)} %get-tuple-element.732, s32[]{:T(128)S(6)} %select_n.152), kind=kOutput, calls=%fused_computation.53.clone.1 | convolution fusion | flops 758904320 | bytes 7612932 | tf_op jit(solution)/shard_map/while/body/eval_jaxpr/rw,kw->rk/dot_general | solution.py:52
  99.0 3.7 fusion.131
  106.7 5.6 %fusion.130 = (f32[2560]{0:T(1024)S(1)}, f32[512,2560]{1,0:T(8,128)}) fusion(pred[512]{0:T(512)(128)(4,1)S(1)} %fusion.129, bf16[2560,288]{1,0:T(8,128)(2,1)} %get-tuple-element.733, bf16[1024,288]{1,0:T(8,128)(2,1)} %get-tuple-element.732, s32[]{:T(128)S(6)} %select_n.152), kind=kOutput, calls=%fused_computation.53.clone.1 | convolution fusion | flops 758904320 | bytes 7612932 | tf_op jit(solution)/shard_map/while/body/eval_jaxpr/rw,kw->rk/dot_general | solution.py:52
  112.3 3.5 fusion.131
  119.2 7.7 %all-gather.9.cloned.1.call-done = bf16[4,4096,288]{1,2,0:T(8,128)(2,1)} async-done(((bf16[4,128,288]{1,2,0:T(8,128)(2,1)}), bf16[4,4096,288]{1,2,0:T(8,128)(2,1)}) %all-gather.9.cloned.1.call-update) | async-done | bytes 9437200 | tf_op jit(solution)/shard_map/all_gather | solution.py:136
  127.0 3.3 constant_dynamic-slice_fusion
  130.3 4.5 %copy.36 = bf16[1,4096,288]{2,1,0:T(8,128)(2,1)} copy(bf16[1,4096,288]{1,2,0:T(8,128)(2,1)} %constant_dynamic-slice_fusion) | data formatting | bytes 4718592 | tf_op jit(solution)/shard_map/jit(dynamic_index_in_dim)/dynamic_slice | solution.py:139
  134.8 62.1 %while.54 = (s32[]{:T(128)}, f32[2560]{0:T(1024)S(1)}, f32[2560]{0:T(1024)S(1)}, f32[2560,256]{1,0:T(8,128)S(1)}, bf16[4096,288]{1,0:T(8,128)(2,1)}, /*index=5*/...) while((s32[]{:T(128)}, f32[2560]{0:T(1024)S(1)}, ...), condition=%wide.region_9.10_spmd.clone, body=%wide.region_6.9_spmd.clone.sunk | while | flops 1439177728 | bytes 23759020 | solution.py:66
  135.4 3.3 fusion.119
  150.8 3.3 fusion.119
  158.6 3.7 fusion.119
  166.6 3.3 fusion.119
  174.4 3.3 fusion.119
  182.1 3.3 fusion.119
  189.8 3.3 fusion.119
  196.9 19.1 %while.55 = (s32[]{:T(128)}, f32[2560]{0:T(1024)S(1)}, f32[2560]{0:T(1024)S(1)}, f32[2560,256]{1,0:T(8,128)S(1)}, bf16[1024,288]{0,1:T(8,128)(2,1)}, /*index=5*/...) while((s32[]{:T(128)}, f32[2560]{0:T(1024)S(1)}, ...), condition=%wide.region_14.15_spmd.clone, body=%wide.region_11.14_spmd.clone.sunk | while | flops 1447041536 | bytes 23730872 | solution.py:66
  197.4 4.0 fusion.124
  206.8 4.0 fusion.124
  220.5 3.9 fusion.59
  227.3 33.4 %all-gather.11.cloned.1.call-done = bf16[512,2560]{1,0:T(8,128)(2,1)} async-done(((bf16[128,2560]{1,0:T(8,128)(2,1)}), bf16[512,2560]{1,0:T(8,128)(2,1)}) %all-gather.11.cloned.1.call-update) | async-done | bytes 2621456 | tf_op jit(solution)/shard_map/all_gather | solution.py:182
  260.6 6.7 %fusion.81 = f32[512,800]{0,1:T(8,128)} fusion(bf16[512,2560]{1,0:T(8,128)(2,1)} %all-gather.11.cloned.1.call-done, bf16[2560,800]{1,0:T(8,128)(2,1)} %all-gather.13.cloned.1.call-done), kind=kOutput, calls=%fused_computation.136 | convolution fusion | flops 2097152000 | bytes 8355840 | tf_op jit(solution)/shard_map/dot_general | solution.py:183
  267.3 41.9 %all-gather.15.cloned.1.call-done = bf16[2560,800]{1,0:T(8,128)(2,1)} async-done(((bf16[80,800]{1,0:T(8,128)(2,1)}), bf16[2560,800]{1,0:T(8,128)(2,1)}) %all-gather.15.cloned.1.call-update) | async-done | bytes 4096016 | tf_op jit(solution)/shard_map/all_gather | solution.py:190
  309.3 48.1 %all-gather.17.cloned.1.call-done = bf16[800,2560]{0,1:T(8,128)(2,1)} async-done(((bf16[800,80]{0,1:T(8,128)(2,1)}), bf16[800,2560]{0,1:T(8,128)(2,1)}) %all-gather.17.cloned.1.call-update) | async-done | bytes 4096016 | tf_op jit(solution)/shard_map/all_gather | solution.py:196
  357.3 11.8 %convolution_convert_fusion = bf16[512,2560]{1,0:T(8,128)(2,1)} fusion(bf16[800,2560]{0,1:T(8,128)(2,1)} %all-gather.17.cloned.1.call-done, f32[512,800]{0,1:T(8,128)} %fusion.81, bf16[512,2560]{1,0:T(8,128)(2,1)} %all-gather.11.cloned.1.call-done, bf16[2560,800]{1,0:T(8,128)(2,1)} %all-gather.15.cloned.1.call-done), kind=kOutput, calls=%fused_computation.77 | convolution fusion | flops 4198072320 | bytes 15073280 | tf_op jit(solution)/shard_map/dot_general | solution.py:194
  369.1 33.7 %reduce-scatter.2.cloned.1.call-done = bf16[128,2560]{1,0:T(8,128)(2,1)} async-done(((bf16[512,2560]{1,0:T(8,128)(2,1)}), bf16[128,2560]{1,0:T(8,128)(2,1)}) %reduce-scatter.2.cloned.1.call-update) | async-done | bytes 655376 | tf_op jit(solution)/shard_map/reduce_scatter | solution.py:199
  (176 shorter events, 112.3 us)
Async XLA Ops:
  7.2 26.4 %copy-start = (bf16[768,1920]{1,0:T(8,128)(2,1)S(1)}, bf16[768,1920]{1,0:T(8,128)(2,1)}, u32[]{:S(2)}) copy-start(bf16[768,1920]{1,0:T(8,128)(2,1)} %param.29) | copy-start | bytes 8847364
  7.2 83.5 %all-gather.7.cloned.1.call-start = ((), (), s32[]{:S(2)}) async-start(), calls=%async_computation.1 | async-start | bytes 6488064 | tf_op jit(solution)/shard_map/all_gather | solution.py:137
  7.9 119.0 %all-gather.9.cloned.1.call-start = ((), (), s32[]{:S(2)}) async-start(), calls=%async_computation.2 | async-start | bytes 9732096 | tf_op jit(solution)/shard_map/all_gather | solution.py:136
  8.7 218.6 %all-gather.13.cloned.1.call-start = ((), (), s32[]{:S(2)}) async-start(), calls=%async_computation.4 | async-start | bytes 4730880 | tf_op jit(solution)/shard_map/all_gather | solution.py:185
  20.8 8.1 %copy-start.8 = (bf16[768]{0:T(1024)(128)(2,1)S(1)}, bf16[768]{0:T(1024)(128)(2,1)}, u32[]{:S(2)}) copy-start(bf16[768]{0:T(1024)(128)(2,1)} %param.28) | copy-start | bytes 4612
  20.8 12.8 %copy-start.6 = (bf16[128,288]{0,1:T(8,128)(2,1)}, bf16[128,288]{0,1:T(8,128)(2,1)S(1)}, u32[]{:S(2)}) copy-start(bf16[128,288]{0,1:T(8,128)(2,1)S(1)} %pad_maximum_fusion.1) | copy-start | bytes 221188
  20.9 8.1 %collective-permute-start = (bf16[128,288]{0,1:T(8,128)(2,1)S(1)}, bf16[128,288]{0,1:T(8,128)(2,1)}, u32[]{:S(2)}, u32[]{:S(2)}) collective-permute-start(bf16[128,288]{0,1:T(8,128)(2,1)S(1)} %pad_maximum_fusion.1), channel_id=1, source_target_pairs={{0,4},{1,5},{2,6},{3,7},{4,8},{5,9},{6,10},{7,11},{8,12},{9,13},{1... | collective-permute-start | bytes 221192 | tf_op jit(solution)/shard_map/ppermute | solution.py:20
  25.7 234.9 %all-gather.11.cloned.1.call-start = ((), (), s32[]{:S(2)}) async-start(), calls=%async_computation.3 | async-start | bytes 3276800 | tf_op jit(solution)/shard_map/all_gather | solution.py:182
  28.9 6.9 %collective-permute-start.1 = (bf16[128,288]{0,1:T(8,128)(2,1)}, bf16[128,288]{0,1:T(8,128)(2,1)}, u32[]{:S(2)}, u32[]{:S(2)}) collective-permute-start(bf16[128,288]{0,1:T(8,128)(2,1)} %collective-permute-done), channel_id=1, source_target_pairs={{0,4},{1,5},{2,6},{3,7},{4,8},{5,9},{6,10},{7,11},{8,12},{9,13},{1... | collective-permute-start | bytes 221192 | tf_op jit(solution)/shard_map/ppermute | solution.py:20
  35.9 7.5 %collective-permute-start.2 = (bf16[128,288]{0,1:T(8,128)(2,1)}, bf16[128,288]{0,1:T(8,128)(2,1)S(1)}, u32[]{:S(2)}, u32[]{:S(2)}) collective-permute-start(bf16[128,288]{0,1:T(8,128)(2,1)} %collective-permute-done.1), channel_id=1, source_target_pairs={{0,4},{1,5},{2,6},{3,7},{4,8},{5,9},{6,10},{7,11},{8,12},{9,13},{1... | collective-permute-start | bytes 221192 | tf_op jit(solution)/shard_map/ppermute | solution.py:20
  43.3 10.8 %collective-permute-start.3 = (bf16[128,288]{0,1:T(8,128)(2,1)S(1)}, bf16[128,288]{0,1:T(8,128)(2,1)S(1)}, u32[]{:S(2)}, u32[]{:S(2)}) collective-permute-start(bf16[128,288]{0,1:T(8,128)(2,1)S(1)} %collective-permute-done.2), channel_id=1, source_target_pairs={{0,4},{1,5},{2,6},{3,7},{4,8},{5,9},{6,10},{7,11},{8,12},{9,13},{1... | collective-permute-start | bytes 221192 | tf_op jit(solution)/shard_map/ppermute | solution.py:20
  54.1 12.6 %collective-permute-start.4 = (bf16[128,288]{0,1:T(8,128)(2,1)S(1)}, bf16[128,288]{0,1:T(8,128)(2,1)S(1)}, u32[]{:S(2)}, u32[]{:S(2)}) collective-permute-start(bf16[128,288]{0,1:T(8,128)(2,1)S(1)} %collective-permute-done.3), channel_id=1, source_target_pairs={{0,4},{1,5},{2,6},{3,7},{4,8},{5,9},{6,10},{7,11},{8,12},{9,13},{1... | collective-permute-start | bytes 221192 | tf_op jit(solution)/shard_map/ppermute | solution.py:20
  66.7 12.0 %copy-start.7 = (bf16[2560]{0:T(1024)(128)(2,1)S(1)}, bf16[2560]{0:T(1024)(128)(2,1)}, u32[]{:S(2)}) copy-start(bf16[2560]{0:T(1024)(128)(2,1)} %param.35) | copy-start | bytes 15364
  66.8 12.0 %collective-permute-start.5 = (bf16[128,288]{0,1:T(8,128)(2,1)S(1)}, bf16[128,288]{0,1:T(8,128)(2,1)S(1)}, u32[]{:S(2)}, u32[]{:S(2)}) collective-permute-start(bf16[128,288]{0,1:T(8,128)(2,1)S(1)} %collective-permute-done.4), channel_id=1, source_target_pairs={{0,4},{1,5},{2,6},{3,7},{4,8},{5,9},{6,10},{7,11},{8,12},{9,13},{1... | collective-permute-start | bytes 221192 | tf_op jit(solution)/shard_map/ppermute | solution.py:20
  78.8 4.9 %collective-permute-start.6 = (bf16[128,288]{0,1:T(8,128)(2,1)S(1)}, bf16[128,288]{0,1:T(8,128)(2,1)S(1)}, u32[]{:S(2)}, u32[]{:S(2)}) collective-permute-start(bf16[128,288]{0,1:T(8,128)(2,1)S(1)} %collective-permute-done.5), channel_id=1, source_target_pairs={{0,4},{1,5},{2,6},{3,7},{4,8},{5,9},{6,10},{7,11},{8,12},{9,13},{1... | collective-permute-start | bytes 221192 | tf_op jit(solution)/shard_map/ppermute | solution.py:20
  99.0 4.2 %copy-start.2 = (f32[512,2560]{1,0:T(8,128)S(1)}, f32[512,2560]{1,0:T(8,128)}, u32[]{:S(2)}) copy-start(f32[512,2560]{1,0:T(8,128)} %get-tuple-element.703) | copy-start | bytes 15728644 | tf_op jit(solution)/shard_map/while
  112.3 4.0 copy-start.2
  217.6 2.3 copy-start.5
  217.6 2.9 copy-start.4
  224.4 42.9 %copy-start.3 = (bf16[128,2560]{1,0:T(8,128)(2,1)}, bf16[128,2560]{1,0:T(8,128)(2,1)S(1)}, u32[]{:S(2)}) copy-start(bf16[128,2560]{1,0:T(8,128)(2,1)S(1)} %fusion.59) | copy-start | bytes 1966084
  225.8 83.5 %all-gather.15.cloned.1.call-start = ((), (), s32[]{:S(2)}) async-start(), calls=%async_computation.5 | async-start | bytes 4730880 | tf_op jit(solution)/shard_map/all_gather | solution.py:190
  226.3 131.0 %all-gather.17.cloned.1.call-start = ((), (), s32[]{:S(2)}) async-start(), calls=%async_computation.6 | async-start | bytes 4730880 | tf_op jit(solution)/shard_map/all_gather | solution.py:196
  226.9 175.9 %reduce-scatter.2.cloned.1.call-start = ((), (), s32[]{:S(2)}) async-start(), calls=%async_computation.7 | async-start | bytes 3276800 | tf_op jit(solution)/shard_map/reduce_scatter | solution.py:199
  357.3 47.8 %copy-start.1 = (bf16[768,1920]{1,0:T(8,128)(2,1)S(1)}, bf16[768,1920]{1,0:T(8,128)(2,1)}, u32[]{:S(2)}) copy-start(bf16[768,1920]{1,0:T(8,128)(2,1)} %param.29) | copy-start | bytes 8847364
Sparse Core Ops, SparseCore 0:
  10.3 52.6 all-gather.6
  65.2 61.7 all-gather.8
  129.3 46.2 all-gather.12
  225.9 34.7 all-gather.10
  262.8 46.3 all-gather.14
  311.4 45.8 all-gather.16
  369.3 33.5 reduce-scatter.1
where the time goes:
time: 415 us; the launch traced here: 412 us
  waiting for transfers between devices  174 us (42%)
  matrix products  109 us (26%)
  starting transfers between devices  39.6 us (10%)
  other arithmetic  37.3 us (9%)
  local copies, waits for them, and re-layouts  33 us (8%)
  between operations  17.6 us (4%)
    all_gather x1, waiting for transfers between devices, body(): lax.all_gather(down_weight, 'tok', axis=1, tiled=True)  48.1 us
    dot_general x12, matrix products, fold_block(): jnp.einsum('rw,kw->rk', queries, key_piece, preferred_element_type=jnp.fl...  46.2 us
    all_gather x1, waiting for transfers between devices, body(): lax.all_gather(up_weight, 'tok', axis=0, tiled=True)  41.9 us
    ppermute x7, starting transfers between devices, passed_along(): return lax.ppermute(block, axis, route)  39.1 us
    reduce_scatter x1, waiting for transfers between devices, body(): lax.psum_scatter(partial_out.astype(jnp.bfloat16), 'grp', scatter_dimensi...  33.7 us
    dot_general x12, matrix products, fold_block(): jnp.dot(weights.astype(jnp.bfloat16), key_piece[:, :KVR], preferred_eleme...  33.7 us
    all_gather x1, waiting for transfers between devices, body(): rows_all = lax.all_gather(post_norm, 'grp', axis=0, tiled=True)  33.4 us
    reduce_sum x12, other arithmetic, fold_block(): running_sum = running_sum * factor + jnp.sum(weights, axis=1)  19.2 us
  transfers between devices with their start and end apart: 14, of which 8 were waited for; matrix products, arithmetic and copies ran while one was open for 40% of the time, Pallas kernels for 0%

commit v1 on v0

--- a/solution.py
+++ b/solution.py
@@ -1,7 +1,7 @@
 import jax
 import jax.numpy as jnp
 from jax import lax
-from jax.sharding import PartitionSpec as P
+from jax.sharding import Mesh, PartitionSpec as P
 
 KVR = 256
 HEADS = 20
@@ -88,13 +88,12 @@
     prompt_of,
 ):
     group_index = lax.axis_index("grp")
-    shard_index = lax.axis_index("tok")
+    span_index = lax.axis_index("tq")
+    local_request = lax.axis_index("tr")
     tok_dev = tokens.shape[0]
-    tok_count = lax.axis_size("tok")
-    group_requests = tok_dev * tok_count // SPAN
-    local_request = shard_index % group_requests
+    group_requests = lax.axis_size("tr")
     owner = group_index * group_requests + local_request
-    offset = shard_index // group_requests * tok_dev
+    offset = span_index * tok_dev
     within = offset + jnp.arange(tok_dev, dtype=jnp.int32)
     own_prompt = prompt_of[owner]
     prompt_live = prompt_len[own_prompt]
@@ -122,22 +121,19 @@
         axis=-1,
     ).astype(jnp.bfloat16)
     latent_width = new_latents.shape[1]
-    shards_back = SPAN // tok_dev
-    earlier_pieces = []
-    passing = new_latents
-    for back in range(1, shards_back):
-        passing = passed_along(passing, "tok", group_requests)
-        earlier_pieces.insert(0, passing)
-    span_rows = jnp.concatenate(earlier_pieces + [new_latents], axis=0)
-    lead_rows = (shards_back - 1) * tok_dev
-    span_lower = jnp.broadcast_to(lead_rows - offset, (tok_dev,))
-    span_limit = lead_rows + 1 + jnp.arange(tok_dev, dtype=jnp.int32)
-    cache_all, prompt_all = (
-        lax.all_gather(cache_latents, "tok", axis=1, tiled=True),
-        lax.all_gather(prompt_latents, "tok", axis=1, tiled=True),
-    )
-    cache_rows = lax.dynamic_index_in_dim(cache_all, local_request, 0, keepdims=False)
-    prompt_rows = lax.dynamic_index_in_dim(prompt_all, own_prompt, 0, keepdims=False)
+    span_rows = lax.all_gather(new_latents, "tq", axis=0, tiled=True)
+    span_lower = jnp.zeros((tok_dev,), jnp.int32)
+    span_limit = within + 1
+    cache_mine = lax.all_to_all(cache_latents, "tr", 0, 1, tiled=True)
+    group_prompts = prompt_of[group_index * group_requests + jnp.arange(group_requests)]
+    prompt_send = jnp.take(prompt_latents, group_prompts, axis=0)
+    prompt_mine = lax.all_to_all(prompt_send, "tr", 0, 1, tiled=True)
+    prompt_piece = prompt_mine.shape[1]
+    key_pieces = lax.all_gather(
+        jnp.concatenate([prompt_mine, cache_mine], axis=1)[0], "tq", axis=0
+    )
+    prompt_rows = key_pieces[:, :prompt_piece].reshape(-1, latent_width)
+    cache_rows = key_pieces[:, prompt_piece:].reshape(-1, latent_width)
     query_rows = queries.reshape(tok_dev * HEADS, latent_width)
     row_count = tok_dev * HEADS
     score_scale = 1.0 / (NOPE + ROPE) ** 0.5
@@ -148,9 +144,9 @@
     )
     no_lower = jnp.zeros((tok_dev,), jnp.int32)
     segments = (
+        (span_rows, span_lower, span_limit),
         (prompt_rows, no_lower, jnp.broadcast_to(prompt_live, (tok_dev,))),
         (cache_rows, no_lower, jnp.broadcast_to(cache_live, (tok_dev,))),
-        (span_rows, span_lower, span_limit),
     )
     for key_rows, token_lower, token_limit in segments:
         lowers = jnp.repeat(token_lower, HEADS)
@@ -175,26 +171,20 @@
         .reshape(tok_dev, HEADS * VDIM)
     )
     attended = jnp.dot(heads_out, output_weight, preferred_element_type=jnp.float32)
-    residual = lax.optimization_barrier(
-        (tokens.astype(jnp.float32) + attended).astype(jnp.bfloat16)
+    weights_full = lax.all_gather(
+        jnp.stack([gate_weight, up_weight, down_weight.T]), ("tq", "tr"), axis=1, tiled=True
+    )
+    residual, weights_full = lax.optimization_barrier(
+        ((tokens.astype(jnp.float32) + attended).astype(jnp.bfloat16), weights_full)
     )
     post_norm = norm_rows(residual.astype(jnp.float32), post_gain).astype(jnp.bfloat16)
     rows_all = lax.all_gather(post_norm, "grp", axis=0, tiled=True)
-    gate_values = jnp.dot(
-        rows_all,
-        lax.all_gather(gate_weight, "tok", axis=0, tiled=True),
-        preferred_element_type=jnp.float32,
-    )
-    up_values = jnp.dot(
-        rows_all,
-        lax.all_gather(up_weight, "tok", axis=0, tiled=True),
-        preferred_element_type=jnp.float32,
-    )
+    gate_full, up_full, down_full = weights_full
+    gate_values = jnp.dot(rows_all, gate_full, preferred_element_type=jnp.float32)
+    up_values = jnp.dot(rows_all, up_full, preferred_element_type=jnp.float32)
     hidden = (jax.nn.silu(gate_values) * up_values).astype(jnp.bfloat16)
-    partial_out = jnp.dot(
-        hidden,
-        lax.all_gather(down_weight, "tok", axis=1, tiled=True),
-        preferred_element_type=jnp.float32,
+    partial_out = lax.dot_general(
+        hidden, down_full, (((1,), (1,)), ((), ())), preferred_element_type=jnp.float32
     )
     down_values = lax.psum_scatter(
         partial_out.astype(jnp.bfloat16), "grp", scatter_dimension=0, tiled=True
@@ -204,26 +194,40 @@
 
 
 def solution(mesh):
+    split = ("grp", "tq", "tr")
+    tokens_spec = P(split, None)
     in_specs = (
-        P(("grp", "tok"), None),
-        P(),
-        P(),
-        P(),
-        P(),
-        P(),
-        P(),
-        P(),
-        P(),
-        P(),
-        P(),
-        P("tok", "grp"),
-        P("tok", "grp"),
-        P("grp", "tok"),
-        P("grp", "tok", None),
-        P(None, "tok", None),
-        P(),
-        P(),
-        P(),
-    )
-    out_specs = (P(("grp", "tok"), None), P(("grp", "tok"), None))
-    return jax.shard_map(body, mesh=mesh, in_specs=in_specs, out_specs=out_specs, check_vma=False)
+        tokens_spec,
+        P(),
+        P(),
+        P(),
+        P(),
+        P(),
+        P(),
+        P(),
+        P(),
+        P(),
+        P(),
+        P(("tq", "tr"), "grp"),
+        P(("tq", "tr"), "grp"),
+        P("grp", ("tq", "tr")),
+        P("grp", ("tq", "tr"), None),
+        P(None, ("tq", "tr"), None),
+        P(),
+        P(),
+        P(),
+    )
+    out_specs = (tokens_spec, tokens_spec)
+
+    def run(*args):
+        n_grp, n_tok = mesh.shape["grp"], mesh.shape["tok"]
+        tok_dev = args[0].shape[0] // (n_grp * n_tok)
+        group_requests = tok_dev * n_tok // SPAN
+        sub = Mesh(
+            mesh.devices.reshape(n_grp, n_tok // group_requests, group_requests), split
+        )
+        return jax.shard_map(
+            body, mesh=sub, in_specs=in_specs, out_specs=out_specs, check_vma=False
+        )(*args)
+
+    return run

time: 415 us -> 327 us (0.79)
  waiting for transfers between devices: 174 us -> 74.4 us
  blocking collectives: 0 us -> 45.4 us
  starting transfers between devices: 39.6 us -> 5.49 us
    all_gather x5 -> x2, waiting for transfers between devices: 97.7 us -> 0.04 us  [the longest x1 0.02 us: body(): lax.all_gather(jnp.stack([gate_weight, up_weight, down_weight.T]), ('tq',...]
    all_gather x0 -> x1, blocking collectives: none -> 39.7 us  [body(): span_rows = lax.all_gather(new_latents, 'tq', axis=0, tiled=True)]
    ppermute x7 -> x0, starting transfers between devices: 39.1 us -> none  [passed_along(): return lax.ppermute(block, axis, route)]
    dynamic_slice x2 -> x0, local copies, waits for them, and re-layouts: 7.81 us -> none  [body(): lax.dynamic_index_in_dim(cache_all, local_request, 0, keepdims=False)]
    ppermute x7 -> x0, waiting for transfers between devices: 6.73 us -> none  [passed_along(): return lax.ppermute(block, axis, route)]
    all_to_all x0 -> x1, blocking collectives: none -> 5.71 us  [body(): prompt_mine = lax.all_to_all(prompt_send, 'tr', 0, 1, tiled=True)]
    slice x0 -> x2, local copies, waits for them, and re-layouts: none -> 5.18 us  [the longest x1 3.25 us: body(): cache_rows = key_pieces[:, prompt_piece:].reshape(-1, latent_width)]
    all_to_all x0 -> x1, starting transfers between devices: none -> 5.1 us  [body(): cache_mine = lax.all_to_all(cache_latents, 'tr', 0, 1, tiled=True)]
  transfers between devices with their start and end apart: 14 -> 5, of which waited for: 8 -> 3; matrix products, arithmetic and copies ran while one was open for 40% -> 47% of each run, Pallas kernels for 0% -> 0%
where the time goes in v1:
time: 327 us; the launch traced here: 325 us
  matrix products  110 us (34%)
  waiting for transfers between devices  74.4 us (23%)
  blocking collectives  45.4 us (14%)
  other arithmetic  40.7 us (12%)
  local copies, waits for them, and re-layouts  30.7 us (9%)
  between operations  17.3 us (5%)
  starting transfers between devices  5.49 us (2%)
    dot_general x12, matrix products, fold_block(): jnp.einsum('rw,kw->rk', queries, key_piece, preferred_element_type=jnp.fl...  46.2 us
    all_gather x1, blocking collectives, body(): span_rows = lax.all_gather(new_latents, 'tq', axis=0, tiled=True)  39.7 us
    all_gather x1, waiting for transfers between devices, body(): rows_all = lax.all_gather(post_norm, 'grp', axis=0, tiled=True)  36 us
    reduce_scatter x1, waiting for transfers between devices, body(): lax.psum_scatter(partial_out.astype(jnp.bfloat16), 'grp', scatter_dimensi...  34.2 us
    dot_general x12, matrix products, fold_block(): jnp.dot(weights.astype(jnp.bfloat16), key_piece[:, :KVR], preferred_eleme...  33.4 us
    reduce_sum x12, other arithmetic, fold_block(): running_sum = running_sum * factor + jnp.sum(weights, axis=1)  18.2 us
    dot_general x1, matrix products, body(): lax.dot_general(hidden, down_full, (((1,), (1,)), ((), ())), preferred_el...  11.8 us
    unnamed x34, local copies, waits for them, and re-layouts  8.71 us
  transfers between devices with their start and end apart: 5, of which 3 were waited for; matrix products, arithmetic and copies ran while one was open for 47% of the time, Pallas kernels for 0%

profile of v1, /device:TPU:8, one launch (start us, length us, event | category | flops | bytes accessed | tf_op | source)
XLA Modules:
  0.0 324.5 jit_solution(5772448848341362100)
XLA Ops:
  10.3 5.7 %all_to_all.24 = bf16[4,32,288]{2,1,0:T(8,128)(2,1)S(1)} all-to-all(bf16[4,32,288]{2,1,0:T(8,128)(2,1)S(1)} %broadcast_select_fusion), channel_id=1, replica_groups=mesh['grp'=4,'tq'=8,'tr'=4] {'tr'}, dimensions={0} | all-to-all | bytes 147456 | tf_op jit(solution)/shard_map/all_to_all | solution.py:130
  16.0 5.1 %all-to-all-start.1 = ((bf16[4,128,288]{1,2,0:T(8,128)(2,1)}), bf16[4,128,288]{1,2,0:T(8,128)(2,1)S(1)}, u32[]{:S(2)}, u32[]{:S(2)}) async-start(bf16[4,128,288]{1,2,0:T(8,128)(2,1)} %param.39), calls=%async_computation.1 | async-start | bytes 589824 | tf_op jit(solution)/shard_map/all_to_all | solution.py:127
  21.9 4.0 %all-to-all-done.1 = bf16[4,128,288]{1,2,0:T(8,128)(2,1)S(1)} async-done(((bf16[4,128,288]{1,2,0:T(8,128)(2,1)}), bf16[4,128,288]{1,2,0:T(8,128)(2,1)S(1)}, u32[]{:S(2)}, u32[]{:S(2)}) %all-to-all-start.1) | async-done | bytes 294944 | tf_op jit(solution)/shard_map/all_to_all | solution.py:127
  41.2 3.1 multiply_reduce_fusion
  55.8 39.7 %all_gather.12 = bf16[1024,288]{0,1:T(8,128)(2,1)} all-gather(bf16[128,288]{0,1:T(8,128)(2,1)S(1)} %pad_maximum_fusion.3), channel_id=1, replica_groups=mesh['grp'=4,'tq'=8,'tr'=4] {'tq'}, dimensions={0}, use_global_device_ids=true | all-gather | bytes 663552 | tf_op jit(solution)/shard_map/all_gather | solution.py:124
  95.5 3.4 %pad_maximum_fusion = bf16[2560,288]{1,0:T(8,128)(2,1)} fusion(bf16[2560,16]{1,0:T(8,128)(2,1)} %copy.62, bf16[2560,16]{1,0:T(8,128)(2,1)} %copy.61, bf16[2560,256]{1,0:T(8,128)(2,1)} %concatenate.19), kind=kLoop, calls=%fused_computation.92 | loop fusion | flops 4423680 | bytes 2949120 | tf_op jit(solution)/shard_map/concatenate | solution.py:117
  98.9 28.0 %while.56 = (s32[]{:T(128)}, f32[2560]{0:T(1024)S(1)}, f32[2560]{0:T(1024)S(1)}, f32[2560,256]{1,0:T(8,128)S(1)}, bf16[1024,288]{0,1:T(8,128)(2,1)}, /*index=5*/...) while((s32[]{:T(128)}, f32[2560]{0:T(1024)S(1)}, ...), condition=%wide.region_6.7_spmd.clone, body=%wide.region_3.6_spmd.clone.sunk | while | flops 1447704576 | bytes 44702416 | solution.py:66
  99.1 6.3 %fusion.144 = (f32[2560]{0:T(1024)S(1)}, f32[512,2560]{1,0:T(8,128)}) fusion(s32[2560]{0:T(1024)S(1)} %lt.227, s32[512]{0:T(512)S(1)} %iota_add_fusion.5, pred[512]{0:T(512)(128)(4,1)S(1)} %broadcast_compare_fusion.2, bf16[2560,288]{1,0:T(8,128)(2,1)} %get-tuple-element.752, bf16[1024,288]{0,1:T(8,128)(2,1)} %get-tuple-element.751, s32[]{:T(128)S(6)} %select_n.176), kind=kOutput, calls=%fused_computation.53.clone.1 | convolution fusion | flops 761525760 | bytes 7526916 | tf_op jit(solution)/shard_map/while/body/eval_jaxpr/rw,kw->rk/dot_general | solution.py:52
  105.4 4.0 %fusion.145 = f32[2560]{0:T(1024)S(1)} fusion(f32[512,2560]{1,0:T(8,128)} %get-tuple-element.722, f32[2560]{0:T(1024)S(1)} %select_maximum_fusion.2, s32[2560]{0:T(1024)S(1)} %lt.227, s32[512]{0:T(512)S(1)} %iota_add_fusion.5, pred[512]{0:T(512)(128)(4,1)S(1)} %broadcast_compare_fusion.2), kind=kLoop, calls=%fused_computation.60.clone.1 | loop fusion | flops 6551040 | bytes 5276160 | tf_op jit(solution)/shard_map/while/body/eval_jaxpr/reduce_sum | solution.py:60
  109.5 3.4 %convolution_add_fusion.9 = f32[2560,256]{1,0:T(8,128)S(1)} fusion(f32[512,2560]{1,0:T(8,128)S(1)} %copy-done.4, f32[2560,256]{1,0:T(8,128)S(1)} %get-tuple-element.739, f32[2560]{0:T(1024)S(1)} %select_maximum_fusion.2, s32[2560]{0:T(1024)S(1)} %lt.227, s32[512]{0:T(512)S(1)} %iota_add_fusion.5, pred[512]{0:T(512)(128)(4,1)S(1)} %broadcast_compare_fusion.2, ...), kind=kOutput, calls=%fused_computation.58.clone.1 | convolution fusion | flops 679608320 | bytes 10781189 | tf_op jit(solution)/shard_map/while/body/eval_jaxpr/dot_general | solution.py:61
  113.1 6.3 %fusion.144 = (f32[2560]{0:T(1024)S(1)}, f32[512,2560]{1,0:T(8,128)}) fusion(s32[2560]{0:T(1024)S(1)} %lt.227, s32[512]{0:T(512)S(1)} %iota_add_fusion.5, pred[512]{0:T(512)(128)(4,1)S(1)} %broadcast_compare_fusion.2, bf16[2560,288]{1,0:T(8,128)(2,1)} %get-tuple-element.752, bf16[1024,288]{0,1:T(8,128)(2,1)} %get-tuple-element.751, s32[]{:T(128)S(6)} %select_n.176), kind=kOutput, calls=%fused_computation.53.clone.1 | convolution fusion | flops 761525760 | bytes 7526916 | tf_op jit(solution)/shard_map/while/body/eval_jaxpr/rw,kw->rk/dot_general | solution.py:52
  119.4 4.0 %fusion.145 = f32[2560]{0:T(1024)S(1)} fusion(f32[512,2560]{1,0:T(8,128)} %get-tuple-element.722, f32[2560]{0:T(1024)S(1)} %select_maximum_fusion.2, s32[2560]{0:T(1024)S(1)} %lt.227, s32[512]{0:T(512)S(1)} %iota_add_fusion.5, pred[512]{0:T(512)(128)(4,1)S(1)} %broadcast_compare_fusion.2), kind=kLoop, calls=%fused_computation.60.clone.1 | loop fusion | flops 6551040 | bytes 5276160 | tf_op jit(solution)/shard_map/while/body/eval_jaxpr/reduce_sum | solution.py:60
  123.6 3.3 %convolution_add_fusion.9 = f32[2560,256]{1,0:T(8,128)S(1)} fusion(f32[512,2560]{1,0:T(8,128)S(1)} %copy-done.4, f32[2560,256]{1,0:T(8,128)S(1)} %get-tuple-element.739, f32[2560]{0:T(1024)S(1)} %select_maximum_fusion.2, s32[2560]{0:T(1024)S(1)} %lt.227, s32[512]{0:T(512)S(1)} %iota_add_fusion.5, pred[512]{0:T(512)(128)(4,1)S(1)} %broadcast_compare_fusion.2, ...), kind=kOutput, calls=%fused_computation.58.clone.1 | convolution fusion | flops 679608320 | bytes 10781189 | tf_op jit(solution)/shard_map/while/body/eval_jaxpr/dot_general | solution.py:61
  131.1 3.2 %slice.75 = bf16[8,512,288]{1,2,0:T(8,128)(2,1)} slice(bf16[8,640,288]{1,2,0:T(8,128)(2,1)} %all-gather.4.cloned.1.call-done), slice={[0:8], [128:640], [0:288]} | slice | bytes 4718592 | tf_op jit(solution)/shard_map/slice | solution.py:136
  134.4 4.5 %copy.73 = bf16[8,512,288]{2,1,0:T(8,128)(2,1)} copy(bf16[8,512,288]{1,2,0:T(8,128)(2,1)} %slice.75) | data formatting | bytes 4718592
  138.9 15.7 %while.54 = (s32[]{:T(128)}, f32[2560]{0:T(1024)S(1)}, f32[2560]{0:T(1024)S(1)}, f32[2560,256]{1,0:T(8,128)S(1)}, bf16[1024,288]{1,0:T(8,128)(2,1)}, /*index=5*/...) while((s32[]{:T(128)}, f32[2560]{0:T(1024)S(1)}, ...), condition=%wide.region_10.11_spmd.clone, body=%wide.region_7.10_spmd.clone.sunk | while | flops 1439177728 | bytes 23759020 | solution.py:66
  139.6 3.5 %fusion.133 = (f32[2560]{0:T(1024)S(1)}, f32[512,2560]{1,0:T(8,128)S(1)}) fusion(pred[512]{0:T(512)(128)(4,1)S(1)} %fusion.132, bf16[2560,288]{1,0:T(8,128)(2,1)} %get-tuple-element.785, bf16[1024,288]{1,0:T(8,128)(2,1)} %get-tuple-element.784, s32[]{:T(128)S(6)} %select_n.168), kind=kOutput, calls=%fused_computation.7.clone.1 | convolution fusion | flops 758904320 | bytes 7612932 | tf_op jit(solution)/shard_map/while/body/eval_jaxpr/rw,kw->rk/dot_general | solution.py:52
  147.5 3.3 %fusion.133 = (f32[2560]{0:T(1024)S(1)}, f32[512,2560]{1,0:T(8,128)S(1)}) fusion(pred[512]{0:T(512)(128)(4,1)S(1)} %fusion.132, bf16[2560,288]{1,0:T(8,128)(2,1)} %get-tuple-element.785, bf16[1024,288]{1,0:T(8,128)(2,1)} %get-tuple-element.784, s32[]{:T(128)S(6)} %select_n.168), kind=kOutput, calls=%fused_computation.7.clone.1 | convolution fusion | flops 758904320 | bytes 7612932 | tf_op jit(solution)/shard_map/while/body/eval_jaxpr/rw,kw->rk/dot_general | solution.py:52
  154.6 61.8 %while.55 = (s32[]{:T(128)}, f32[2560]{0:T(1024)S(1)}, f32[2560]{0:T(1024)S(1)}, f32[2560,256]{1,0:T(8,128)S(1)}, bf16[4096,288]{1,0:T(8,128)(2,1)}, /*index=5*/...) while((s32[]{:T(128)}, f32[2560]{0:T(1024)S(1)}, ...), condition=%wide.region_14.15_spmd.clone, body=%wide.region_11.14_spmd.clone.sunk | while | flops 1439177728 | bytes 23759020 | solution.py:66
  155.4 3.6 %fusion.139 = (f32[2560]{0:T(1024)S(1)}, f32[512,2560]{1,0:T(8,128)S(1)}) fusion(pred[512]{0:T(512)(128)(4,1)S(1)} %fusion.138, bf16[2560,288]{1,0:T(8,128)(2,1)} %get-tuple-element.818, bf16[4096,288]{1,0:T(8,128)(2,1)} %get-tuple-element.817, s32[]{:T(128)S(6)} %select_n.172), kind=kOutput, calls=%fused_computation.30.clone.1 | convolution fusion | flops 758904320 | bytes 7612932 | tf_op jit(solution)/shard_map/while/body/eval_jaxpr/rw,kw->rk/dot_general | solution.py:52
  163.3 3.3 %fusion.139 = (f32[2560]{0:T(1024)S(1)}, f32[512,2560]{1,0:T(8,128)S(1)}) fusion(pred[512]{0:T(512)(128)(4,1)S(1)} %fusion.138, bf16[2560,288]{1,0:T(8,128)(2,1)} %get-tuple-element.818, bf16[4096,288]{1,0:T(8,128)(2,1)} %get-tuple-element.817, s32[]{:T(128)S(6)} %select_n.172), kind=kOutput, calls=%fused_computation.30.clone.1 | convolution fusion | flops 758904320 | bytes 7612932 | tf_op jit(solution)/shard_map/while/body/eval_jaxpr/rw,kw->rk/dot_general | solution.py:52
  171.0 3.3 %fusion.139 = (f32[2560]{0:T(1024)S(1)}, f32[512,2560]{1,0:T(8,128)S(1)}) fusion(pred[512]{0:T(512)(128)(4,1)S(1)} %fusion.138, bf16[2560,288]{1,0:T(8,128)(2,1)} %get-tuple-element.818, bf16[4096,288]{1,0:T(8,128)(2,1)} %get-tuple-element.817, s32[]{:T(128)S(6)} %select_n.172), kind=kOutput, calls=%fused_computation.30.clone.1 | convolution fusion | flops 758904320 | bytes 7612932 | tf_op jit(solution)/shard_map/while/body/eval_jaxpr/rw,kw->rk/dot_general | solution.py:52
  178.7 3.3 %fusion.139 = (f32[2560]{0:T(1024)S(1)}, f32[512,2560]{1,0:T(8,128)S(1)}) fusion(pred[512]{0:T(512)(128)(4,1)S(1)} %fusion.138, bf16[2560,288]{1,0:T(8,128)(2,1)} %get-tuple-element.818, bf16[4096,288]{1,0:T(8,128)(2,1)} %get-tuple-element.817, s32[]{:T(128)S(6)} %select_n.172), kind=kOutput, calls=%fused_computation.30.clone.1 | convolution fusion | flops 758904320 | bytes 7612932 | tf_op jit(solution)/shard_map/while/body/eval_jaxpr/rw,kw->rk/dot_general | solution.py:52
  186.3 3.3 %fusion.139 = (f32[2560]{0:T(1024)S(1)}, f32[512,2560]{1,0:T(8,128)S(1)}) fusion(pred[512]{0:T(512)(128)(4,1)S(1)} %fusion.138, bf16[2560,288]{1,0:T(8,128)(2,1)} %get-tuple-element.818, bf16[4096,288]{1,0:T(8,128)(2,1)} %get-tuple-element.817, s32[]{:T(128)S(6)} %select_n.172), kind=kOutput, calls=%fused_computation.30.clone.1 | convolution fusion | flops 758904320 | bytes 7612932 | tf_op jit(solution)/shard_map/while/body/eval_jaxpr/rw,kw->rk/dot_general | solution.py:52
  194.0 3.3 %fusion.139 = (f32[2560]{0:T(1024)S(1)}, f32[512,2560]{1,0:T(8,128)S(1)}) fusion(pred[512]{0:T(512)(128)(4,1)S(1)} %fusion.138, bf16[2560,288]{1,0:T(8,128)(2,1)} %get-tuple-element.818, bf16[4096,288]{1,0:T(8,128)(2,1)} %get-tuple-element.817, s32[]{:T(128)S(6)} %select_n.172), kind=kOutput, calls=%fused_computation.30.clone.1 | convolution fusion | flops 758904320 | bytes 7612932 | tf_op jit(solution)/shard_map/while/body/eval_jaxpr/rw,kw->rk/dot_general | solution.py:52
  201.7 3.3 %fusion.139 = (f32[2560]{0:T(1024)S(1)}, f32[512,2560]{1,0:T(8,128)S(1)}) fusion(pred[512]{0:T(512)(128)(4,1)S(1)} %fusion.138, bf16[2560,288]{1,0:T(8,128)(2,1)} %get-tuple-element.818, bf16[4096,288]{1,0:T(8,128)(2,1)} %get-tuple-element.817, s32[]{:T(128)S(6)} %select_n.172), kind=kOutput, calls=%fused_computation.30.clone.1 | convolution fusion | flops 758904320 | bytes 7612932 | tf_op jit(solution)/shard_map/while/body/eval_jaxpr/rw,kw->rk/dot_general | solution.py:52
  209.3 3.3 %fusion.139 = (f32[2560]{0:T(1024)S(1)}, f32[512,2560]{1,0:T(8,128)S(1)}) fusion(pred[512]{0:T(512)(128)(4,1)S(1)} %fusion.138, bf16[2560,288]{1,0:T(8,128)(2,1)} %get-tuple-element.818, bf16[4096,288]{1,0:T(8,128)(2,1)} %get-tuple-element.817, s32[]{:T(128)S(6)} %select_n.172), kind=kOutput, calls=%fused_computation.30.clone.1 | convolution fusion | flops 758904320 | bytes 7612932 | tf_op jit(solution)/shard_map/while/body/eval_jaxpr/rw,kw->rk/dot_general | solution.py:52
  220.8 3.9 %fusion.69 = bf16[128,2560]{1,0:T(8,128)(2,1)S(1)} fusion(bf16[128,1280]{0,1:T(8,128)(2,1)S(1)} %bitcast.129, bf16[1280,2560]{1,0:T(8,128)(2,1)} %param.34, bf16[128,2560]{1,0:T(8,128)(2,1)S(1)} %copy-done.7), kind=kOutput, calls=%fused_computation.89 | convolution fusion | flops 839843840 | bytes 8192000 | tf_op jit(solution)/shard_map/dot_general | solution.py:173
  227.0 36.0 %all-gather.8.cloned.1.call-done = bf16[512,2560]{1,0:T(8,128)(2,1)} async-done(((bf16[128,2560]{1,0:T(8,128)(2,1)}), bf16[512,2560]{1,0:T(8,128)(2,1)}) %all-gather.8.cloned.1.call-update) | async-done | bytes 2621456 | tf_op jit(solution)/shard_map/all_gather | solution.py:181
  263.0 6.7 %fusion.61 = f32[512,800]{0,1:T(8,128)} fusion(bf16[512,2560]{1,0:T(8,128)(2,1)} %all-gather.8.cloned.1.call-done, bf16[3,2560,800]{2,1,0:T(8,128)(2,1)} %all-gather.6.cloned.1.call-done), kind=kOutput, calls=%fused_computation.82 | convolution fusion | flops 2097152000 | bytes 8847360 | tf_op jit(solution)/shard_map/dot_general | solution.py:183
  269.6 11.8 %fusion.66 = bf16[512,2560]{1,0:T(8,128)(2,1)} fusion(bf16[3,2560,800]{2,1,0:T(8,128)(2,1)} %all-gather.6.cloned.1.call-done, f32[512,800]{0,1:T(8,128)} %fusion.61, bf16[512,2560]{1,0:T(8,128)(2,1)} %all-gather.8.cloned.1.call-done), kind=kOutput, calls=%fused_computation.87 | convolution fusion | flops 4198072320 | bytes 16056320 | tf_op jit(solution)/shard_map/dot_general | solution.py:186
  281.5 34.2 %reduce-scatter.2.cloned.1.call-done = bf16[128,2560]{1,0:T(8,128)(2,1)} async-done(((bf16[512,2560]{1,0:T(8,128)(2,1)}), bf16[128,2560]{1,0:T(8,128)(2,1)}) %reduce-scatter.2.cloned.1.call-update) | async-done | bytes 655376 | tf_op jit(solution)/shard_map/reduce_scatter | solution.py:189
  (177 shorter events, 84.0 us)
Async XLA Ops:
  7.2 37.2 %copy-start = (bf16[768,1920]{1,0:T(8,128)(2,1)S(1)}, bf16[768,1920]{1,0:T(8,128)(2,1)}, u32[]{:S(2)}) copy-start(bf16[768,1920]{1,0:T(8,128)(2,1)} %param.29) | copy-start | bytes 8847364
  7.2 22.7 %copy-start.2 = (s32[16]{0:T(128)S(1)}, s32[16]{0:T(128)}, u32[]{:S(2)}) copy-start(s32[16]{0:T(128)} %param.43) | copy-start | bytes 196
  16.0 9.8 %all-to-all-start.1 = ((bf16[4,128,288]{1,2,0:T(8,128)(2,1)}), bf16[4,128,288]{1,2,0:T(8,128)(2,1)S(1)}, u32[]{:S(2)}, u32[]{:S(2)}) async-start(bf16[4,128,288]{1,2,0:T(8,128)(2,1)} %param.39), calls=%async_computation.1 | async-start | bytes 589824 | tf_op jit(solution)/shard_map/all_to_all | solution.py:127
  21.1 105.8 %all-gather.4.cloned.1.call-start = ((), (), s32[]{:S(2)}) async-start(), calls=%async_computation.3 | async-start | bytes 3317760 | tf_op jit(solution)/shard_map/all_gather | solution.py:132
  27.8 196.9 %all-gather.6.cloned.1.call-start = ((), (), s32[]{:S(2)}) async-start(), calls=%async_computation.4 | async-start | bytes 14192640 | tf_op jit(solution)/shard_map/all_gather | solution.py:174
  29.8 233.2 %all-gather.8.cloned.1.call-start = ((), (), s32[]{:S(2)}) async-start(), calls=%async_computation.5 | async-start | bytes 3276800 | tf_op jit(solution)/shard_map/all_gather | solution.py:181
  36.2 5.0 %copy-start.6 = (bf16[128,2560]{1,0:T(8,128)(2,1)S(1)}, bf16[128,2560]{1,0:T(8,128)(2,1)}, u32[]{:S(2)}) copy-start(bf16[128,2560]{1,0:T(8,128)(2,1)} %param.25) | copy-start | bytes 1966084
  41.2 3.1 copy-start.14
  45.2 6.5 %copy-start.8 = (bf16[256,1280]{1,0:T(8,128)(2,1)S(1)}, bf16[256,1280]{1,0:T(8,128)(2,1)}, u32[]{:S(2)}) copy-start(bf16[256,1280]{1,0:T(8,128)(2,1)} %param.32) | copy-start | bytes 1966084
  52.6 2.0 copy-start.15
  53.3 1.3 copy-start.9
  53.3 2.4 copy-start.13
  53.3 2.4 copy-start.11
  55.8 43.1 %copy-start.12 = (bf16[128,288]{0,1:T(8,128)(2,1)}, bf16[128,288]{0,1:T(8,128)(2,1)S(1)}, u32[]{:S(2)}) copy-start(bf16[128,288]{0,1:T(8,128)(2,1)S(1)} %pad_maximum_fusion.3) | copy-start | bytes 221188
  55.8 43.1 %copy-start.3 = (f32[2560,256]{1,0:T(8,128)S(1)}, f32[2560,256]{1,0:T(8,128)}, u32[]{:S(2)}) copy-start(f32[2560,256]{1,0:T(8,128)} %custom-call.2) | copy-start | bytes 7864324
  105.4 4.1 %copy-start.4 = (f32[512,2560]{1,0:T(8,128)S(1)}, f32[512,2560]{1,0:T(8,128)}, u32[]{:S(2)}) copy-start(f32[512,2560]{1,0:T(8,128)} %get-tuple-element.722) | copy-start | bytes 15728644 | tf_op jit(solution)/shard_map/while
  119.4 4.2 %copy-start.4 = (f32[512,2560]{1,0:T(8,128)S(1)}, f32[512,2560]{1,0:T(8,128)}, u32[]{:S(2)}) copy-start(f32[512,2560]{1,0:T(8,128)} %get-tuple-element.722) | copy-start | bytes 15728644 | tf_op jit(solution)/shard_map/while
  217.9 2.3 copy-start.10
  217.9 2.9 copy-start.7
  224.7 0.8 copy-start.5
  226.6 89.1 %reduce-scatter.2.cloned.1.call-start = ((), (), s32[]{:S(2)}) async-start(), calls=%async_computation.6 | async-start | bytes 3276800 | tf_op jit(solution)/shard_map/reduce_scatter | solution.py:189
  269.6 48.4 %copy-start.1 = (bf16[768,1920]{1,0:T(8,128)(2,1)S(1)}, bf16[768,1920]{1,0:T(8,128)(2,1)}, u32[]{:S(2)}) copy-start(bf16[768,1920]{1,0:T(8,128)(2,1)} %param.29) | copy-start | bytes 8847364
Sparse Core Ops, SparseCore 0:
  27.9 71.8 all-gather.3
  102.2 63.7 all-gather.5
  226.8 36.1 all-gather.7
  281.6 34.0 reduce-scatter.1

commit v2 on v1

--- a/solution.py
+++ b/solution.py
@@ -121,19 +121,20 @@
         axis=-1,
     ).astype(jnp.bfloat16)
     latent_width = new_latents.shape[1]
-    span_rows = lax.all_gather(new_latents, "tq", axis=0, tiled=True)
+    span_blocks = lax.axis_size("tq")
+    span_rows = lax.all_to_all(
+        jnp.broadcast_to(new_latents, (span_blocks,) + new_latents.shape), "tq", 0, 0, tiled=True
+    ).reshape(-1, latent_width)
     span_lower = jnp.zeros((tok_dev,), jnp.int32)
     span_limit = within + 1
-    cache_mine = lax.all_to_all(cache_latents, "tr", 0, 1, tiled=True)
+    cache_rows = lax.all_to_all(
+        jnp.tile(cache_latents, (span_blocks, 1, 1)), ("tq", "tr"), 0, 0, tiled=True
+    ).reshape(-1, latent_width)
     group_prompts = prompt_of[group_index * group_requests + jnp.arange(group_requests)]
     prompt_send = jnp.take(prompt_latents, group_prompts, axis=0)
-    prompt_mine = lax.all_to_all(prompt_send, "tr", 0, 1, tiled=True)
-    prompt_piece = prompt_mine.shape[1]
-    key_pieces = lax.all_gather(
-        jnp.concatenate([prompt_mine, cache_mine], axis=1)[0], "tq", axis=0
-    )
-    prompt_rows = key_pieces[:, :prompt_piece].reshape(-1, latent_width)
-    cache_rows = key_pieces[:, prompt_piece:].reshape(-1, latent_width)
+    prompt_rows = lax.all_to_all(
+        jnp.tile(prompt_send, (span_blocks, 1, 1)), ("tq", "tr"), 0, 0, tiled=True
+    ).reshape(-1, latent_width)
     query_rows = queries.reshape(tok_dev * HEADS, latent_width)
     row_count = tok_dev * HEADS
     score_scale = 1.0 / (NOPE + ROPE) ** 0.5
@@ -144,9 +145,9 @@
     )
     no_lower = jnp.zeros((tok_dev,), jnp.int32)
     segments = (
-        (span_rows, span_lower, span_limit),
         (prompt_rows, no_lower, jnp.broadcast_to(prompt_live, (tok_dev,))),
         (cache_rows, no_lower, jnp.broadcast_to(cache_live, (tok_dev,))),
+        (span_rows, span_lower, span_limit),
     )
     for key_rows, token_lower, token_limit in segments:
         lowers = jnp.repeat(token_lower, HEADS)

time: 327 us -> 320 us (0.979)
  blocking collectives: 45.4 us -> 0 us
  starting transfers between devices: 5.49 us -> 24 us
  local copies, waits for them, and re-layouts: 30.7 us -> 40.5 us
  waiting for transfers between devices: 74.4 us -> 82.4 us
    all_gather x1 -> x0, blocking collectives: 39.7 us -> none  [body(): span_rows = lax.all_gather(new_latents, 'tq', axis=0, tiled=True)]
    all_to_all x1 -> x3, starting transfers between devices: 5.1 us -> 23.4 us  [the longest x1 8.73 us: body(): lax.all_to_all(jnp.tile(prompt_send, (span_blocks, 1, 1)), ('tq', 'tr'),...]
    all_to_all x1 -> x3, waiting for transfers between devices: 3.98 us -> 15.1 us  [the longest x1 15.1 us: body(): lax.all_to_all(jnp.tile(cache_latents, (span_blocks, 1, 1)), ('tq', 'tr')...]
    all_to_all x1 -> x0, blocking collectives: 5.71 us -> none  [body(): prompt_mine = lax.all_to_all(prompt_send, 'tr', 0, 1, tiled=True)]
    slice x2 -> x0, local copies, waits for them, and re-layouts: 5.18 us -> none  [the longest x1 3.25 us: body(): cache_rows = key_pieces[:, prompt_piece:].reshape(-1, latent_width)]
    concatenate x5, local copies, waits for them, and re-layouts: 5.15 us -> 9.09 us  [body(): queries = jnp.concatenate([absorbed, turned], axis=-1).astype(jnp.bfloat16)]
    another operation x0 -> x2, local copies, waits for them, and re-layouts: none -> 3.78 us  [the longest x1 2.79 us: body(): jnp.tile(cache_latents, (span_blocks, 1, 1))]
    unnamed x34 -> x36, local copies, waits for them, and re-layouts: 8.71 us -> 10.5 us
  transfers between devices with their start and end apart: 5 -> 6, of which waited for: 3 -> 3; matrix products, arithmetic and copies ran while one was open for 47% -> 50% of each run, Pallas kernels for 0% -> 0%
where the time goes in v2:
time: 320 us; the launch traced here: 317 us
  matrix products  110 us (34%)
  waiting for transfers between devices  82.4 us (26%)
  other arithmetic  42.1 us (13%)
  local copies, waits for them, and re-layouts  40.5 us (13%)
  starting transfers between devices  24 us (8%)
  between operations  17.4 us (5%)
    dot_general x12, matrix products, fold_block(): jnp.einsum('rw,kw->rk', queries, key_piece, preferred_element_type=jnp.fl...  44.8 us
    reduce_scatter x1, waiting for transfers between devices, body(): lax.psum_scatter(partial_out.astype(jnp.bfloat16), 'grp', scatter_dimensi...  34.2 us
    dot_general x12, matrix products, fold_block(): jnp.dot(weights.astype(jnp.bfloat16), key_piece[:, :KVR], preferred_eleme...  33.8 us
    all_gather x1, waiting for transfers between devices, body(): rows_all = lax.all_gather(post_norm, 'grp', axis=0, tiled=True)  33 us
    reduce_sum x12, other arithmetic, fold_block(): running_sum = running_sum * factor + jnp.sum(weights, axis=1)  19.3 us
    all_to_all x1, waiting for transfers between devices, body(): lax.all_to_all(jnp.tile(cache_latents, (span_blocks, 1, 1)), ('tq', 'tr')...  15.1 us
    dot_general x1, matrix products, body(): lax.dot_general(hidden, down_full, (((1,), (1,)), ((), ())), preferred_el...  11.8 us
    unnamed x36, local copies, waits for them, and re-layouts  10.5 us
  transfers between devices with their start and end apart: 6, of which 3 were waited for; matrix products, arithmetic and copies ran while one was open for 50% of the time, Pallas kernels for 0%

profile of v2, /device:TPU:8, one launch (start us, length us, event | category | flops | bytes accessed | tf_op | source)
XLA Modules:
  0.0 317.2 jit_solution(1311973714059208490)
XLA Ops:
  20.4 7.0 %all-to-all-start.2 = ((bf16[8,128,288]{1,2,0:T(8,128)(2,1)}), bf16[8,128,288]{1,2,0:T(8,128)(2,1)S(1)}, u32[]{:S(2)}, u32[]{:S(2)}) async-start(bf16[8,128,288]{1,2,0:T(8,128)(2,1)} %broadcast_in_dim.116), calls=%async_computation.2 | async-start | bytes 1179648 | tf_op jit(solution)/shard_map/all_to_all | solution.py:125
  45.2 8.7 %all-to-all-start = ((bf16[32,32,288]{2,1,0:T(8,128)(2,1)}), bf16[32,32,288]{2,1,0:T(8,128)(2,1)}, u32[]{:S(2)}, u32[]{:S(2)}) async-start(bf16[32,32,288]{2,1,0:T(8,128)(2,1)} %bitcast.3), calls=%async_computation | async-start | bytes 1572864 | tf_op jit(solution)/shard_map/all_to_all | solution.py:135
  62.0 3.2 %copy.51 = bf16[128,20,256]{2,1,0:T(8,128)(2,1)} copy(bf16[128,20,256]{2,0,1:T(8,128)(2,1)} %fusion.72) | data formatting | bytes 2621440 | tf_op jit(solution)/shard_map/thd,khd->thk/transpose | solution.py:110
  65.2 3.3 %concatenate.15 = bf16[2560,256]{1,0:T(8,128)(2,1)} reshape(bf16[128,20,256]{2,1,0:T(8,128)(2,1)} %copy.51) | data formatting | bytes 2621440 | tf_op jit(solution)/shard_map/concatenate | solution.py:117
  70.7 3.6 %pad_maximum_fusion = bf16[2560,288]{1,0:T(8,128)(2,1)} fusion(bf16[2560,16]{1,0:T(8,128)(2,1)} %copy.55, bf16[2560,16]{1,0:T(8,128)(2,1)} %copy.54, bf16[2560,256]{1,0:T(8,128)(2,1)} %concatenate.15), kind=kLoop, calls=%fused_computation.92 | loop fusion | flops 4423680 | bytes 2949120 | tf_op jit(solution)/shard_map/concatenate | solution.py:117
  78.3 7.6 %all-to-all-start.1 = ((bf16[32,128,288]{1,2,0:T(8,128)(2,1)}), bf16[32,128,288]{1,2,0:T(8,128)(2,1)}, u32[]{:S(2)}, u32[]{:S(2)}) async-start(bf16[32,128,288]{1,2,0:T(8,128)(2,1)} %bitcast.124), calls=%async_computation.1 | async-start | bytes 4718592 | tf_op jit(solution)/shard_map/all_to_all | solution.py:130
  86.1 26.6 %while.56 = (s32[]{:T(128)}, f32[2560]{0:T(1024)S(1)}, f32[2560]{0:T(1024)S(1)}, f32[2560,256]{1,0:T(8,128)S(1)}, bf16[1024,288]{1,0:T(8,128)(2,1)}, /*index=5*/...) while((s32[]{:T(128)}, f32[2560]{0:T(1024)S(1)}, ...), condition=%wide.region_5.6_spmd.clone, body=%wide.region_2.5_spmd.clone.sunk | while | flops 1439840768 | bytes 44730576 | solution.py:66
  86.9 5.6 %fusion.144 = (f32[2560]{0:T(1024)S(1)}, f32[512,2560]{1,0:T(8,128)}) fusion(pred[512]{0:T(512)(128)(4,1)S(1)} %fusion.143, bf16[2560,288]{1,0:T(8,128)(2,1)} %get-tuple-element.708, bf16[1024,288]{1,0:T(8,128)(2,1)} %get-tuple-element.707, s32[]{:T(128)S(6)} %select_n.180), kind=kOutput, calls=%fused_computation.54.clone.1 | convolution fusion | flops 758904320 | bytes 7612932 | tf_op jit(solution)/shard_map/while/body/eval_jaxpr/rw,kw->rk/dot_general | solution.py:52
  92.5 3.5 %fusion.145 = f32[2560]{0:T(1024)S(1)} fusion(f32[512,2560]{1,0:T(8,128)} %get-tuple-element.678, f32[2560]{0:T(1024)S(1)} %select_maximum_fusion.2, pred[512]{0:T(512)(128)(4,1)S(1)} %fusion.143), kind=kLoop, calls=%fused_computation.59.clone.1 | loop fusion | flops 3929600 | bytes 5263872 | tf_op jit(solution)/shard_map/while/body/eval_jaxpr/reduce_sum | solution.py:60
  100.1 5.6 %fusion.144 = (f32[2560]{0:T(1024)S(1)}, f32[512,2560]{1,0:T(8,128)}) fusion(pred[512]{0:T(512)(128)(4,1)S(1)} %fusion.143, bf16[2560,288]{1,0:T(8,128)(2,1)} %get-tuple-element.708, bf16[1024,288]{1,0:T(8,128)(2,1)} %get-tuple-element.707, s32[]{:T(128)S(6)} %select_n.180), kind=kOutput, calls=%fused_computation.54.clone.1 | convolution fusion | flops 758904320 | bytes 7612932 | tf_op jit(solution)/shard_map/while/body/eval_jaxpr/rw,kw->rk/dot_general | solution.py:52
  105.7 3.7 %fusion.145 = f32[2560]{0:T(1024)S(1)} fusion(f32[512,2560]{1,0:T(8,128)} %get-tuple-element.678, f32[2560]{0:T(1024)S(1)} %select_maximum_fusion.2, pred[512]{0:T(512)(128)(4,1)S(1)} %fusion.143), kind=kLoop, calls=%fused_computation.59.clone.1 | loop fusion | flops 3929600 | bytes 5263872 | tf_op jit(solution)/shard_map/while/body/eval_jaxpr/reduce_sum | solution.py:60
  112.8 15.1 %all-to-all-done.1 = bf16[32,128,288]{1,2,0:T(8,128)(2,1)} async-done(((bf16[32,128,288]{1,2,0:T(8,128)(2,1)}), bf16[32,128,288]{1,2,0:T(8,128)(2,1)}, u32[]{:S(2)}, u32[]{:S(2)}) %all-to-all-start.1) | async-done | bytes 2359328 | tf_op jit(solution)/shard_map/all_to_all | solution.py:130
  127.8 4.5 %copy.62 = bf16[32,128,288]{2,1,0:T(8,128)(2,1)} copy(bf16[32,128,288]{1,2,0:T(8,128)(2,1)} %all-to-all-done.1) | data formatting | bytes 4718592
  132.3 61.4 %while.54 = (s32[]{:T(128)}, f32[2560]{0:T(1024)S(1)}, f32[2560]{0:T(1024)S(1)}, f32[2560,256]{1,0:T(8,128)S(1)}, bf16[4096,288]{1,0:T(8,128)(2,1)}, /*index=5*/...) while((s32[]{:T(128)}, f32[2560]{0:T(1024)S(1)}, ...), condition=%wide.region_9.10_spmd.clone, body=%wide.region_6.0_spmd.clone.sunk | while | flops 1439177728 | bytes 23759020 | solution.py:66
  132.9 3.3 %fusion.133 = (f32[2560]{0:T(1024)S(1)}, f32[512,2560]{1,0:T(8,128)S(1)}) fusion(pred[512]{0:T(512)(128)(4,1)S(1)} %fusion.132, bf16[2560,288]{1,0:T(8,128)(2,1)} %get-tuple-element.741, bf16[4096,288]{1,0:T(8,128)(2,1)} %get-tuple-element.740, s32[]{:T(128)S(6)} %select_n.172), kind=kOutput, calls=%fused_computation.7.clone.1 | convolution fusion | flops 758904320 | bytes 7612932 | tf_op jit(solution)/shard_map/while/body/eval_jaxpr/rw,kw->rk/dot_general | solution.py:52
  140.6 3.3 %fusion.133 = (f32[2560]{0:T(1024)S(1)}, f32[512,2560]{1,0:T(8,128)S(1)}) fusion(pred[512]{0:T(512)(128)(4,1)S(1)} %fusion.132, bf16[2560,288]{1,0:T(8,128)(2,1)} %get-tuple-element.741, bf16[4096,288]{1,0:T(8,128)(2,1)} %get-tuple-element.740, s32[]{:T(128)S(6)} %select_n.172), kind=kOutput, calls=%fused_computation.7.clone.1 | convolution fusion | flops 758904320 | bytes 7612932 | tf_op jit(solution)/shard_map/while/body/eval_jaxpr/rw,kw->rk/dot_general | solution.py:52
  148.3 3.3 %fusion.133 = (f32[2560]{0:T(1024)S(1)}, f32[512,2560]{1,0:T(8,128)S(1)}) fusion(pred[512]{0:T(512)(128)(4,1)S(1)} %fusion.132, bf16[2560,288]{1,0:T(8,128)(2,1)} %get-tuple-element.741, bf16[4096,288]{1,0:T(8,128)(2,1)} %get-tuple-element.740, s32[]{:T(128)S(6)} %select_n.172), kind=kOutput, calls=%fused_computation.7.clone.1 | convolution fusion | flops 758904320 | bytes 7612932 | tf_op jit(solution)/shard_map/while/body/eval_jaxpr/rw,kw->rk/dot_general | solution.py:52
  156.0 3.3 %fusion.133 = (f32[2560]{0:T(1024)S(1)}, f32[512,2560]{1,0:T(8,128)S(1)}) fusion(pred[512]{0:T(512)(128)(4,1)S(1)} %fusion.132, bf16[2560,288]{1,0:T(8,128)(2,1)} %get-tuple-element.741, bf16[4096,288]{1,0:T(8,128)(2,1)} %get-tuple-element.740, s32[]{:T(128)S(6)} %select_n.172), kind=kOutput, calls=%fused_computation.7.clone.1 | convolution fusion | flops 758904320 | bytes 7612932 | tf_op jit(solution)/shard_map/while/body/eval_jaxpr/rw,kw->rk/dot_general | solution.py:52
  163.6 3.3 %fusion.133 = (f32[2560]{0:T(1024)S(1)}, f32[512,2560]{1,0:T(8,128)S(1)}) fusion(pred[512]{0:T(512)(128)(4,1)S(1)} %fusion.132, bf16[2560,288]{1,0:T(8,128)(2,1)} %get-tuple-element.741, bf16[4096,288]{1,0:T(8,128)(2,1)} %get-tuple-element.740, s32[]{:T(128)S(6)} %select_n.172), kind=kOutput, calls=%fused_computation.7.clone.1 | convolution fusion | flops 758904320 | bytes 7612932 | tf_op jit(solution)/shard_map/while/body/eval_jaxpr/rw,kw->rk/dot_general | solution.py:52
  171.3 3.3 %fusion.133 = (f32[2560]{0:T(1024)S(1)}, f32[512,2560]{1,0:T(8,128)S(1)}) fusion(pred[512]{0:T(512)(128)(4,1)S(1)} %fusion.132, bf16[2560,288]{1,0:T(8,128)(2,1)} %get-tuple-element.741, bf16[4096,288]{1,0:T(8,128)(2,1)} %get-tuple-element.740, s32[]{:T(128)S(6)} %select_n.172), kind=kOutput, calls=%fused_computation.7.clone.1 | convolution fusion | flops 758904320 | bytes 7612932 | tf_op jit(solution)/shard_map/while/body/eval_jaxpr/rw,kw->rk/dot_general | solution.py:52
  179.0 3.3 %fusion.133 = (f32[2560]{0:T(1024)S(1)}, f32[512,2560]{1,0:T(8,128)S(1)}) fusion(pred[512]{0:T(512)(128)(4,1)S(1)} %fusion.132, bf16[2560,288]{1,0:T(8,128)(2,1)} %get-tuple-element.741, bf16[4096,288]{1,0:T(8,128)(2,1)} %get-tuple-element.740, s32[]{:T(128)S(6)} %select_n.172), kind=kOutput, calls=%fused_computation.7.clone.1 | convolution fusion | flops 758904320 | bytes 7612932 | tf_op jit(solution)/shard_map/while/body/eval_jaxpr/rw,kw->rk/dot_general | solution.py:52
  186.7 3.3 %fusion.133 = (f32[2560]{0:T(1024)S(1)}, f32[512,2560]{1,0:T(8,128)S(1)}) fusion(pred[512]{0:T(512)(128)(4,1)S(1)} %fusion.132, bf16[2560,288]{1,0:T(8,128)(2,1)} %get-tuple-element.741, bf16[4096,288]{1,0:T(8,128)(2,1)} %get-tuple-element.740, s32[]{:T(128)S(6)} %select_n.172), kind=kOutput, calls=%fused_computation.7.clone.1 | convolution fusion | flops 758904320 | bytes 7612932 | tf_op jit(solution)/shard_map/while/body/eval_jaxpr/rw,kw->rk/dot_general | solution.py:52
  193.7 18.4 %while.55 = (s32[]{:T(128)}, f32[2560]{0:T(1024)S(1)}, f32[2560]{0:T(1024)S(1)}, f32[2560,256]{1,0:T(8,128)S(1)}, bf16[1024,288]{1,0:T(8,128)(2,1)}, /*index=5*/...) while((s32[]{:T(128)}, f32[2560]{0:T(1024)S(1)}, ...), condition=%wide.region_14.15_spmd.clone, body=%wide.region_11.14_spmd.clone.sunk | while | flops 1447041536 | bytes 23829164 | solution.py:66
  194.2 3.5 %fusion.138 = (f32[2560]{0:T(1024)S(1)}, f32[512,2560]{1,0:T(8,128)S(1)}) fusion(s32[2560]{0:T(1024)S(1)} %lt.225, s32[512]{0:T(512)S(1)} %iota_add_fusion.5, pred[512]{0:T(512)(128)(4,1)S(1)} %broadcast_compare_fusion.2, bf16[2560,288]{1,0:T(8,128)(2,1)} %get-tuple-element.774, bf16[1024,288]{1,0:T(8,128)(2,1)} %get-tuple-element.773, ...), kind=kOutput, calls=%fused_computation.30.clone.1 | convolution fusion | flops 761525760 | bytes 7625220 | tf_op jit(solution)/shard_map/while/body/eval_jaxpr/rw,kw->rk/dot_general | solution.py:52
  199.7 3.4 %convolution_add_fusion.8 = f32[2560,256]{1,0:T(8,128)S(1)} fusion(f32[512,2560]{1,0:T(8,128)S(1)} %get-tuple-element.667, f32[2560,256]{1,0:T(8,128)S(1)} %get-tuple-element.761, f32[2560]{0:T(1024)S(1)} %max.29, s32[2560]{0:T(1024)S(1)} %lt.225, s32[512]{0:T(512)S(1)} %iota_add_fusion.5, pred[512]{0:T(512)(128)(4,1)S(1)} %broadcast_compare_fusion.2, ...), kind=kOutput, calls=%fused_computation.35.clone.1 | convolution fusion | flops 678952960 | bytes 10781188 | tf_op jit(solution)/shard_map/while/body/eval_jaxpr/dot_general | solution.py:61
  203.3 3.5 %fusion.138 = (f32[2560]{0:T(1024)S(1)}, f32[512,2560]{1,0:T(8,128)S(1)}) fusion(s32[2560]{0:T(1024)S(1)} %lt.225, s32[512]{0:T(512)S(1)} %iota_add_fusion.5, pred[512]{0:T(512)(128)(4,1)S(1)} %broadcast_compare_fusion.2, bf16[2560,288]{1,0:T(8,128)(2,1)} %get-tuple-element.774, bf16[1024,288]{1,0:T(8,128)(2,1)} %get-tuple-element.773, ...), kind=kOutput, calls=%fused_computation.30.clone.1 | convolution fusion | flops 761525760 | bytes 7625220 | tf_op jit(solution)/shard_map/while/body/eval_jaxpr/rw,kw->rk/dot_general | solution.py:52
  208.8 3.4 %convolution_add_fusion.8 = f32[2560,256]{1,0:T(8,128)S(1)} fusion(f32[512,2560]{1,0:T(8,128)S(1)} %get-tuple-element.667, f32[2560,256]{1,0:T(8,128)S(1)} %get-tuple-element.761, f32[2560]{0:T(1024)S(1)} %max.29, s32[2560]{0:T(1024)S(1)} %lt.225, s32[512]{0:T(512)S(1)} %iota_add_fusion.5, pred[512]{0:T(512)(128)(4,1)S(1)} %broadcast_compare_fusion.2, ...), kind=kOutput, calls=%fused_computation.35.clone.1 | convolution fusion | flops 678952960 | bytes 10781188 | tf_op jit(solution)/shard_map/while/body/eval_jaxpr/dot_general | solution.py:61
  216.5 3.9 %fusion.69 = bf16[128,2560]{1,0:T(8,128)(2,1)S(1)} fusion(bf16[128,1280]{0,1:T(8,128)(2,1)S(1)} %bitcast.129, bf16[1280,2560]{1,0:T(8,128)(2,1)} %param.34, bf16[128,2560]{1,0:T(8,128)(2,1)S(1)} %copy-done.5), kind=kOutput, calls=%fused_computation.89 | convolution fusion | flops 839843840 | bytes 8192000 | tf_op jit(solution)/shard_map/dot_general | solution.py:174
  222.7 33.0 %all-gather.5.cloned.1.call-done = bf16[512,2560]{1,0:T(8,128)(2,1)} async-done(((bf16[128,2560]{1,0:T(8,128)(2,1)}), bf16[512,2560]{1,0:T(8,128)(2,1)}) %all-gather.5.cloned.1.call-update) | async-done | bytes 2621456 | tf_op jit(solution)/shard_map/all_gather | solution.py:182
  255.7 6.7 %fusion.61 = f32[512,800]{0,1:T(8,128)} fusion(bf16[512,2560]{1,0:T(8,128)(2,1)} %all-gather.5.cloned.1.call-done, bf16[3,2560,800]{2,1,0:T(8,128)(2,1)} %all-gather.3.cloned.1.call-done), kind=kOutput, calls=%fused_computation.82 | convolution fusion | flops 2097152000 | bytes 8847360 | tf_op jit(solution)/shard_map/dot_general | solution.py:184
  262.3 11.8 %fusion.66 = bf16[512,2560]{1,0:T(8,128)(2,1)} fusion(bf16[3,2560,800]{2,1,0:T(8,128)(2,1)} %all-gather.3.cloned.1.call-done, f32[512,800]{0,1:T(8,128)} %fusion.61, bf16[512,2560]{1,0:T(8,128)(2,1)} %all-gather.5.cloned.1.call-done), kind=kOutput, calls=%fused_computation.87 | convolution fusion | flops 4198072320 | bytes 16056320 | tf_op jit(solution)/shard_map/dot_general | solution.py:187
  274.2 34.2 %reduce-scatter.2.cloned.1.call-done = bf16[128,2560]{1,0:T(8,128)(2,1)} async-done(((bf16[512,2560]{1,0:T(8,128)(2,1)}), bf16[128,2560]{1,0:T(8,128)(2,1)}) %reduce-scatter.2.cloned.1.call-update) | async-done | bytes 655376 | tf_op jit(solution)/shard_map/reduce_scatter | solution.py:190
  (175 shorter events, 97.4 us)
Async XLA Ops:
  7.2 29.6 %copy-start = (bf16[768,1920]{1,0:T(8,128)(2,1)S(1)}, bf16[768,1920]{1,0:T(8,128)(2,1)}, u32[]{:S(2)}) copy-start(bf16[768,1920]{1,0:T(8,128)(2,1)} %param.29) | copy-start | bytes 8847364
  7.2 8.3 %copy-start.15 = (bf16[256]{0:T(256)(128)(2,1)S(1)}, bf16[256]{0:T(256)(128)(2,1)}, u32[]{:S(2)}) copy-start(bf16[256]{0:T(256)(128)(2,1)} %param.31) | copy-start | bytes 1540
  7.2 8.9 %copy-start.16 = (s32[8]{0:T(128)S(1)}, s32[8]{0:T(128)}, u32[]{:S(2)}) copy-start(s32[8]{0:T(128)} %param.42) | copy-start | bytes 100
  13.2 4.9 %copy-start.12 = (f32[128]{0:T(128)}, f32[128]{0:T(128)S(1)}, u32[]{:S(2)}) copy-start(f32[128]{0:T(128)S(1)} %add_rsqrt_fusion.3) | copy-start | bytes 1540
  13.2 16.9 %copy-start.2 = (s32[16]{0:T(128)S(1)}, s32[16]{0:T(128)}, u32[]{:S(2)}) copy-start(s32[16]{0:T(128)} %param.43) | copy-start | bytes 196
  18.9 0.6 copy-start.7
  20.4 23.8 %all-to-all-start.2 = ((bf16[8,128,288]{1,2,0:T(8,128)(2,1)}), bf16[8,128,288]{1,2,0:T(8,128)(2,1)S(1)}, u32[]{:S(2)}, u32[]{:S(2)}) async-start(bf16[8,128,288]{1,2,0:T(8,128)(2,1)} %broadcast_in_dim.116), calls=%async_computation.2 | async-start | bytes 1179648 | tf_op jit(solution)/shard_map/all_to_all | solution.py:125
  27.5 193.0 %all-gather.3.cloned.1.call-start = ((), (), s32[]{:S(2)}) async-start(), calls=%async_computation.4 | async-start | bytes 14192640 | tf_op jit(solution)/shard_map/all_gather | solution.py:175
  31.3 5.5 %copy-start.11 = (bf16[768]{0:T(1024)(128)(2,1)S(1)}, bf16[768]{0:T(1024)(128)(2,1)}, u32[]{:S(2)}) copy-start(bf16[768]{0:T(1024)(128)(2,1)} %param.28) | copy-start | bytes 4612
  36.8 4.1 %copy-start.14 = (s32[4]{0:T(128)S(1)}, s32[4]{0:T(128)}, u32[]{:S(2)}) copy-start(s32[4]{0:T(128)} %fusion.96) | copy-start | bytes 52
  36.8 5.6 %copy-start.13 = (pred[4]{0:T(512)(128)(4,1)S(1)}, pred[4]{0:T(512)(128)(4,1)}, u32[]{:S(2)}) copy-start(pred[4]{0:T(512)(128)(4,1)} %compare_and_fusion.1) | copy-start | bytes 16
  42.5 11.4 %copy-start.8 = (f32[128,16]{0,1:T(8,128)S(1)}, f32[128,16]{0,1:T(8,128)}, u32[]{:S(2)}) copy-start(f32[128,16]{0,1:T(8,128)} %get-tuple-element.524) | copy-start | bytes 24580
  42.5 11.4 %copy-start.9 = (f32[128,16]{0,1:T(8,128)S(1)}, f32[128,16]{0,1:T(8,128)}, u32[]{:S(2)}) copy-start(f32[128,16]{0,1:T(8,128)} %get-tuple-element.525) | copy-start | bytes 24580
  45.2 30.3 %all-to-all-start = ((bf16[32,32,288]{2,1,0:T(8,128)(2,1)}), bf16[32,32,288]{2,1,0:T(8,128)(2,1)}, u32[]{:S(2)}, u32[]{:S(2)}) async-start(bf16[32,32,288]{2,1,0:T(8,128)(2,1)} %bitcast.3), calls=%async_computation | async-start | bytes 1572864 | tf_op jit(solution)/shard_map/all_to_all | solution.py:135
  65.2 5.5 %copy-start.10 = (bf16[2560]{0:T(1024)(128)(2,1)S(1)}, bf16[2560]{0:T(1024)(128)(2,1)}, u32[]{:S(2)}) copy-start(bf16[2560]{0:T(1024)(128)(2,1)} %param.35) | copy-start | bytes 15364
  78.3 49.6 %all-to-all-start.1 = ((bf16[32,128,288]{1,2,0:T(8,128)(2,1)}), bf16[32,128,288]{1,2,0:T(8,128)(2,1)}, u32[]{:S(2)}, u32[]{:S(2)}) async-start(bf16[32,128,288]{1,2,0:T(8,128)(2,1)} %bitcast.124), calls=%async_computation.1 | async-start | bytes 4718592 | tf_op jit(solution)/shard_map/all_to_all | solution.py:130
  85.9 169.8 %all-gather.5.cloned.1.call-start = ((), (), s32[]{:S(2)}) async-start(), calls=%async_computation.5 | async-start | bytes 3276800 | tf_op jit(solution)/shard_map/all_gather | solution.py:182
  92.5 4.0 %copy-start.3 = (f32[512,2560]{1,0:T(8,128)S(1)}, f32[512,2560]{1,0:T(8,128)}, u32[]{:S(2)}) copy-start(f32[512,2560]{1,0:T(8,128)} %get-tuple-element.678) | copy-start | bytes 15728644 | tf_op jit(solution)/shard_map/while
  105.7 4.2 %copy-start.3 = (f32[512,2560]{1,0:T(8,128)S(1)}, f32[512,2560]{1,0:T(8,128)}, u32[]{:S(2)}) copy-start(f32[512,2560]{1,0:T(8,128)} %get-tuple-element.678) | copy-start | bytes 15728644 | tf_op jit(solution)/shard_map/while
  213.6 2.3 copy-start.6
  213.6 2.9 copy-start.5
  220.5 0.8 copy-start.4
  222.4 86.0 %reduce-scatter.2.cloned.1.call-start = ((), (), s32[]{:S(2)}) async-start(), calls=%async_computation.6 | async-start | bytes 3276800 | tf_op jit(solution)/shard_map/reduce_scatter | solution.py:190
  262.3 48.4 %copy-start.1 = (bf16[768,1920]{1,0:T(8,128)(2,1)S(1)}, bf16[768,1920]{1,0:T(8,128)(2,1)}, u32[]{:S(2)}) copy-start(bf16[768,1920]{1,0:T(8,128)(2,1)} %param.29) | copy-start | bytes 8847364
Sparse Core Ops, SparseCore 0:
  30.7 96.0 all-gather.2
  222.5 33.1 all-gather.4
  274.3 34.0 reduce-scatter.1

commit v3 on v2

--- a/solution.py
+++ b/solution.py
@@ -2,6 +2,9 @@
 import jax.numpy as jnp
 from jax import lax
 from jax.sharding import Mesh, PartitionSpec as P
+import functools
+from jax.experimental import pallas as pl
+from jax.experimental.pallas import tpu as pltpu
 
 KVR = 256
 HEADS = 20
@@ -38,6 +41,83 @@
     return jnp.concatenate(
         [leading * cosine - trailing * sine_part, trailing * cosine + leading * sine_part], axis=-1
     )
+
+
+KEY_BLOCK = 1024
+ROW_BLOCK = 640
+
+
+def flash_kernel(lims_ref, lim_row_ref, q_ref, kp_ref, kc_ref, ks_ref, o_ref, m_sc, l_sc, acc_sc, *, cache_blocks, score_scale, value_width):
+    j = pl.program_id(1)
+    last = cache_blocks + 1
+
+    @pl.when(j == 0)
+    def _init():
+        m_sc[...] = jnp.full(m_sc.shape, -1e30, jnp.float32)
+        l_sc[...] = jnp.zeros(l_sc.shape, jnp.float32)
+        acc_sc[...] = jnp.zeros(acc_sc.shape, jnp.float32)
+
+    def step(k_ref, base, limit):
+        keys = k_ref[...]
+        scores = lax.dot_general(q_ref[...], keys, (((1,), (1,)), ((), ())), preferred_element_type=jnp.float32) * score_scale
+        place = lax.broadcasted_iota(jnp.int32, scores.shape, 1) + base
+        live = place < limit
+        m_old = m_sc[...]
+        m_new = jnp.maximum(m_old, jnp.max(jnp.where(live, scores, -1e30), axis=1, keepdims=True))
+        weights = jnp.where(live, jnp.exp(scores - m_new), 0.0)
+        factor = jnp.exp(m_old - m_new)
+        l_sc[...] = l_sc[...] * factor + jnp.sum(weights, axis=1, keepdims=True)
+        acc_sc[...] = acc_sc[...] * factor + jnp.dot(weights.astype(jnp.bfloat16), keys[:, :value_width], preferred_element_type=jnp.float32)
+        m_sc[...] = m_new
+
+    rows = q_ref.shape[0]
+
+    @pl.when(j == 0)
+    def _prompt():
+        step(kp_ref, 0, jnp.full((rows, 1), lims_ref[0], jnp.int32))
+
+    @pl.when(jnp.logical_and(j >= 1, j < last))
+    def _cache():
+        step(kc_ref, (j - 1) * KEY_BLOCK, jnp.full((rows, 1), lims_ref[1], jnp.int32))
+
+    @pl.when(j == last)
+    def _span():
+        step(ks_ref, 0, lim_row_ref[...])
+        o_ref[...] = (acc_sc[...] / l_sc[...]).astype(o_ref.dtype)
+
+
+def flash_attend(lims, lim_rows, queries, prompt_rows, cache_rows, span_rows, score_scale, value_width, interpret=False):
+    row_count, width = queries.shape
+    cache_blocks = cache_rows.shape[0] // KEY_BLOCK
+    assert prompt_rows.shape[0] == KEY_BLOCK and span_rows.shape[0] == KEY_BLOCK
+    assert cache_blocks * KEY_BLOCK == cache_rows.shape[0] and row_count % ROW_BLOCK == 0
+    grid = (row_count // ROW_BLOCK, cache_blocks + 2)
+    key_spec = pl.BlockSpec((KEY_BLOCK, width), lambda i, j, lims: (0, 0))
+    cache_spec = pl.BlockSpec((KEY_BLOCK, width), lambda i, j, lims: (jnp.minimum(jnp.maximum(j - 1, 0), cache_blocks - 1), 0))
+    kernel = functools.partial(flash_kernel, cache_blocks=cache_blocks, score_scale=score_scale, value_width=value_width)
+    return pl.pallas_call(
+        kernel,
+        grid_spec=pltpu.PrefetchScalarGridSpec(
+            num_scalar_prefetch=1,
+            grid=grid,
+            in_specs=[
+                pl.BlockSpec((ROW_BLOCK, 1), lambda i, j, lims: (i, 0)),
+                pl.BlockSpec((ROW_BLOCK, width), lambda i, j, lims: (i, 0)),
+                key_spec,
+                cache_spec,
+                key_spec,
+            ],
+            out_specs=pl.BlockSpec((ROW_BLOCK, value_width), lambda i, j, lims: (i, 0)),
+            scratch_shapes=[
+                pltpu.VMEM((ROW_BLOCK, 1), jnp.float32),
+                pltpu.VMEM((ROW_BLOCK, 1), jnp.float32),
+                pltpu.VMEM((ROW_BLOCK, value_width), jnp.float32),
+            ],
+        ),
+        out_shape=jax.ShapeDtypeStruct((row_count, value_width), jnp.bfloat16),
+        compiler_params=pltpu.CompilerParams(dimension_semantics=("arbitrary", "arbitrary")),
+        interpret=interpret,
+    )(lims, lim_rows, queries, prompt_rows, cache_rows, span_rows)
 
 
 def attend_segment(
@@ -136,31 +216,12 @@
         jnp.tile(prompt_send, (span_blocks, 1, 1)), ("tq", "tr"), 0, 0, tiled=True
     ).reshape(-1, latent_width)
     query_rows = queries.reshape(tok_dev * HEADS, latent_width)
-    row_count = tok_dev * HEADS
     score_scale = 1.0 / (NOPE + ROPE) ** 0.5
-    softmax_state = (
-        jnp.full((row_count,), -1e30, jnp.float32),
-        jnp.zeros((row_count,), jnp.float32),
-        jnp.zeros((row_count, KVR), jnp.float32),
-    )
-    no_lower = jnp.zeros((tok_dev,), jnp.int32)
-    segments = (
-        (prompt_rows, no_lower, jnp.broadcast_to(prompt_live, (tok_dev,))),
-        (cache_rows, no_lower, jnp.broadcast_to(cache_live, (tok_dev,))),
-        (span_rows, span_lower, span_limit),
-    )
-    for key_rows, token_lower, token_limit in segments:
-        lowers = jnp.repeat(token_lower, HEADS)
-        limits = jnp.repeat(token_limit, HEADS)
-        key_block = min(512, key_rows.shape[0])
-        block_count = key_rows.shape[0] // key_block
-        softmax_state = attend_segment(
-            softmax_state, query_rows, key_rows, lowers, limits, block_count, key_block, score_scale
-        )
-    running_max, running_sum, running_out = softmax_state
-    latent_out = (
-        (running_out / running_sum[:, None]).astype(jnp.bfloat16).reshape(tok_dev, HEADS, KVR)
-    )
+    lims = jnp.stack([prompt_live, cache_live]).astype(jnp.int32)
+    lim_rows = jnp.repeat(span_limit, HEADS)[:, None]
+    latent_out = flash_attend(
+        lims, lim_rows, query_rows, prompt_rows, cache_rows, span_rows, score_scale, KVR
+    ).reshape(tok_dev, HEADS, KVR)
     heads_out = (
         jnp.einsum(
             "thk,khv->thv",

time: 320 us -> 307 us (0.959)
  matrix products: 110 us -> 28.5 us
  Pallas kernels: 0 us -> 66 us
  waiting for transfers between devices: 82.4 us -> 128 us
  other arithmetic: 42.1 us -> 14.9 us
  local copies, waits for them, and re-layouts: 40.5 us -> 32.1 us
  starting transfers between devices: 24 us -> 18.6 us
    dot_general x24 -> x0, matrix products: 78.6 us -> none  [the longest x12 44.8 us: fold_block(): jnp.einsum('rw,kw->rk', queries, key_piece, preferred_element_type=jnp.fl...]
    pallas_call x0 -> x1, Pallas kernels: none -> 66 us  [flash_attend(): pl.pallas_call(kernel, grid_spec=pltpu.PrefetchScalarGridSpec(num_scalar_...]
    all_to_all x1, waiting for transfers between devices: 15.1 us -> 44.9 us  [body(): lax.all_to_all(jnp.tile(cache_latents, (span_blocks, 1, 1)), ('tq', 'tr')...]
    reduce_sum x12 -> x0, other arithmetic: 19.3 us -> none  [fold_block(): running_sum = running_sum * factor + jnp.sum(weights, axis=1)]
    all_to_all x1, waiting for transfers between devices: 0.01 us -> 12.4 us  [body(): lax.all_to_all(jnp.broadcast_to(new_latents, (span_blocks,) + new_latents...]
    and x10 -> x0, other arithmetic: 5.99 us -> none  [fold_block(): jnp.logical_and(key_place >= lowers[:, None], key_place < limits[:, None])]
    all_to_all x0 -> x2, local copies, waits for them, and re-layouts: none -> 5.68 us  [the longest x1 4.48 us: body(): lax.all_to_all(jnp.tile(cache_latents, (span_blocks, 1, 1)), ('tq', 'tr')...]
    unnamed x36 -> x32, local copies, waits for them, and re-layouts: 10.5 us -> 4.81 us
  transfers between devices with their start and end apart: 6 -> 6, of which waited for: 3 -> 4; matrix products, arithmetic and copies ran while one was open for 50% -> 17% of each run, Pallas kernels for 0% -> 22%
where the time goes in v3:
time: 307 us; the launch traced here: 305 us
  waiting for transfers between devices  128 us (42%)
  Pallas kernels  66 us (21%)
  local copies, waits for them, and re-layouts  32.1 us (10%)
  matrix products  28.5 us (9%)
  starting transfers between devices  18.6 us (6%)
  between operations  17.3 us (6%)
  other arithmetic  14.9 us (5%)
    pallas_call x1, Pallas kernels, flash_attend(): pl.pallas_call(kernel, grid_spec=pltpu.PrefetchScalarGridSpec(num_scalar_...  66 us
    all_to_all x1, waiting for transfers between devices, body(): lax.all_to_all(jnp.tile(cache_latents, (span_blocks, 1, 1)), ('tq', 'tr')...  44.9 us
    all_gather x1, waiting for transfers between devices, body(): rows_all = lax.all_gather(post_norm, 'grp', axis=0, tiled=True)  36.2 us
    reduce_scatter x1, waiting for transfers between devices, body(): lax.psum_scatter(partial_out.astype(jnp.bfloat16), 'grp', scatter_dimensi...  34.2 us
    all_to_all x1, waiting for transfers between devices, body(): lax.all_to_all(jnp.broadcast_to(new_latents, (span_blocks,) + new_latents...  12.4 us
    dot_general x1, matrix products, body(): lax.dot_general(hidden, down_full, (((1,), (1,)), ((), ())), preferred_el...  11.2 us
    all_to_all x1, starting transfers between devices, body(): lax.all_to_all(jnp.broadcast_to(new_latents, (span_blocks,) + new_latents...  7.16 us
  transfers between devices with their start and end apart: 6, of which 4 were waited for; matrix products, arithmetic and copies ran while one was open for 17% of the time, Pallas kernels for 22%

profile of v3, /device:TPU:8, one launch (start us, length us, event | category | flops | bytes accessed | tf_op | source)
XLA Modules:
  0.0 305.1 jit_solution(3642330998339649439)
XLA Ops:
  7.2 2.1 pad_maximum_fusion.1
  9.3 1.2 dynamic_slice.9
  11.9 1.3 dynamic_slice.11
  15.2 1.3 dynamic_slice.10
  18.3 1.3 fusion.18
  19.7 2.2 fusion.34
  24.3 7.2 %all-to-all-start.2 = ((bf16[8,128,288]{1,2,0:T(8,128)(2,1)}), bf16[8,128,288]{1,2,0:T(8,128)(2,1)S(1)}, u32[]{:S(2)}, u32[]{:S(2)}) async-start(bf16[8,128,288]{1,2,0:T(8,128)(2,1)} %broadcast_in_dim.14), calls=%async_computation.2 | async-start | bytes 1179648 | tf_op jit(solution)/shard_map/all_to_all | solution.py:205
  32.1 12.4 %all-to-all-done.2 = bf16[8,128,288]{1,2,0:T(8,128)(2,1)S(1)} async-done(((bf16[8,128,288]{1,2,0:T(8,128)(2,1)}), bf16[8,128,288]{1,2,0:T(8,128)(2,1)S(1)}, u32[]{:S(2)}, u32[]{:S(2)}) %all-to-all-start.2) | async-done | bytes 589856 | tf_op jit(solution)/shard_map/all_to_all | solution.py:205
  44.5 2.8 tile.20
  47.3 5.5 %all-to-all-start.1 = ((bf16[32,128,288]{1,2,0:T(8,128)(2,1)}), bf16[32,128,288]{1,2,0:T(8,128)(2,1)}, u32[]{:S(2)}, u32[]{:S(2)}) async-start(bf16[32,128,288]{1,2,0:T(8,128)(2,1)} %bitcast.55), calls=%async_computation.1 | async-start | bytes 4718592 | tf_op jit(solution)/shard_map/all_to_all | solution.py:210
  52.7 3.1 %multiply_reduce_fusion = (f32[128]{0:T(128)S(1)}, f32[128,768]{1,0:T(8,128)S(1)}) fusion(bf16[2560,768]{1,0:T(8,128)(2,1)} %param.21, bf16[128,2560]{1,0:T(8,128)(2,1)} %param.19, f32[2560]{0:T(1024)S(1)} %convert_element_type.68, f32[128]{0:T(128)} %copy-done.14), kind=kOutput, calls=%fused_computation.37 | convolution fusion | flops 504823680 | bytes 4992000 | tf_op jit(solution)/shard_map/dot_general | solution.py:184
  55.9 1.4 convolution_convert_fusion
  57.3 1.4 copy.42
  58.7 1.3 copy.43
  62.7 44.9 %all-to-all-done.1 = bf16[32,128,288]{1,2,0:T(8,128)(2,1)} async-done(((bf16[32,128,288]{1,2,0:T(8,128)(2,1)}), bf16[32,128,288]{1,2,0:T(8,128)(2,1)}, u32[]{:S(2)}, u32[]{:S(2)}) %all-to-all-start.1) | async-done | bytes 2359328 | tf_op jit(solution)/shard_map/all_to_all | solution.py:210
  107.6 1.9 tile.8
  109.4 5.6 %all-to-all-start = ((bf16[32,32,288]{2,1,0:T(8,128)(2,1)}), bf16[32,32,288]{2,1,0:T(8,128)(2,1)}, u32[]{:S(2)}, u32[]{:S(2)}) async-start(bf16[32,32,288]{2,1,0:T(8,128)(2,1)} %bitcast.8), calls=%async_computation | async-start | bytes 1572864 | tf_op jit(solution)/shard_map/all_to_all | solution.py:215
  116.4 1.1 copy.47
  121.2 1.5 broadcast_in_dim_reshape.4.lim_row_ref
  122.7 2.2 copy.52
  124.9 1.9 pad_add_fusion.lims_ref
  126.8 1.7 pad_maximum_fusion.q_ref
  128.5 1.2 copy.50
  129.7 4.5 %copy.49 = bf16[32,128,288]{2,1,0:T(8,128)(2,1)} copy(bf16[32,128,288]{1,2,0:T(8,128)(2,1)} %all-to-all-done.1) | data formatting | bytes 4718592 | tf_op jit(solution)/shard_map/all_to_all | solution.py:210
  134.2 66.0 %shard_map.194 = bf16[2560,256]{1,0:T(8,128)(2,1)} custom-call(s32[2]{0:T(128)} %pad_add_fusion.lims_ref, s32[2560,1]{1,0:T(8,128)} %broadcast_in_dim_reshape.4.lim_row_ref, bf16[2560,288]{1,0:T(8,128)(2,1)} %pad_maximum_fusion.q_ref, bf16[1024,288]{1,0:T(8,128)(2,1)} %bitcast.9.kp_ref, bf16[4096,288]{1,0:T(8,128)(2,1)} %bitcast.54, bf16[1024,288]{1,0:T(8,128)(2,1)} %bitcast.56), custom_call_target="tpu_custom_call" | custom-call | tf_op jit(solution)/shard_map/pallas_call | solution.py:98
  200.2 2.3 reshape.182
  203.6 3.9 %fusion.12 = bf16[128,2560]{1,0:T(8,128)(2,1)S(1)} fusion(bf16[128,1280]{0,1:T(8,128)(2,1)S(1)} %bitcast.60, bf16[1280,2560]{1,0:T(8,128)(2,1)} %param.28, bf16[128,2560]{1,0:T(8,128)(2,1)S(1)} %copy-done.4), kind=kOutput, calls=%fused_computation.13 | convolution fusion | flops 839843840 | bytes 8192000 | tf_op jit(solution)/shard_map/dot_general | solution.py:235
  209.1 36.2 %all-gather.5.cloned.1.call-done = bf16[512,2560]{1,0:T(8,128)(2,1)} async-done(((bf16[128,2560]{1,0:T(8,128)(2,1)}), bf16[512,2560]{1,0:T(8,128)(2,1)}) %all-gather.5.cloned.1.call-update) | async-done | bytes 2621456 | tf_op jit(solution)/shard_map/all_gather | solution.py:243
  245.3 5.5 %fusion.4 = f32[512,800]{0,1:T(8,128)S(1)} fusion(bf16[512,2560]{1,0:T(8,128)(2,1)} %all-gather.5.cloned.1.call-done, bf16[3,2560,800]{2,1,0:T(8,128)(2,1)} %all-gather.3.cloned.1.call-done), kind=kOutput, calls=%fused_computation.6 | convolution fusion | flops 2097152000 | bytes 8847360 | tf_op jit(solution)/shard_map/dot_general | solution.py:245
  250.8 11.2 %fusion.9 = bf16[512,2560]{1,0:T(8,128)(2,1)} fusion(bf16[3,2560,800]{2,1,0:T(8,128)(2,1)} %all-gather.3.cloned.1.call-done, f32[512,800]{0,1:T(8,128)S(1)} %fusion.4, bf16[512,2560]{1,0:T(8,128)(2,1)} %all-gather.5.cloned.1.call-done), kind=kOutput, calls=%fused_computation.11 | convolution fusion | flops 4198072320 | bytes 16056320 | tf_op jit(solution)/shard_map/dot_general | solution.py:248
  262.0 34.2 %reduce-scatter.2.cloned.1.call-done = bf16[128,2560]{1,0:T(8,128)(2,1)} async-done(((bf16[512,2560]{1,0:T(8,128)(2,1)}), bf16[128,2560]{1,0:T(8,128)(2,1)}) %reduce-scatter.2.cloned.1.call-update) | async-done | bytes 655376 | tf_op jit(solution)/shard_map/reduce_scatter | solution.py:251
  296.3 2.3 fusion.24
  (75 shorter events, 15.3 us)
Async XLA Ops:
  7.2 48.7 %copy-start = (bf16[768,1920]{1,0:T(8,128)(2,1)S(1)}, bf16[768,1920]{1,0:T(8,128)(2,1)}, u32[]{:S(2)}) copy-start(bf16[768,1920]{1,0:T(8,128)(2,1)} %param.23) | copy-start | bytes 8847364
  7.2 200.4 %all-gather.3.cloned.1.call-start = ((), (), s32[]{:S(2)}) async-start(), calls=%async_computation.4 | async-start | bytes 14192640 | tf_op jit(solution)/shard_map/all_gather | solution.py:236
  19.6 4.6 %copy-start.14 = (f32[128]{0:T(128)}, f32[128]{0:T(128)S(1)}, u32[]{:S(2)}) copy-start(f32[128]{0:T(128)S(1)} %add_rsqrt_fusion.3) | copy-start | bytes 1540
  22.8 0.6 copy-start.8
  24.3 20.2 %all-to-all-start.2 = ((bf16[8,128,288]{1,2,0:T(8,128)(2,1)}), bf16[8,128,288]{1,2,0:T(8,128)(2,1)S(1)}, u32[]{:S(2)}, u32[]{:S(2)}) async-start(bf16[8,128,288]{1,2,0:T(8,128)(2,1)} %broadcast_in_dim.14), calls=%async_computation.2 | async-start | bytes 1179648 | tf_op jit(solution)/shard_map/all_to_all | solution.py:205
  47.3 60.3 %all-to-all-start.1 = ((bf16[32,128,288]{1,2,0:T(8,128)(2,1)}), bf16[32,128,288]{1,2,0:T(8,128)(2,1)}, u32[]{:S(2)}, u32[]{:S(2)}) async-start(bf16[32,128,288]{1,2,0:T(8,128)(2,1)} %bitcast.55), calls=%async_computation.1 | async-start | bytes 4718592 | tf_op jit(solution)/shard_map/all_to_all | solution.py:210
  57.3 2.8 copy-start.2
  57.3 3.4 %copy-start.9 = (bf16[8,32,288]{2,1,0:T(8,128)(2,1)S(1)}, bf16[8,32,288]{2,1,0:T(8,128)(2,1)}, u32[]{:S(2)}) copy-start(bf16[8,32,288]{2,1,0:T(8,128)(2,1)} %param.34) | copy-start | bytes 442372
  62.6 52.5 %copy-start.10 = (f32[128,16]{0,1:T(8,128)S(1)}, f32[128,16]{0,1:T(8,128)}, u32[]{:S(2)}) copy-start(f32[128,16]{0,1:T(8,128)} %get-tuple-element.10) | copy-start | bytes 24580
  62.7 52.5 %copy-start.11 = (f32[128,16]{0,1:T(8,128)S(1)}, f32[128,16]{0,1:T(8,128)}, u32[]{:S(2)}) copy-start(f32[128,16]{0,1:T(8,128)} %get-tuple-element.11) | copy-start | bytes 24580
  109.4 24.8 %all-to-all-start = ((bf16[32,32,288]{2,1,0:T(8,128)(2,1)}), bf16[32,32,288]{2,1,0:T(8,128)(2,1)}, u32[]{:S(2)}, u32[]{:S(2)}) async-start(bf16[32,32,288]{2,1,0:T(8,128)(2,1)} %bitcast.8), calls=%async_computation | async-start | bytes 1572864 | tf_op jit(solution)/shard_map/all_to_all | solution.py:215
  115.1 130.2 %all-gather.5.cloned.1.call-start = ((), (), s32[]{:S(2)}) async-start(), calls=%async_computation.5 | async-start | bytes 3276800 | tf_op jit(solution)/shard_map/all_gather | solution.py:243
  120.5 0.7 copy-start.13
  121.0 3.9 %copy-start.12 = (bf16[2560]{0:T(1024)(128)(2,1)S(1)}, bf16[2560]{0:T(1024)(128)(2,1)}, u32[]{:S(2)}) copy-start(bf16[2560]{0:T(1024)(128)(2,1)} %param.29) | copy-start | bytes 15364
  121.0 5.8 %copy-start.5 = (bf16[2560,16]{1,0:T(8,128)(2,1)S(1)}, bf16[2560,16]{1,0:T(8,128)(2,1)}, u32[]{:S(2)}) copy-start(bf16[2560,16]{1,0:T(8,128)(2,1)} %copy.47) | copy-start | bytes 245764
  121.0 5.8 %copy-start.6 = (bf16[2560,16]{1,0:T(8,128)(2,1)S(1)}, bf16[2560,16]{1,0:T(8,128)(2,1)}, u32[]{:S(2)}) copy-start(bf16[2560,16]{1,0:T(8,128)(2,1)} %copy.48) | copy-start | bytes 245764
  200.2 2.3 copy-start.7
  202.5 1.1 copy-start.4
  207.5 43.3 %copy-start.3 = (bf16[128,2560]{1,0:T(8,128)(2,1)}, bf16[128,2560]{1,0:T(8,128)(2,1)S(1)}, u32[]{:S(2)}) copy-start(bf16[128,2560]{1,0:T(8,128)(2,1)S(1)} %fusion.12) | copy-start | bytes 1966084
  208.9 87.4 %reduce-scatter.2.cloned.1.call-start = ((), (), s32[]{:S(2)}) async-start(), calls=%async_computation.6 | async-start | bytes 3276800 | tf_op jit(solution)/shard_map/reduce_scatter | solution.py:251
  262.0 36.5 %copy-start.1 = (bf16[768,1920]{1,0:T(8,128)(2,1)S(1)}, bf16[768,1920]{1,0:T(8,128)(2,1)}, u32[]{:S(2)}) copy-start(bf16[768,1920]{1,0:T(8,128)(2,1)} %param.23) | copy-start | bytes 8847364
Sparse Core Ops, SparseCore 0:
  10.4 96.5 all-gather.2
  209.0 36.2 all-gather.4
  262.1 34.0 reduce-scatter.1

commit v4 on v3

--- a/solution.py
+++ b/solution.py
@@ -240,7 +240,23 @@
         ((tokens.astype(jnp.float32) + attended).astype(jnp.bfloat16), weights_full)
     )
     post_norm = norm_rows(residual.astype(jnp.float32), post_gain).astype(jnp.bfloat16)
-    rows_all = lax.all_gather(post_norm, "grp", axis=0, tiled=True)
+    half_width = post_norm.shape[1] // 2
+    group_count = lax.axis_size("grp")
+    rows_all = jnp.concatenate(
+        [
+            lax.all_gather(post_norm[:, :half_width], "grp", axis=0, tiled=True),
+            lax.all_to_all(
+                jnp.broadcast_to(
+                    post_norm[:, half_width:], (group_count, tok_dev, half_width)
+                ),
+                "grp",
+                0,
+                0,
+                tiled=True,
+            ).reshape(group_count * tok_dev, half_width),
+        ],
+        axis=1,
+    )
     gate_full, up_full, down_full = weights_full
     gate_values = jnp.dot(rows_all, gate_full, preferred_element_type=jnp.float32)
     up_values = jnp.dot(rows_all, up_full, preferred_element_type=jnp.float32)
@@ -248,9 +264,24 @@
     partial_out = lax.dot_general(
         hidden, down_full, (((1,), (1,)), ((), ())), preferred_element_type=jnp.float32
     )
-    down_values = lax.psum_scatter(
-        partial_out.astype(jnp.bfloat16), "grp", scatter_dimension=0, tiled=True
-    ).astype(jnp.float32)
+    partial_out = partial_out.astype(jnp.bfloat16)
+    down_values = jnp.concatenate(
+        [
+            lax.psum_scatter(
+                partial_out[:, :half_width], "grp", scatter_dimension=0, tiled=True
+            ).astype(jnp.float32),
+            lax.all_to_all(
+                partial_out[:, half_width:].reshape(group_count, tok_dev, half_width),
+                "grp",
+                0,
+                0,
+                tiled=True,
+            )
+            .astype(jnp.float32)
+            .sum(axis=0),
+        ],
+        axis=1,
+    )
     layer_out = (residual.astype(jnp.float32) + down_values).astype(jnp.bfloat16)
     return (layer_out, new_latents)
 

time: 307 us -> 306 us (level)
  waiting for transfers between devices: 128 us -> 59.7 us
  blocking collectives: 0 us -> 61.5 us
  local copies, waits for them, and re-layouts: 32.1 us -> 35.9 us
    all_to_all x0 -> x2, blocking collectives: none -> 61.5 us  [the longest x1 30.8 us: body(): lax.all_to_all(partial_out[:, half_width:].reshape(group_count, tok_dev,...]
    all_gather x1, waiting for transfers between devices: 36.2 us -> 2.14 us  [body(): lax.all_gather(post_norm[:, :half_width], 'grp', axis=0, tiled=True)]
    reduce_scatter x1, waiting for transfers between devices: 34.2 us -> 0.23 us  [body(): lax.psum_scatter(partial_out[:, :half_width], 'grp', scatter_dimension=0,...]
    slice x0 -> x2, local copies, waits for them, and re-layouts: none -> 3.74 us  [the longest x1 2.97 us: body(): partial_out[:, :half_width]]
where the time goes in v4:
time: 306 us; the launch traced here: 304 us
  Pallas kernels  66 us (22%)
  blocking collectives  61.5 us (20%)
  waiting for transfers between devices  59.7 us (20%)
  local copies, waits for them, and re-layouts  35.9 us (12%)
  matrix products  29 us (9%)
  starting transfers between devices  18.4 us (6%)
  between operations  17.3 us (6%)
  other arithmetic  16.1 us (5%)
    pallas_call x1, Pallas kernels, flash_attend(): pl.pallas_call(kernel, grid_spec=pltpu.PrefetchScalarGridSpec(num_scalar_...  66 us
    all_to_all x1, waiting for transfers between devices, body(): lax.all_to_all(jnp.tile(cache_latents, (span_blocks, 1, 1)), ('tq', 'tr')...  44.9 us
    all_to_all x1, blocking collectives, body(): lax.all_to_all(partial_out[:, half_width:].reshape(group_count, tok_dev,...  30.8 us
    all_to_all x1, blocking collectives, body(): lax.all_to_all(jnp.broadcast_to(post_norm[:, half_width:], (group_count,...  30.7 us
    all_to_all x1, waiting for transfers between devices, body(): lax.all_to_all(jnp.broadcast_to(new_latents, (span_blocks,) + new_latents...  12.4 us
    dot_general x1, matrix products, body(): lax.dot_general(hidden, down_full, (((1,), (1,)), ((), ())), preferred_el...  10.9 us
    all_to_all x1, starting transfers between devices, body(): lax.all_to_all(jnp.broadcast_to(new_latents, (span_blocks,) + new_latents...  7.16 us
    dot_general x1, matrix products, body(): jnp.dot(rows_all, gate_full, preferred_element_type=jnp.float32)  6.37 us
  transfers between devices with their start and end apart: 6, of which 4 were waited for; matrix products, arithmetic and copies ran while one was open for 17% of the time, Pallas kernels for 22%

profile of v4, /device:TPU:8, one launch (start us, length us, event | category | flops | bytes accessed | tf_op | source)
XLA Modules:
  0.0 303.9 jit_solution(416581023207218941)
XLA Ops:
  7.2 2.1 pad_maximum_fusion.8
  9.3 1.2 dynamic_slice.9
  11.9 1.3 dynamic_slice.11
  15.2 1.3 dynamic_slice.10
  18.3 1.3 fusion.18
  19.7 2.2 fusion.34
  24.3 7.2 %all-to-all-start.2 = ((bf16[8,128,288]{1,2,0:T(8,128)(2,1)}), bf16[8,128,288]{1,2,0:T(8,128)(2,1)S(1)}, u32[]{:S(2)}, u32[]{:S(2)}) async-start(bf16[8,128,288]{1,2,0:T(8,128)(2,1)} %broadcast_in_dim.19), calls=%async_computation.2 | async-start | bytes 1179648 | tf_op jit(solution)/shard_map/all_to_all | solution.py:205
  32.1 12.4 %all-to-all-done.2 = bf16[8,128,288]{1,2,0:T(8,128)(2,1)S(1)} async-done(((bf16[8,128,288]{1,2,0:T(8,128)(2,1)}), bf16[8,128,288]{1,2,0:T(8,128)(2,1)S(1)}, u32[]{:S(2)}, u32[]{:S(2)}) %all-to-all-start.2) | async-done | bytes 589856 | tf_op jit(solution)/shard_map/all_to_all | solution.py:205
  44.5 2.8 tile.20
  47.3 5.5 %all-to-all-start.1 = ((bf16[32,128,288]{1,2,0:T(8,128)(2,1)}), bf16[32,128,288]{1,2,0:T(8,128)(2,1)}, u32[]{:S(2)}, u32[]{:S(2)}) async-start(bf16[32,128,288]{1,2,0:T(8,128)(2,1)} %bitcast.55), calls=%async_computation.1 | async-start | bytes 4718592 | tf_op jit(solution)/shard_map/all_to_all | solution.py:210
  52.7 3.1 %multiply_reduce_fusion = (f32[128]{0:T(128)S(1)}, f32[128,768]{1,0:T(8,128)S(1)}) fusion(bf16[2560,768]{1,0:T(8,128)(2,1)} %param.21, bf16[128,2560]{1,0:T(8,128)(2,1)} %param.19, f32[2560]{0:T(1024)S(1)} %convert_element_type.71, f32[128]{0:T(128)} %copy-done.14), kind=kOutput, calls=%fused_computation.39 | convolution fusion | flops 504823680 | bytes 4992000 | tf_op jit(solution)/shard_map/dot_general | solution.py:184
  55.9 1.4 convolution_convert_fusion
  57.3 1.4 copy.42
  58.7 1.3 copy.43
  62.7 44.9 %all-to-all-done.1 = bf16[32,128,288]{1,2,0:T(8,128)(2,1)} async-done(((bf16[32,128,288]{1,2,0:T(8,128)(2,1)}), bf16[32,128,288]{1,2,0:T(8,128)(2,1)}, u32[]{:S(2)}, u32[]{:S(2)}) %all-to-all-start.1) | async-done | bytes 2359328 | tf_op jit(solution)/shard_map/all_to_all | solution.py:210
  107.6 1.9 tile.8
  109.4 5.6 %all-to-all-start = ((bf16[32,32,288]{2,1,0:T(8,128)(2,1)}), bf16[32,32,288]{2,1,0:T(8,128)(2,1)}, u32[]{:S(2)}, u32[]{:S(2)}) async-start(bf16[32,32,288]{2,1,0:T(8,128)(2,1)} %bitcast.8), calls=%async_computation | async-start | bytes 1572864 | tf_op jit(solution)/shard_map/all_to_all | solution.py:215
  121.2 1.5 broadcast_in_dim_reshape.4.lim_row_ref
  122.7 2.2 copy.52
  124.9 1.9 pad_add_fusion.lims_ref
  126.8 1.7 pad_maximum_fusion.1.q_ref
  129.7 4.5 %copy.49 = bf16[32,128,288]{2,1,0:T(8,128)(2,1)} copy(bf16[32,128,288]{1,2,0:T(8,128)(2,1)} %all-to-all-done.1) | data formatting | bytes 4718592 | tf_op jit(solution)/shard_map/all_to_all | solution.py:210
  134.2 66.0 %shard_map.194 = bf16[2560,256]{1,0:T(8,128)(2,1)} custom-call(s32[2]{0:T(128)} %pad_add_fusion.lims_ref, s32[2560,1]{1,0:T(8,128)} %broadcast_in_dim_reshape.4.lim_row_ref, bf16[2560,288]{1,0:T(8,128)(2,1)} %pad_maximum_fusion.1.q_ref, bf16[1024,288]{1,0:T(8,128)(2,1)} %bitcast.9.kp_ref, bf16[4096,288]{1,0:T(8,128)(2,1)} %bitcast.54, bf16[1024,288]{1,0:T(8,128)(2,1)} %bitcast.57), custom_call_target="tpu_custom_call" | custom-call | tf_op jit(solution)/shard_map/pallas_call | solution.py:98
  200.2 2.3 reshape.188
  203.6 3.9 %fusion.12 = bf16[128,2560]{1,0:T(8,128)(2,1)S(1)} fusion(bf16[128,1280]{0,1:T(8,128)(2,1)S(1)} %bitcast.63, bf16[1280,2560]{1,0:T(8,128)(2,1)} %param.28, bf16[128,2560]{1,0:T(8,128)(2,1)S(1)} %copy-done.4), kind=kOutput, calls=%fused_computation.13 | convolution fusion | flops 839843840 | bytes 8192000 | tf_op jit(solution)/shard_map/dot_general | solution.py:235
  209.0 30.7 %all_to_all.25 = bf16[4,128,1280]{2,1,0:T(8,128)(2,1)S(1)} all-to-all(bf16[4,128,1280]{2,1,0:T(8,128)(2,1)S(1)} %broadcast_in_dim.20), channel_id=1, replica_groups=mesh['grp'=4,'tq'=8,'tr'=4] {'grp'}, dimensions={0} | all-to-all | bytes 2621440 | tf_op jit(solution)/shard_map/all_to_all | solution.py:248
  239.7 2.1 all-gather.5.cloned.1.call-done
  241.8 6.4 %fusion.4 = f32[512,800]{0,1:T(8,128)} fusion(bf16[3,2560,800]{2,1,0:T(8,128)(2,1)} %all-gather.3.cloned.1.call-done, bf16[512,1280]{1,0:T(8,128)(2,1)S(1)} %bitcast.61, bf16[512,1280]{1,0:T(8,128)(2,1)} %all-gather.5.cloned.1.call-done), kind=kOutput, calls=%fused_computation.6 | convolution fusion | flops 2102394880 | bytes 8847360 | tf_op jit(solution)/shard_map/dot_general | solution.py:261
  248.2 10.9 %fusion.9 = bf16[512,2560]{1,0:T(8,128)(2,1)} fusion(bf16[3,2560,800]{2,1,0:T(8,128)(2,1)} %all-gather.3.cloned.1.call-done, f32[512,800]{0,1:T(8,128)} %fusion.4, bf16[512,1280]{1,0:T(8,128)(2,1)S(1)} %bitcast.62, bf16[512,1280]{1,0:T(8,128)(2,1)S(1)} %copy-done.15), kind=kOutput, calls=%fused_computation.11 | convolution fusion | flops 4203315200 | bytes 16056320 | tf_op jit(solution)/shard_map/dot_general | solution.py:264
  259.1 3.0 fusion.45
  262.1 30.8 %all_to_all.26 = bf16[4,128,1280]{2,1,0:T(8,128)(2,1)S(1)} all-to-all(bf16[4,128,1280]{2,1,0:T(8,128)(2,1)S(1)} %bitcast.56), channel_id=1, replica_groups=mesh['grp'=4,'tq'=8,'tr'=4] {'grp'}, dimensions={0} | all-to-all | bytes 2621440 | tf_op jit(solution)/shard_map/all_to_all | solution.py:273
  295.1 2.3 fusion.24
  (84 shorter events, 19.7 us)
Async XLA Ops:
  7.2 48.7 %copy-start = (bf16[768,1920]{1,0:T(8,128)(2,1)S(1)}, bf16[768,1920]{1,0:T(8,128)(2,1)}, u32[]{:S(2)}) copy-start(bf16[768,1920]{1,0:T(8,128)(2,1)} %param.23) | copy-start | bytes 8847364
  7.2 200.4 %all-gather.3.cloned.1.call-start = ((), (), s32[]{:S(2)}) async-start(), calls=%async_computation.6 | async-start | bytes 14192640 | tf_op jit(solution)/shard_map/all_gather | solution.py:236
  19.6 4.6 %copy-start.14 = (f32[128]{0:T(128)}, f32[128]{0:T(128)S(1)}, u32[]{:S(2)}) copy-start(f32[128]{0:T(128)S(1)} %add_rsqrt_fusion.3) | copy-start | bytes 1540
  22.8 0.6 copy-start.8
  24.3 20.2 %all-to-all-start.2 = ((bf16[8,128,288]{1,2,0:T(8,128)(2,1)}), bf16[8,128,288]{1,2,0:T(8,128)(2,1)S(1)}, u32[]{:S(2)}, u32[]{:S(2)}) async-start(bf16[8,128,288]{1,2,0:T(8,128)(2,1)} %broadcast_in_dim.19), calls=%async_computation.2 | async-start | bytes 1179648 | tf_op jit(solution)/shard_map/all_to_all | solution.py:205
  47.3 60.3 %all-to-all-start.1 = ((bf16[32,128,288]{1,2,0:T(8,128)(2,1)}), bf16[32,128,288]{1,2,0:T(8,128)(2,1)}, u32[]{:S(2)}, u32[]{:S(2)}) async-start(bf16[32,128,288]{1,2,0:T(8,128)(2,1)} %bitcast.55), calls=%async_computation.1 | async-start | bytes 4718592 | tf_op jit(solution)/shard_map/all_to_all | solution.py:210
  57.3 2.8 copy-start.2
  57.3 3.4 %copy-start.9 = (bf16[8,32,288]{2,1,0:T(8,128)(2,1)S(1)}, bf16[8,32,288]{2,1,0:T(8,128)(2,1)}, u32[]{:S(2)}) copy-start(bf16[8,32,288]{2,1,0:T(8,128)(2,1)} %param.34) | copy-start | bytes 442372
  62.6 52.5 %copy-start.10 = (f32[128,16]{0,1:T(8,128)S(1)}, f32[128,16]{0,1:T(8,128)}, u32[]{:S(2)}) copy-start(f32[128,16]{0,1:T(8,128)} %get-tuple-element.14) | copy-start | bytes 24580
  62.7 52.5 %copy-start.11 = (f32[128,16]{0,1:T(8,128)S(1)}, f32[128,16]{0,1:T(8,128)}, u32[]{:S(2)}) copy-start(f32[128,16]{0,1:T(8,128)} %get-tuple-element.15) | copy-start | bytes 24580
  109.4 24.8 %all-to-all-start = ((bf16[32,32,288]{2,1,0:T(8,128)(2,1)}), bf16[32,32,288]{2,1,0:T(8,128)(2,1)}, u32[]{:S(2)}, u32[]{:S(2)}) async-start(bf16[32,32,288]{2,1,0:T(8,128)(2,1)} %bitcast.8), calls=%async_computation | async-start | bytes 1572864 | tf_op jit(solution)/shard_map/all_to_all | solution.py:215
  115.1 126.7 %all-gather.5.cloned.1.call-start = ((), (), s32[]{:S(2)}) async-start(), calls=%async_computation.7 | async-start | bytes 1638400 | tf_op jit(solution)/shard_map/all_gather | solution.py:247
  120.5 0.7 copy-start.13
  121.0 3.9 %copy-start.12 = (bf16[2560]{0:T(1024)(128)(2,1)S(1)}, bf16[2560]{0:T(1024)(128)(2,1)}, u32[]{:S(2)}) copy-start(bf16[2560]{0:T(1024)(128)(2,1)} %param.29) | copy-start | bytes 15364
  121.0 5.8 %copy-start.5 = (bf16[2560,16]{1,0:T(8,128)(2,1)S(1)}, bf16[2560,16]{1,0:T(8,128)(2,1)}, u32[]{:S(2)}) copy-start(bf16[2560,16]{1,0:T(8,128)(2,1)} %copy.47) | copy-start | bytes 245764
  121.0 5.8 %copy-start.6 = (bf16[2560,16]{1,0:T(8,128)(2,1)S(1)}, bf16[2560,16]{1,0:T(8,128)(2,1)}, u32[]{:S(2)}) copy-start(bf16[2560,16]{1,0:T(8,128)(2,1)} %copy.48) | copy-start | bytes 245764
  200.2 2.3 copy-start.7
  202.5 1.1 copy-start.4
  207.5 1.3 copy-start.3
  208.8 85.3 %reduce-scatter.2.cloned.1.call-start = ((), (), s32[]{:S(2)}) async-start(), calls=%async_computation.8 | async-start | bytes 1638400 | tf_op jit(solution)/shard_map/reduce_scatter | solution.py:270
  241.8 6.4 %copy-start.15 = (bf16[512,1280]{1,0:T(8,128)(2,1)S(1)}, bf16[512,1280]{1,0:T(8,128)(2,1)}, u32[]{:S(2)}) copy-start(bf16[512,1280]{1,0:T(8,128)(2,1)} %all-gather.5.cloned.1.call-done) | copy-start | bytes 3932164
  292.9 4.5 %copy-start.1 = (bf16[768,1920]{1,0:T(8,128)(2,1)S(1)}, bf16[768,1920]{1,0:T(8,128)(2,1)}, u32[]{:S(2)}) copy-start(bf16[768,1920]{1,0:T(8,128)(2,1)} %param.23) | copy-start | bytes 8847364
Sparse Core Ops, SparseCore 0:
  10.4 96.5 all-gather.2
  208.9 32.8 all-gather.4
  262.2 31.9 reduce-scatter.1

commit v5 on v4

--- a/solution.py
+++ b/solution.py
@@ -47,15 +47,33 @@
 ROW_BLOCK = 640
 
 
-def flash_kernel(lims_ref, lim_row_ref, q_ref, kp_ref, kc_ref, ks_ref, o_ref, m_sc, l_sc, acc_sc, *, cache_blocks, score_scale, value_width):
+def flash_kernel(lims_ref, lim_row_ref, q_ref, *refs, plan, first, final, score_scale, value_width):
+    key_refs = refs[: len(plan)]
+    rest = refs[len(plan) :]
+    if not first:
+        m_in, l_in, acc_in = rest[:3]
+        rest = rest[3:]
+    if final:
+        o_ref = rest[0]
+        rest = rest[1:]
+    else:
+        m_out, l_out, acc_out = rest[:3]
+        rest = rest[3:]
+    m_sc, l_sc, acc_sc = rest
     j = pl.program_id(1)
-    last = cache_blocks + 1
+    total = sum(count for _, count in plan)
+    rows = q_ref.shape[0]
 
     @pl.when(j == 0)
     def _init():
-        m_sc[...] = jnp.full(m_sc.shape, -1e30, jnp.float32)
-        l_sc[...] = jnp.zeros(l_sc.shape, jnp.float32)
-        acc_sc[...] = jnp.zeros(acc_sc.shape, jnp.float32)
+        if first:
+            m_sc[...] = jnp.full(m_sc.shape, -1e30, jnp.float32)
+            l_sc[...] = jnp.zeros(l_sc.shape, jnp.float32)
+            acc_sc[...] = jnp.zeros(acc_sc.shape, jnp.float32)
+        else:
+            m_sc[...] = m_in[...]
+            l_sc[...] = l_in[...]
+            acc_sc[...] = acc_in[...]
 
     def step(k_ref, base, limit):
         keys = k_ref[...]
@@ -70,54 +88,77 @@
         acc_sc[...] = acc_sc[...] * factor + jnp.dot(weights.astype(jnp.bfloat16), keys[:, :value_width], preferred_element_type=jnp.float32)
         m_sc[...] = m_new
 
-    rows = q_ref.shape[0]
-
-    @pl.when(j == 0)
-    def _prompt():
-        step(kp_ref, 0, jnp.full((rows, 1), lims_ref[0], jnp.int32))
-
-    @pl.when(jnp.logical_and(j >= 1, j < last))
-    def _cache():
-        step(kc_ref, (j - 1) * KEY_BLOCK, jnp.full((rows, 1), lims_ref[1], jnp.int32))
-
-    @pl.when(j == last)
-    def _span():
-        step(ks_ref, 0, lim_row_ref[...])
-        o_ref[...] = (acc_sc[...] / l_sc[...]).astype(o_ref.dtype)
-
-
-def flash_attend(lims, lim_rows, queries, prompt_rows, cache_rows, span_rows, score_scale, value_width, interpret=False):
+    begin = 0
+    for (kind, count), k_ref in zip(plan, key_refs):
+        def run(k_ref=k_ref, kind=kind, begin=begin):
+            if kind == "span":
+                limit = lim_row_ref[...]
+            else:
+                limit = jnp.full((rows, 1), lims_ref[0 if kind == "prompt" else 1], jnp.int32)
+            step(k_ref, (j - begin) * KEY_BLOCK, limit)
+        pl.when(jnp.logical_and(j >= begin, j < begin + count))(run)
+        begin += count
+
+    @pl.when(j == total - 1)
+    def _finish():
+        if final:
+            o_ref[...] = (acc_sc[...] / l_sc[...]).astype(o_ref.dtype)
+        else:
+            m_out[...] = m_sc[...]
+            l_out[...] = l_sc[...]
+            acc_out[...] = acc_sc[...]
+
+
+def flash_part(lims, lim_rows, queries, segments, state, final, score_scale, value_width, interpret=False):
     row_count, width = queries.shape
-    cache_blocks = cache_rows.shape[0] // KEY_BLOCK
-    assert prompt_rows.shape[0] == KEY_BLOCK and span_rows.shape[0] == KEY_BLOCK
-    assert cache_blocks * KEY_BLOCK == cache_rows.shape[0] and row_count % ROW_BLOCK == 0
-    grid = (row_count // ROW_BLOCK, cache_blocks + 2)
-    key_spec = pl.BlockSpec((KEY_BLOCK, width), lambda i, j, lims: (0, 0))
-    cache_spec = pl.BlockSpec((KEY_BLOCK, width), lambda i, j, lims: (jnp.minimum(jnp.maximum(j - 1, 0), cache_blocks - 1), 0))
-    kernel = functools.partial(flash_kernel, cache_blocks=cache_blocks, score_scale=score_scale, value_width=value_width)
+    plan = tuple((kind, rows.shape[0] // KEY_BLOCK) for kind, rows in segments)
+    total = sum(count for _, count in plan)
+    grid = (row_count // ROW_BLOCK, total)
+    key_specs = []
+    begin = 0
+    for _, count in plan:
+        key_specs.append(pl.BlockSpec((KEY_BLOCK, width), lambda i, j, lims, b=begin, c=count: (jnp.minimum(jnp.maximum(j - b, 0), c - 1), 0)))
+        begin += count
+    row_spec = lambda cols: pl.BlockSpec((ROW_BLOCK, cols), lambda i, j, lims: (i, 0))
+    in_specs = [row_spec(1), row_spec(width)] + key_specs
+    operands = [lims, lim_rows, queries] + [rows for _, rows in segments]
+    if state is not None:
+        in_specs += [row_spec(1), row_spec(1), row_spec(value_width)]
+        operands += list(state)
+    if final:
+        out_specs = row_spec(value_width)
+        out_shape = jax.ShapeDtypeStruct((row_count, value_width), jnp.bfloat16)
+    else:
+        out_specs = [row_spec(1), row_spec(1), row_spec(value_width)]
+        out_shape = [
+            jax.ShapeDtypeStruct((row_count, 1), jnp.float32),
+            jax.ShapeDtypeStruct((row_count, 1), jnp.float32),
+            jax.ShapeDtypeStruct((row_count, value_width), jnp.float32),
+        ]
+    key_count = total * KEY_BLOCK
+    kernel = functools.partial(flash_kernel, plan=plan, first=state is None, final=final, score_scale=score_scale, value_width=value_width)
     return pl.pallas_call(
         kernel,
         grid_spec=pltpu.PrefetchScalarGridSpec(
             num_scalar_prefetch=1,
             grid=grid,
-            in_specs=[
-                pl.BlockSpec((ROW_BLOCK, 1), lambda i, j, lims: (i, 0)),
-                pl.BlockSpec((ROW_BLOCK, width), lambda i, j, lims: (i, 0)),
-                key_spec,
-                cache_spec,
-                key_spec,
-            ],
-            out_specs=pl.BlockSpec((ROW_BLOCK, value_width), lambda i, j, lims: (i, 0)),
+            in_specs=in_specs,
+            out_specs=out_specs,
             scratch_shapes=[
                 pltpu.VMEM((ROW_BLOCK, 1), jnp.float32),
                 pltpu.VMEM((ROW_BLOCK, 1), jnp.float32),
                 pltpu.VMEM((ROW_BLOCK, value_width), jnp.float32),
             ],
         ),
-        out_shape=jax.ShapeDtypeStruct((row_count, value_width), jnp.bfloat16),
+        out_shape=out_shape,
         compiler_params=pltpu.CompilerParams(dimension_semantics=("arbitrary", "arbitrary")),
         interpret=interpret,
-    )(lims, lim_rows, queries, prompt_rows, cache_rows, span_rows)
+        cost_estimate=pl.CostEstimate(
+            flops=2 * row_count * key_count * (width + value_width),
+            transcendentals=row_count * key_count,
+            bytes_accessed=2 * (row_count * (width + value_width) + key_count * width),
+        ),
+    )(*operands)
 
 
 def attend_segment(
@@ -207,20 +248,33 @@
     ).reshape(-1, latent_width)
     span_lower = jnp.zeros((tok_dev,), jnp.int32)
     span_limit = within + 1
-    cache_rows = lax.all_to_all(
-        jnp.tile(cache_latents, (span_blocks, 1, 1)), ("tq", "tr"), 0, 0, tiled=True
-    ).reshape(-1, latent_width)
     group_prompts = prompt_of[group_index * group_requests + jnp.arange(group_requests)]
     prompt_send = jnp.take(prompt_latents, group_prompts, axis=0)
     prompt_rows = lax.all_to_all(
         jnp.tile(prompt_send, (span_blocks, 1, 1)), ("tq", "tr"), 0, 0, tiled=True
     ).reshape(-1, latent_width)
+    cache_send, _ = lax.optimization_barrier(
+        (jnp.tile(cache_latents, (span_blocks, 1, 1)), prompt_rows)
+    )
+    cache_rows = lax.all_to_all(cache_send, ("tq", "tr"), 0, 0, tiled=True).reshape(
+        -1, latent_width
+    )
     query_rows = queries.reshape(tok_dev * HEADS, latent_width)
     score_scale = 1.0 / (NOPE + ROPE) ** 0.5
     lims = jnp.stack([prompt_live, cache_live]).astype(jnp.int32)
     lim_rows = jnp.repeat(span_limit, HEADS)[:, None]
-    latent_out = flash_attend(
-        lims, lim_rows, query_rows, prompt_rows, cache_rows, span_rows, score_scale, KVR
+    early_state = flash_part(
+        lims,
+        lim_rows,
+        query_rows,
+        (("span", span_rows), ("prompt", prompt_rows)),
+        None,
+        False,
+        score_scale,
+        KVR,
+    )
+    latent_out = flash_part(
+        lims, lim_rows, query_rows, (("cache", cache_rows),), early_state, True, score_scale, KVR
     ).reshape(tok_dev, HEADS, KVR)
     heads_out = (
         jnp.einsum(

time: 306 us -> 262 us (0.86)
  waiting for transfers between devices: 59.7 us -> 20.7 us
  local copies, waits for them, and re-layouts: 35.9 us -> 30.1 us
    all_to_all x1, waiting for transfers between devices: 44.9 us -> 3.28 us  [body(): lax.all_to_all(cache_send, ('tq', 'tr'), 0, 0, tiled=True)]
    all_to_all x1, waiting for transfers between devices: 0.01 us -> 8.07 us  [body(): lax.all_to_all(jnp.tile(prompt_send, (span_blocks, 1, 1)), ('tq', 'tr'),...]
    all_to_all x1, starting transfers between devices: 7.16 us -> 3.54 us  [body(): lax.all_to_all(jnp.broadcast_to(new_latents, (span_blocks,) + new_latents...]
    all_to_all x1, waiting for transfers between devices: 12.4 us -> 9.32 us  [body(): lax.all_to_all(jnp.broadcast_to(new_latents, (span_blocks,) + new_latents...]
    pallas_call x1 -> x2, Pallas kernels: 66 us -> 68.4 us  [flash_part(): pl.pallas_call(kernel, grid_spec=pltpu.PrefetchScalarGridSpec(num_scalar_...]
  transfers between devices with their start and end apart: 6 -> 6, of which waited for: 4 -> 3; matrix products, arithmetic and copies ran while one was open for 17% -> 18% of each run, Pallas kernels for 22% -> 26%
where the time goes in v5:
time: 262 us; the launch traced here: 261 us
  Pallas kernels  68.4 us (26%)
  blocking collectives  62.8 us (24%)
  matrix products  30.7 us (12%)
  local copies, waits for them, and re-layouts  30.1 us (11%)
  waiting for transfers between devices  20.7 us (8%)
  between operations  17.4 us (7%)
  starting transfers between devices  16.9 us (6%)
  other arithmetic  13.8 us (5%)
    pallas_call x2, Pallas kernels, flash_part(): pl.pallas_call(kernel, grid_spec=pltpu.PrefetchScalarGridSpec(num_scalar_...  68.4 us
    all_to_all x1, blocking collectives, body(): lax.all_to_all(jnp.broadcast_to(post_norm[:, half_width:], (group_count,...  31.8 us
    all_to_all x1, blocking collectives, body(): lax.all_to_all(partial_out[:, half_width:].reshape(group_count, tok_dev,...  31 us
    dot_general x1, matrix products, body(): lax.dot_general(hidden, down_full, (((1,), (1,)), ((), ())), preferred_el...  10.9 us
    all_to_all x1, waiting for transfers between devices, body(): lax.all_to_all(jnp.broadcast_to(new_latents, (span_blocks,) + new_latents...  9.32 us
    all_to_all x1, starting transfers between devices, body(): lax.all_to_all(jnp.tile(prompt_send, (span_blocks, 1, 1)), ('tq', 'tr'),...  8.6 us
    all_to_all x1, waiting for transfers between devices, body(): lax.all_to_all(jnp.tile(prompt_send, (span_blocks, 1, 1)), ('tq', 'tr'),...  8.07 us
    dot_general x1, matrix products, body(): jnp.dot(rows_all, gate_full, preferred_element_type=jnp.float32)  6.36 us
  transfers between devices with their start and end apart: 6, of which 3 were waited for; matrix products, arithmetic and copies ran while one was open for 18% of the time, Pallas kernels for 26%

profile of v5, /device:TPU:8, one launch (start us, length us, event | category | flops | bytes accessed | tf_op | source)
XLA Modules:
  0.0 260.9 jit_solution(1192976550556750887)
XLA Ops:
  7.2 2.0 pad_maximum_fusion.8
  11.7 8.6 %all-to-all-start = ((bf16[32,32,288]{2,1,0:T(8,128)(2,1)}), bf16[32,32,288]{2,1,0:T(8,128)(2,1)}, u32[]{:S(2)}, u32[]{:S(2)}) async-start(bf16[32,32,288]{2,1,0:T(8,128)(2,1)} %bitcast.56), calls=%async_computation | async-start | bytes 1572864 | tf_op jit(solution)/shard_map/all_to_all | solution.py:253
  25.8 1.3 fusion.18
  27.1 2.2 fusion.34
  30.3 8.1 %all-to-all-done = bf16[32,32,288]{2,1,0:T(8,128)(2,1)} async-done(((bf16[32,32,288]{2,1,0:T(8,128)(2,1)}), bf16[32,32,288]{2,1,0:T(8,128)(2,1)}, u32[]{:S(2)}, u32[]{:S(2)}) %all-to-all-start) | async-done | bytes 589856 | tf_op jit(solution)/shard_map/all_to_all | solution.py:253
  39.2 3.5 %all-to-all-start.2 = ((bf16[8,128,288]{1,2,0:T(8,128)(2,1)}), bf16[8,128,288]{1,2,0:T(8,128)(2,1)S(1)}, u32[]{:S(2)}, u32[]{:S(2)}) async-start(bf16[8,128,288]{1,2,0:T(8,128)(2,1)} %broadcast_in_dim.19), calls=%async_computation.2 | async-start | bytes 1179648 | tf_op jit(solution)/shard_map/all_to_all | solution.py:246
  43.4 3.8 %multiply_reduce_fusion = (f32[128]{0:T(128)S(1)}, f32[128,768]{1,0:T(8,128)}) fusion(bf16[2560,768]{1,0:T(8,128)(2,1)} %param.21, bf16[128,2560]{1,0:T(8,128)(2,1)} %param.19, f32[2560]{0:T(1024)S(1)} %convert_element_type.71, f32[128]{0:T(128)} %copy-done.18), kind=kOutput, calls=%fused_computation.39 | convolution fusion | flops 504823680 | bytes 4992000 | tf_op jit(solution)/shard_map/dot_general | solution.py:225
  47.2 1.8 tile.8
  49.0 9.3 %all-to-all-done.2 = bf16[8,128,288]{1,2,0:T(8,128)(2,1)S(1)} async-done(((bf16[8,128,288]{1,2,0:T(8,128)(2,1)}), bf16[8,128,288]{1,2,0:T(8,128)(2,1)S(1)}, u32[]{:S(2)}, u32[]{:S(2)}) %all-to-all-start.2) | async-done | bytes 589856 | tf_op jit(solution)/shard_map/all_to_all | solution.py:246
  58.3 4.6 %all-to-all-start.1 = ((bf16[32,128,288]{1,2,0:T(8,128)(2,1)}), bf16[32,128,288]{1,2,0:T(8,128)(2,1)}, u32[]{:S(2)}, u32[]{:S(2)}) async-start(bf16[32,128,288]{1,2,0:T(8,128)(2,1)} %bitcast.54), calls=%async_computation.1 | async-start | bytes 4718592 | tf_op jit(solution)/shard_map/all_to_all | solution.py:259
  63.0 2.4 convolution_convert_fusion
  65.5 1.3 copy.43
  68.1 1.1 copy.48
  70.3 1.1 copy.49
  73.7 1.6 broadcast_in_dim_reshape.4.lim_row_ref
  75.2 2.2 copy.54
  77.4 1.7 pad_add_fusion.lims_ref
  79.2 1.7 pad_maximum_fusion.1.q_ref
  80.8 1.2 copy.51
  82.0 24.0 %shard_map.194 = (f32[2560,1]{1,0:T(8,128)}, f32[2560,1]{1,0:T(8,128)}, f32[2560,256]{1,0:T(8,128)}) custom-call(s32[2]{0:T(128)} %pad_add_fusion.lims_ref, s32[2560,1]{1,0:T(8,128)} %broadcast_in_dim_reshape.4.lim_row_ref, bf16[2560,288]{1,0:T(8,128)(2,1)} %pad_maximum_fusion.1.q_ref, bf16[1024,288]{1,0:T(8,128)(2,1)} %bitcast.64, ...), custom_call_target="tpu_custom_call" | custom-call | flops 5704253440 | bytes 3964928 | tf_op jit(solution)/shard_map/pallas_call | solution.py:140
  106.0 3.3 %all-to-all-done.1 = bf16[32,128,288]{1,2,0:T(8,128)(2,1)} async-done(((bf16[32,128,288]{1,2,0:T(8,128)(2,1)}), bf16[32,128,288]{1,2,0:T(8,128)(2,1)}, u32[]{:S(2)}, u32[]{:S(2)}) %all-to-all-start.1) | async-done | bytes 2359328 | tf_op jit(solution)/shard_map/all_to_all | solution.py:259
  109.3 4.5 %copy.50 = bf16[32,128,288]{2,1,0:T(8,128)(2,1)} copy(bf16[32,128,288]{1,2,0:T(8,128)(2,1)} %all-to-all-done.1) | data formatting | bytes 4718592 | tf_op jit(solution)/shard_map/all_to_all | solution.py:259
  113.8 44.4 %shard_map.195 = bf16[2560,256]{1,0:T(8,128)(2,1)} custom-call(s32[2]{0:T(128)} %pad_add_fusion.lims_ref, s32[2560,1]{1,0:T(8,128)} %broadcast_in_dim_reshape.4.lim_row_ref, bf16[2560,288]{1,0:T(8,128)(2,1)} %pad_maximum_fusion.1.q_ref, bf16[4096,288]{1,0:T(8,128)(2,1)} %bitcast.57, f32[2560,1]{1,0:T(8,128)} %get-tuple-element.9.refs_1_, ...), custom_call_target="tpu_custom_call" | custom-call | flops 11408506880 | bytes 5144576 | tf_op jit(solution)/shard_map/pallas_call | solution.py:140
  158.2 2.3 reshape.188
  161.6 3.9 %fusion.12 = bf16[128,2560]{1,0:T(8,128)(2,1)S(1)} fusion(bf16[128,1280]{0,1:T(8,128)(2,1)S(1)} %bitcast.63, bf16[1280,2560]{1,0:T(8,128)(2,1)} %param.28, bf16[128,2560]{1,0:T(8,128)(2,1)S(1)} %copy-done.4), kind=kOutput, calls=%fused_computation.13 | convolution fusion | flops 839843840 | bytes 8192000 | tf_op jit(solution)/shard_map/dot_general | solution.py:289
  166.9 31.8 %all_to_all.25 = bf16[4,128,1280]{2,1,0:T(8,128)(2,1)S(1)} all-to-all(bf16[4,128,1280]{2,1,0:T(8,128)(2,1)S(1)} %broadcast_in_dim.20), channel_id=1, replica_groups=mesh['grp'=4,'tq'=8,'tr'=4] {'grp'}, dimensions={0} | all-to-all | bytes 2621440 | tf_op jit(solution)/shard_map/all_to_all | solution.py:302
  198.7 6.4 %fusion.4 = f32[512,800]{0,1:T(8,128)} fusion(bf16[3,2560,800]{2,1,0:T(8,128)(2,1)} %all-gather.3.cloned.1.call-done, bf16[512,1280]{1,0:T(8,128)(2,1)S(1)} %bitcast.61, bf16[512,1280]{1,0:T(8,128)(2,1)} %all-gather.5.cloned.1.call-done), kind=kOutput, calls=%fused_computation.6 | convolution fusion | flops 2102394880 | bytes 8847360 | tf_op jit(solution)/shard_map/dot_general | solution.py:315
  205.1 10.9 %fusion.9 = bf16[512,2560]{1,0:T(8,128)(2,1)} fusion(bf16[3,2560,800]{2,1,0:T(8,128)(2,1)} %all-gather.3.cloned.1.call-done, f32[512,800]{0,1:T(8,128)} %fusion.4, bf16[512,1280]{1,0:T(8,128)(2,1)S(1)} %bitcast.62, bf16[512,1280]{1,0:T(8,128)(2,1)S(1)} %copy-done.19), kind=kOutput, calls=%fused_computation.11 | convolution fusion | flops 4203315200 | bytes 16056320 | tf_op jit(solution)/shard_map/dot_general | solution.py:318
  216.0 2.9 %fusion.45 = (bf16[512,1280]{1,0:T(8,128)(2,1)}, bf16[512,1280]{1,0:T(8,128)(2,1)S(1)}) fusion(bf16[512,2560]{1,0:T(8,128)(2,1)} %fusion.9), kind=kLoop, calls=%fused_computation.76 | loop fusion | bytes 5242880 | tf_op jit(solution)/shard_map/slice | solution.py:325
  218.9 31.0 %all_to_all.26 = bf16[4,128,1280]{2,1,0:T(8,128)(2,1)S(1)} all-to-all(bf16[4,128,1280]{2,1,0:T(8,128)(2,1)S(1)} %bitcast.55), channel_id=1, replica_groups=mesh['grp'=4,'tq'=8,'tr'=4] {'grp'}, dimensions={0} | all-to-all | bytes 2621440 | tf_op jit(solution)/shard_map/all_to_all | solution.py:327
  251.0 1.1 convert_element_type.87
  252.1 2.3 fusion.24
  (99 shorter events, 15.3 us)
Async XLA Ops:
  7.2 55.8 %copy-start = (bf16[768,1920]{1,0:T(8,128)(2,1)S(1)}, bf16[768,1920]{1,0:T(8,128)(2,1)}, u32[]{:S(2)}) copy-start(bf16[768,1920]{1,0:T(8,128)(2,1)} %param.23) | copy-start | bytes 8847364
  7.2 2.2 copy-start.2
  7.2 2.9 %copy-start.11 = (bf16[8,32,288]{2,1,0:T(8,128)(2,1)S(1)}, bf16[8,32,288]{2,1,0:T(8,128)(2,1)}, u32[]{:S(2)}) copy-start(bf16[8,32,288]{2,1,0:T(8,128)(2,1)} %param.34) | copy-start | bytes 442372
  7.2 158.3 %all-gather.3.cloned.1.call-start = ((), (), s32[]{:S(2)}) async-start(), calls=%async_computation.6 | async-start | bytes 14192640 | tf_op jit(solution)/shard_map/all_gather | solution.py:290
  9.3 12.9 %copy-start.20 = (s32[16]{0:T(128)S(1)}, s32[16]{0:T(128)}, u32[]{:S(2)}) copy-start(s32[16]{0:T(128)} %param.35) | copy-start | bytes 196
  9.4 13.4 %copy-start.14 = (bf16[2560]{0:T(1024)(128)(2,1)S(1)}, bf16[2560]{0:T(1024)(128)(2,1)}, u32[]{:S(2)}) copy-start(bf16[2560]{0:T(1024)(128)(2,1)} %param.20) | copy-start | bytes 15364
  9.4 14.1 %copy-start.21 = (s32[8]{0:T(128)S(1)}, s32[8]{0:T(128)}, u32[]{:S(2)}) copy-start(s32[8]{0:T(128)} %param.36) | copy-start | bytes 100
  11.7 26.6 %all-to-all-start = ((bf16[32,32,288]{2,1,0:T(8,128)(2,1)}), bf16[32,32,288]{2,1,0:T(8,128)(2,1)}, u32[]{:S(2)}, u32[]{:S(2)}) async-start(bf16[32,32,288]{2,1,0:T(8,128)(2,1)} %bitcast.56), calls=%async_computation | async-start | bytes 1572864 | tf_op jit(solution)/shard_map/all_to_all | solution.py:253
  22.8 6.6 %copy-start.22 = (bf16[256]{0:T(256)(128)(2,1)S(1)}, bf16[256]{0:T(256)(128)(2,1)}, u32[]{:S(2)}) copy-start(bf16[256]{0:T(256)(128)(2,1)} %param.25) | copy-start | bytes 1540
  27.1 2.3 copy-start.18
  29.3 13.5 %copy-start.17 = (bf16[768]{0:T(1024)(128)(2,1)S(1)}, bf16[768]{0:T(1024)(128)(2,1)}, u32[]{:S(2)}) copy-start(bf16[768]{0:T(1024)(128)(2,1)} %param.22) | copy-start | bytes 4612
  30.3 9.0 %copy-start.9 = (bf16[128,288]{0,1:T(8,128)(2,1)}, bf16[128,288]{0,1:T(8,128)(2,1)S(1)}, u32[]{:S(2)}) copy-start(bf16[128,288]{0,1:T(8,128)(2,1)S(1)} %pad_maximum_fusion.9) | copy-start | bytes 221188
  39.2 19.1 %all-to-all-start.2 = ((bf16[8,128,288]{1,2,0:T(8,128)(2,1)}), bf16[8,128,288]{1,2,0:T(8,128)(2,1)S(1)}, u32[]{:S(2)}, u32[]{:S(2)}) async-start(bf16[8,128,288]{1,2,0:T(8,128)(2,1)} %broadcast_in_dim.19), calls=%async_computation.2 | async-start | bytes 1179648 | tf_op jit(solution)/shard_map/all_to_all | solution.py:246
  43.4 3.8 %copy-start.10 = (bf16[4,128,288]{1,2,0:T(8,128)(2,1)S(1)}, bf16[4,128,288]{1,2,0:T(8,128)(2,1)}, u32[]{:S(2)}) copy-start(bf16[4,128,288]{1,2,0:T(8,128)(2,1)} %param.33) | copy-start | bytes 884740
  58.3 51.0 %all-to-all-start.1 = ((bf16[32,128,288]{1,2,0:T(8,128)(2,1)}), bf16[32,128,288]{1,2,0:T(8,128)(2,1)}, u32[]{:S(2)}, u32[]{:S(2)}) async-start(bf16[32,128,288]{1,2,0:T(8,128)(2,1)} %bitcast.54), calls=%async_computation.1 | async-start | bytes 4718592 | tf_op jit(solution)/shard_map/all_to_all | solution.py:259
  62.9 135.8 %all-gather.5.cloned.1.call-start = ((), (), s32[]{:S(2)}) async-start(), calls=%async_computation.7 | async-start | bytes 1638400 | tf_op jit(solution)/shard_map/all_gather | solution.py:301
  63.0 3.8 %copy-start.12 = (f32[128,16]{0,1:T(8,128)S(1)}, f32[128,16]{0,1:T(8,128)}, u32[]{:S(2)}) copy-start(f32[128,16]{0,1:T(8,128)} %get-tuple-element.22) | copy-start | bytes 24580
  63.0 3.8 %copy-start.13 = (f32[128,16]{0,1:T(8,128)S(1)}, f32[128,16]{0,1:T(8,128)}, u32[]{:S(2)}) copy-start(f32[128,16]{0,1:T(8,128)} %get-tuple-element.23) | copy-start | bytes 24580
  67.2 4.2 %copy-start.7 = (bf16[256,1280]{1,0:T(8,128)(2,1)S(1)}, bf16[256,1280]{1,0:T(8,128)(2,1)}, u32[]{:S(2)}) copy-start(bf16[256,1280]{1,0:T(8,128)(2,1)} %param.26) | copy-start | bytes 1966084
  73.0 0.6 copy-start.16
  73.5 3.9 %copy-start.15 = (bf16[2560]{0:T(1024)(128)(2,1)S(1)}, bf16[2560]{0:T(1024)(128)(2,1)}, u32[]{:S(2)}) copy-start(bf16[2560]{0:T(1024)(128)(2,1)} %param.29) | copy-start | bytes 15364
  73.5 5.6 %copy-start.5 = (bf16[2560,16]{1,0:T(8,128)(2,1)S(1)}, bf16[2560,16]{1,0:T(8,128)(2,1)}, u32[]{:S(2)}) copy-start(bf16[2560,16]{1,0:T(8,128)(2,1)} %copy.48) | copy-start | bytes 245764
  73.5 5.6 %copy-start.6 = (bf16[2560,16]{1,0:T(8,128)(2,1)S(1)}, bf16[2560,16]{1,0:T(8,128)(2,1)}, u32[]{:S(2)}) copy-start(bf16[2560,16]{1,0:T(8,128)(2,1)} %copy.49) | copy-start | bytes 245764
  158.2 2.3 copy-start.8
  160.5 1.1 copy-start.4
  165.5 1.3 copy-start.3
  166.8 84.2 %reduce-scatter.2.cloned.1.call-start = ((), (), s32[]{:S(2)}) async-start(), calls=%async_computation.8 | async-start | bytes 1638400 | tf_op jit(solution)/shard_map/reduce_scatter | solution.py:324
  198.7 6.4 %copy-start.19 = (bf16[512,1280]{1,0:T(8,128)(2,1)S(1)}, bf16[512,1280]{1,0:T(8,128)(2,1)}, u32[]{:S(2)}) copy-start(bf16[512,1280]{1,0:T(8,128)(2,1)} %all-gather.5.cloned.1.call-done) | copy-start | bytes 3932164
  250.0 4.4 %copy-start.1 = (bf16[768,1920]{1,0:T(8,128)(2,1)S(1)}, bf16[768,1920]{1,0:T(8,128)(2,1)}, u32[]{:S(2)}) copy-start(bf16[768,1920]{1,0:T(8,128)(2,1)} %param.23) | copy-start | bytes 8847364
Sparse Core Ops, SparseCore 0:
  10.4 98.1 all-gather.2
  166.9 31.4 all-gather.4
  219.1 31.2 reduce-scatter.1

commit v6 on v5

--- a/solution.py
+++ b/solution.py
@@ -75,14 +75,18 @@
             l_sc[...] = l_in[...]
             acc_sc[...] = acc_in[...]
 
-    def step(k_ref, base, limit):
+    def step(k_ref, base, limit, masked=True):
         keys = k_ref[...]
         scores = lax.dot_general(q_ref[...], keys, (((1,), (1,)), ((), ())), preferred_element_type=jnp.float32) * score_scale
-        place = lax.broadcasted_iota(jnp.int32, scores.shape, 1) + base
-        live = place < limit
         m_old = m_sc[...]
-        m_new = jnp.maximum(m_old, jnp.max(jnp.where(live, scores, -1e30), axis=1, keepdims=True))
-        weights = jnp.where(live, jnp.exp(scores - m_new), 0.0)
+        if masked:
+            place = lax.broadcasted_iota(jnp.int32, scores.shape, 1) + base
+            live = place < limit
+            m_new = jnp.maximum(m_old, jnp.max(jnp.where(live, scores, -1e30), axis=1, keepdims=True))
+            weights = jnp.where(live, jnp.exp(scores - m_new), 0.0)
+        else:
+            m_new = jnp.maximum(m_old, jnp.max(scores, axis=1, keepdims=True))
+            weights = jnp.exp(scores - m_new)
         factor = jnp.exp(m_old - m_new)
         l_sc[...] = l_sc[...] * factor + jnp.sum(weights, axis=1, keepdims=True)
         acc_sc[...] = acc_sc[...] * factor + jnp.dot(weights.astype(jnp.bfloat16), keys[:, :value_width], preferred_element_type=jnp.float32)
@@ -90,13 +94,20 @@
 
     begin = 0
     for (kind, count), k_ref in zip(plan, key_refs):
-        def run(k_ref=k_ref, kind=kind, begin=begin):
-            if kind == "span":
-                limit = lim_row_ref[...]
-            else:
-                limit = jnp.full((rows, 1), lims_ref[0 if kind == "prompt" else 1], jnp.int32)
-            step(k_ref, (j - begin) * KEY_BLOCK, limit)
-        pl.when(jnp.logical_and(j >= begin, j < begin + count))(run)
+        inside = jnp.logical_and(j >= begin, j < begin + count)
+        base = (j - begin) * KEY_BLOCK
+        if kind == "span":
+            pl.when(inside)(functools.partial(step, k_ref, base, lim_row_ref[...]))
+        else:
+            live_rows = lims_ref[0 if kind == "prompt" else 1]
+            whole = base + KEY_BLOCK <= live_rows
+            part = jnp.logical_and(jnp.logical_not(whole), base < live_rows)
+            pl.when(jnp.logical_and(inside, whole))(
+                functools.partial(step, k_ref, base, live_rows, False)
+            )
+            pl.when(jnp.logical_and(inside, part))(
+                functools.partial(step, k_ref, base, jnp.full((rows, 1), live_rows, jnp.int32))
+            )
         begin += count
 
     @pl.when(j == total - 1)

time: 262 us -> 261 us (level)
  no operation moved by 1% of the time
where the time goes in v6:
time: 261 us
  Pallas kernels  68.6 us (26%)
  blocking collectives  62.5 us (24%)
  matrix products  30.7 us (12%)
  local copies, waits for them, and re-layouts  30.1 us (12%)
  waiting for transfers between devices  20.6 us (8%)
  between operations  17.4 us (7%)
  starting transfers between devices  16.9 us (6%)
  other arithmetic  13.8 us (5%)
    pallas_call x2, Pallas kernels, flash_part(): pl.pallas_call(kernel, grid_spec=pltpu.PrefetchScalarGridSpec(num_scalar_...  68.6 us
    all_to_all x1, blocking collectives, body(): lax.all_to_all(jnp.broadcast_to(post_norm[:, half_width:], (group_count,...  31.5 us
    all_to_all x1, blocking collectives, body(): lax.all_to_all(partial_out[:, half_width:].reshape(group_count, tok_dev,...  31 us
    dot_general x1, matrix products, body(): lax.dot_general(hidden, down_full, (((1,), (1,)), ((), ())), preferred_el...  10.9 us
    all_to_all x1, waiting for transfers between devices, body(): lax.all_to_all(jnp.broadcast_to(new_latents, (span_blocks,) + new_latents...  9.32 us
    all_to_all x1, starting transfers between devices, body(): lax.all_to_all(jnp.tile(prompt_send, (span_blocks, 1, 1)), ('tq', 'tr'),...  8.6 us
    all_to_all x1, waiting for transfers between devices, body(): lax.all_to_all(jnp.tile(prompt_send, (span_blocks, 1, 1)), ('tq', 'tr'),...  8.07 us
    dot_general x1, matrix products, body(): jnp.dot(rows_all, gate_full, preferred_element_type=jnp.float32)  6.36 us
  transfers between devices with their start and end apart: 6, of which 3 were waited for; matrix products, arithmetic and copies ran while one was open for 18% of the time, Pallas kernels for 26%

profile of v6, /device:TPU:8, one launch (start us, length us, event | category | flops | bytes accessed | tf_op | source)
XLA Modules:
  0.0 260.6 jit_solution(3654870937717855725)
XLA Ops:
  7.2 2.0 pad_maximum_fusion.8
  11.7 8.6 %all-to-all-start = ((bf16[32,32,288]{2,1,0:T(8,128)(2,1)}), bf16[32,32,288]{2,1,0:T(8,128)(2,1)}, u32[]{:S(2)}, u32[]{:S(2)}) async-start(bf16[32,32,288]{2,1,0:T(8,128)(2,1)} %bitcast.56), calls=%async_computation | async-start | bytes 1572864 | tf_op jit(solution)/shard_map/all_to_all | solution.py:264
  25.8 1.3 fusion.18
  27.1 2.2 fusion.34
  30.3 8.1 %all-to-all-done = bf16[32,32,288]{2,1,0:T(8,128)(2,1)} async-done(((bf16[32,32,288]{2,1,0:T(8,128)(2,1)}), bf16[32,32,288]{2,1,0:T(8,128)(2,1)}, u32[]{:S(2)}, u32[]{:S(2)}) %all-to-all-start) | async-done | bytes 589856 | tf_op jit(solution)/shard_map/all_to_all | solution.py:264
  39.2 3.5 %all-to-all-start.2 = ((bf16[8,128,288]{1,2,0:T(8,128)(2,1)}), bf16[8,128,288]{1,2,0:T(8,128)(2,1)S(1)}, u32[]{:S(2)}, u32[]{:S(2)}) async-start(bf16[8,128,288]{1,2,0:T(8,128)(2,1)} %broadcast_in_dim.19), calls=%async_computation.2 | async-start | bytes 1179648 | tf_op jit(solution)/shard_map/all_to_all | solution.py:257
  43.4 3.8 %multiply_reduce_fusion = (f32[128]{0:T(128)S(1)}, f32[128,768]{1,0:T(8,128)}) fusion(bf16[2560,768]{1,0:T(8,128)(2,1)} %param.21, bf16[128,2560]{1,0:T(8,128)(2,1)} %param.19, f32[2560]{0:T(1024)S(1)} %convert_element_type.71, f32[128]{0:T(128)} %copy-done.18), kind=kOutput, calls=%fused_computation.39 | convolution fusion | flops 504823680 | bytes 4992000 | tf_op jit(solution)/shard_map/dot_general | solution.py:236
  47.2 1.8 tile.8
  49.0 9.3 %all-to-all-done.2 = bf16[8,128,288]{1,2,0:T(8,128)(2,1)S(1)} async-done(((bf16[8,128,288]{1,2,0:T(8,128)(2,1)}), bf16[8,128,288]{1,2,0:T(8,128)(2,1)S(1)}, u32[]{:S(2)}, u32[]{:S(2)}) %all-to-all-start.2) | async-done | bytes 589856 | tf_op jit(solution)/shard_map/all_to_all | solution.py:257
  58.3 4.6 %all-to-all-start.1 = ((bf16[32,128,288]{1,2,0:T(8,128)(2,1)}), bf16[32,128,288]{1,2,0:T(8,128)(2,1)}, u32[]{:S(2)}, u32[]{:S(2)}) async-start(bf16[32,128,288]{1,2,0:T(8,128)(2,1)} %bitcast.54), calls=%async_computation.1 | async-start | bytes 4718592 | tf_op jit(solution)/shard_map/all_to_all | solution.py:270
  63.0 2.4 convolution_convert_fusion
  65.5 1.3 copy.43
  68.1 1.1 copy.48
  70.3 1.1 copy.49
  73.7 1.6 broadcast_in_dim_reshape.4.lim_row_ref
  75.2 2.2 copy.54
  77.4 1.7 pad_add_fusion.lims_ref
  79.2 1.7 pad_maximum_fusion.1.q_ref
  80.8 1.2 copy.51
  82.0 24.2 %shard_map.194 = (f32[2560,1]{1,0:T(8,128)}, f32[2560,1]{1,0:T(8,128)}, f32[2560,256]{1,0:T(8,128)}) custom-call(s32[2]{0:T(128)} %pad_add_fusion.lims_ref, s32[2560,1]{1,0:T(8,128)} %broadcast_in_dim_reshape.4.lim_row_ref, bf16[2560,288]{1,0:T(8,128)(2,1)} %pad_maximum_fusion.1.q_ref, bf16[1024,288]{1,0:T(8,128)(2,1)} %bitcast.64, ...), custom_call_target="tpu_custom_call" | custom-call | flops 5704253440 | bytes 3964928 | tf_op jit(solution)/shard_map/pallas_call | solution.py:151
  106.2 3.1 %all-to-all-done.1 = bf16[32,128,288]{1,2,0:T(8,128)(2,1)} async-done(((bf16[32,128,288]{1,2,0:T(8,128)(2,1)}), bf16[32,128,288]{1,2,0:T(8,128)(2,1)}, u32[]{:S(2)}, u32[]{:S(2)}) %all-to-all-start.1) | async-done | bytes 2359328 | tf_op jit(solution)/shard_map/all_to_all | solution.py:270
  109.3 4.5 %copy.50 = bf16[32,128,288]{2,1,0:T(8,128)(2,1)} copy(bf16[32,128,288]{1,2,0:T(8,128)(2,1)} %all-to-all-done.1) | data formatting | bytes 4718592 | tf_op jit(solution)/shard_map/all_to_all | solution.py:270
  113.8 44.4 %shard_map.195 = bf16[2560,256]{1,0:T(8,128)(2,1)} custom-call(s32[2]{0:T(128)} %pad_add_fusion.lims_ref, s32[2560,1]{1,0:T(8,128)} %broadcast_in_dim_reshape.4.lim_row_ref, bf16[2560,288]{1,0:T(8,128)(2,1)} %pad_maximum_fusion.1.q_ref, bf16[4096,288]{1,0:T(8,128)(2,1)} %bitcast.57, f32[2560,1]{1,0:T(8,128)} %get-tuple-element.9.refs_1_, ...), custom_call_target="tpu_custom_call" | custom-call | flops 11408506880 | bytes 5144576 | tf_op jit(solution)/shard_map/pallas_call | solution.py:151
  158.2 2.3 reshape.188
  161.5 3.9 %fusion.12 = bf16[128,2560]{1,0:T(8,128)(2,1)S(1)} fusion(bf16[128,1280]{0,1:T(8,128)(2,1)S(1)} %bitcast.63, bf16[1280,2560]{1,0:T(8,128)(2,1)} %param.28, bf16[128,2560]{1,0:T(8,128)(2,1)S(1)} %copy-done.4), kind=kOutput, calls=%fused_computation.13 | convolution fusion | flops 839843840 | bytes 8192000 | tf_op jit(solution)/shard_map/dot_general | solution.py:300
  166.9 31.5 %all_to_all.25 = bf16[4,128,1280]{2,1,0:T(8,128)(2,1)S(1)} all-to-all(bf16[4,128,1280]{2,1,0:T(8,128)(2,1)S(1)} %broadcast_in_dim.20), channel_id=1, replica_groups=mesh['grp'=4,'tq'=8,'tr'=4] {'grp'}, dimensions={0} | all-to-all | bytes 2621440 | tf_op jit(solution)/shard_map/all_to_all | solution.py:313
  198.4 6.4 %fusion.4 = f32[512,800]{0,1:T(8,128)} fusion(bf16[3,2560,800]{2,1,0:T(8,128)(2,1)} %all-gather.3.cloned.1.call-done, bf16[512,1280]{1,0:T(8,128)(2,1)S(1)} %bitcast.61, bf16[512,1280]{1,0:T(8,128)(2,1)} %all-gather.5.cloned.1.call-done), kind=kOutput, calls=%fused_computation.6 | convolution fusion | flops 2102394880 | bytes 8847360 | tf_op jit(solution)/shard_map/dot_general | solution.py:326
  204.8 10.9 %fusion.9 = bf16[512,2560]{1,0:T(8,128)(2,1)} fusion(bf16[3,2560,800]{2,1,0:T(8,128)(2,1)} %all-gather.3.cloned.1.call-done, f32[512,800]{0,1:T(8,128)} %fusion.4, bf16[512,1280]{1,0:T(8,128)(2,1)S(1)} %bitcast.62, bf16[512,1280]{1,0:T(8,128)(2,1)S(1)} %copy-done.19), kind=kOutput, calls=%fused_computation.11 | convolution fusion | flops 4203315200 | bytes 16056320 | tf_op jit(solution)/shard_map/dot_general | solution.py:329
  215.7 2.9 %fusion.45 = (bf16[512,1280]{1,0:T(8,128)(2,1)}, bf16[512,1280]{1,0:T(8,128)(2,1)S(1)}) fusion(bf16[512,2560]{1,0:T(8,128)(2,1)} %fusion.9), kind=kLoop, calls=%fused_computation.76 | loop fusion | bytes 5242880 | tf_op jit(solution)/shard_map/slice | solution.py:336
  218.7 31.0 %all_to_all.26 = bf16[4,128,1280]{2,1,0:T(8,128)(2,1)S(1)} all-to-all(bf16[4,128,1280]{2,1,0:T(8,128)(2,1)S(1)} %bitcast.55), channel_id=1, replica_groups=mesh['grp'=4,'tq'=8,'tr'=4] {'grp'}, dimensions={0} | all-to-all | bytes 2621440 | tf_op jit(solution)/shard_map/all_to_all | solution.py:338
  250.7 1.1 convert_element_type.87
  251.8 2.3 fusion.24
  (99 shorter events, 15.3 us)
Async XLA Ops:
  7.2 55.8 %copy-start = (bf16[768,1920]{1,0:T(8,128)(2,1)S(1)}, bf16[768,1920]{1,0:T(8,128)(2,1)}, u32[]{:S(2)}) copy-start(bf16[768,1920]{1,0:T(8,128)(2,1)} %param.23) | copy-start | bytes 8847364
  7.2 2.2 copy-start.2
  7.2 2.9 %copy-start.11 = (bf16[8,32,288]{2,1,0:T(8,128)(2,1)S(1)}, bf16[8,32,288]{2,1,0:T(8,128)(2,1)}, u32[]{:S(2)}) copy-start(bf16[8,32,288]{2,1,0:T(8,128)(2,1)} %param.34) | copy-start | bytes 442372
  7.2 158.3 %all-gather.3.cloned.1.call-start = ((), (), s32[]{:S(2)}) async-start(), calls=%async_computation.6 | async-start | bytes 14192640 | tf_op jit(solution)/shard_map/all_gather | solution.py:301
  9.3 12.9 %copy-start.20 = (s32[16]{0:T(128)S(1)}, s32[16]{0:T(128)}, u32[]{:S(2)}) copy-start(s32[16]{0:T(128)} %param.35) | copy-start | bytes 196
  9.4 13.4 %copy-start.14 = (bf16[2560]{0:T(1024)(128)(2,1)S(1)}, bf16[2560]{0:T(1024)(128)(2,1)}, u32[]{:S(2)}) copy-start(bf16[2560]{0:T(1024)(128)(2,1)} %param.20) | copy-start | bytes 15364
  9.4 14.1 %copy-start.21 = (s32[8]{0:T(128)S(1)}, s32[8]{0:T(128)}, u32[]{:S(2)}) copy-start(s32[8]{0:T(128)} %param.36) | copy-start | bytes 100
  11.7 26.6 %all-to-all-start = ((bf16[32,32,288]{2,1,0:T(8,128)(2,1)}), bf16[32,32,288]{2,1,0:T(8,128)(2,1)}, u32[]{:S(2)}, u32[]{:S(2)}) async-start(bf16[32,32,288]{2,1,0:T(8,128)(2,1)} %bitcast.56), calls=%async_computation | async-start | bytes 1572864 | tf_op jit(solution)/shard_map/all_to_all | solution.py:264
  22.8 6.6 %copy-start.22 = (bf16[256]{0:T(256)(128)(2,1)S(1)}, bf16[256]{0:T(256)(128)(2,1)}, u32[]{:S(2)}) copy-start(bf16[256]{0:T(256)(128)(2,1)} %param.25) | copy-start | bytes 1540
  27.1 2.3 copy-start.18
  29.3 13.5 %copy-start.17 = (bf16[768]{0:T(1024)(128)(2,1)S(1)}, bf16[768]{0:T(1024)(128)(2,1)}, u32[]{:S(2)}) copy-start(bf16[768]{0:T(1024)(128)(2,1)} %param.22) | copy-start | bytes 4612
  30.3 9.0 %copy-start.9 = (bf16[128,288]{0,1:T(8,128)(2,1)}, bf16[128,288]{0,1:T(8,128)(2,1)S(1)}, u32[]{:S(2)}) copy-start(bf16[128,288]{0,1:T(8,128)(2,1)S(1)} %pad_maximum_fusion.9) | copy-start | bytes 221188
  39.2 19.1 %all-to-all-start.2 = ((bf16[8,128,288]{1,2,0:T(8,128)(2,1)}), bf16[8,128,288]{1,2,0:T(8,128)(2,1)S(1)}, u32[]{:S(2)}, u32[]{:S(2)}) async-start(bf16[8,128,288]{1,2,0:T(8,128)(2,1)} %broadcast_in_dim.19), calls=%async_computation.2 | async-start | bytes 1179648 | tf_op jit(solution)/shard_map/all_to_all | solution.py:257
  43.4 3.8 %copy-start.10 = (bf16[4,128,288]{1,2,0:T(8,128)(2,1)S(1)}, bf16[4,128,288]{1,2,0:T(8,128)(2,1)}, u32[]{:S(2)}) copy-start(bf16[4,128,288]{1,2,0:T(8,128)(2,1)} %param.33) | copy-start | bytes 884740
  58.3 51.0 %all-to-all-start.1 = ((bf16[32,128,288]{1,2,0:T(8,128)(2,1)}), bf16[32,128,288]{1,2,0:T(8,128)(2,1)}, u32[]{:S(2)}, u32[]{:S(2)}) async-start(bf16[32,128,288]{1,2,0:T(8,128)(2,1)} %bitcast.54), calls=%async_computation.1 | async-start | bytes 4718592 | tf_op jit(solution)/shard_map/all_to_all | solution.py:270
  62.9 135.5 %all-gather.5.cloned.1.call-start = ((), (), s32[]{:S(2)}) async-start(), calls=%async_computation.7 | async-start | bytes 1638400 | tf_op jit(solution)/shard_map/all_gather | solution.py:312
  63.0 3.8 %copy-start.12 = (f32[128,16]{0,1:T(8,128)S(1)}, f32[128,16]{0,1:T(8,128)}, u32[]{:S(2)}) copy-start(f32[128,16]{0,1:T(8,128)} %get-tuple-element.22) | copy-start | bytes 24580
  63.0 3.8 %copy-start.13 = (f32[128,16]{0,1:T(8,128)S(1)}, f32[128,16]{0,1:T(8,128)}, u32[]{:S(2)}) copy-start(f32[128,16]{0,1:T(8,128)} %get-tuple-element.23) | copy-start | bytes 24580
  67.2 4.2 %copy-start.7 = (bf16[256,1280]{1,0:T(8,128)(2,1)S(1)}, bf16[256,1280]{1,0:T(8,128)(2,1)}, u32[]{:S(2)}) copy-start(bf16[256,1280]{1,0:T(8,128)(2,1)} %param.26) | copy-start | bytes 1966084
  73.0 0.6 copy-start.16
  73.5 3.9 %copy-start.15 = (bf16[2560]{0:T(1024)(128)(2,1)S(1)}, bf16[2560]{0:T(1024)(128)(2,1)}, u32[]{:S(2)}) copy-start(bf16[2560]{0:T(1024)(128)(2,1)} %param.29) | copy-start | bytes 15364
  73.5 5.6 %copy-start.5 = (bf16[2560,16]{1,0:T(8,128)(2,1)S(1)}, bf16[2560,16]{1,0:T(8,128)(2,1)}, u32[]{:S(2)}) copy-start(bf16[2560,16]{1,0:T(8,128)(2,1)} %copy.48) | copy-start | bytes 245764
  73.5 5.6 %copy-start.6 = (bf16[2560,16]{1,0:T(8,128)(2,1)S(1)}, bf16[2560,16]{1,0:T(8,128)(2,1)}, u32[]{:S(2)}) copy-start(bf16[2560,16]{1,0:T(8,128)(2,1)} %copy.49) | copy-start | bytes 245764
  158.2 2.3 copy-start.8
  160.4 1.1 copy-start.4
  165.4 1.3 copy-start.3
  166.7 84.0 %reduce-scatter.2.cloned.1.call-start = ((), (), s32[]{:S(2)}) async-start(), calls=%async_computation.8 | async-start | bytes 1638400 | tf_op jit(solution)/shard_map/reduce_scatter | solution.py:335
  198.4 6.4 %copy-start.19 = (bf16[512,1280]{1,0:T(8,128)(2,1)S(1)}, bf16[512,1280]{1,0:T(8,128)(2,1)}, u32[]{:S(2)}) copy-start(bf16[512,1280]{1,0:T(8,128)(2,1)} %all-gather.5.cloned.1.call-done) | copy-start | bytes 3932164
  249.7 4.4 %copy-start.1 = (bf16[768,1920]{1,0:T(8,128)(2,1)S(1)}, bf16[768,1920]{1,0:T(8,128)(2,1)}, u32[]{:S(2)}) copy-start(bf16[768,1920]{1,0:T(8,128)(2,1)} %param.23) | copy-start | bytes 8847364
Sparse Core Ops, SparseCore 0:
  10.4 98.1 all-gather.2
  166.9 31.2 all-gather.4
  218.8 31.2 reduce-scatter.1

commit v7 on v5

--- a/solution.py
+++ b/solution.py
@@ -44,7 +44,7 @@
 
 
 KEY_BLOCK = 1024
-ROW_BLOCK = 640
+ROW_BLOCK = 1280
 
 
 def flash_kernel(lims_ref, lim_row_ref, q_ref, *refs, plan, first, final, score_scale, value_width):

time: 262 us -> 259 us (0.989)
  Pallas kernels: 68.4 us -> 65 us
    pallas_call x2, Pallas kernels: 68.4 us -> 65 us  [flash_part(): pl.pallas_call(kernel, grid_spec=pltpu.PrefetchScalarGridSpec(num_scalar_...]
  transfers between devices with their start and end apart: 6 -> 6, of which waited for: 3 -> 3; matrix products, arithmetic and copies ran while one was open for 18% -> 18% of each run, Pallas kernels for 26% -> 25%
where the time goes in v7:
time: 259 us; the launch traced here: 258 us
  Pallas kernels  65 us (25%)
  blocking collectives  62.8 us (24%)
  matrix products  30.7 us (12%)
  local copies, waits for them, and re-layouts  30.1 us (12%)
  waiting for transfers between devices  21.4 us (8%)
  between operations  17.4 us (7%)
  starting transfers between devices  16.9 us (7%)
  other arithmetic  13.8 us (5%)
    pallas_call x2, Pallas kernels, flash_part(): pl.pallas_call(kernel, grid_spec=pltpu.PrefetchScalarGridSpec(num_scalar_...  65 us
    all_to_all x1, blocking collectives, body(): lax.all_to_all(jnp.broadcast_to(post_norm[:, half_width:], (group_count,...  31.8 us
    all_to_all x1, blocking collectives, body(): lax.all_to_all(partial_out[:, half_width:].reshape(group_count, tok_dev,...  31 us
    dot_general x1, matrix products, body(): lax.dot_general(hidden, down_full, (((1,), (1,)), ((), ())), preferred_el...  10.9 us
    all_to_all x1, waiting for transfers between devices, body(): lax.all_to_all(jnp.broadcast_to(new_latents, (span_blocks,) + new_latents...  9.32 us
    all_to_all x1, starting transfers between devices, body(): lax.all_to_all(jnp.tile(prompt_send, (span_blocks, 1, 1)), ('tq', 'tr'),...  8.6 us
    all_to_all x1, waiting for transfers between devices, body(): lax.all_to_all(jnp.tile(prompt_send, (span_blocks, 1, 1)), ('tq', 'tr'),...  8.07 us
    dot_general x1, matrix products, body(): jnp.dot(rows_all, gate_full, preferred_element_type=jnp.float32)  6.36 us
  transfers between devices with their start and end apart: 6, of which 3 were waited for; matrix products, arithmetic and copies ran while one was open for 18% of the time, Pallas kernels for 25%

profile of v7, /device:TPU:8, one launch (start us, length us, event | category | flops | bytes accessed | tf_op | source)
XLA Modules:
  0.0 258.2 jit_solution(2811090478231236629)
XLA Ops:
  7.2 2.0 pad_maximum_fusion.8
  11.7 8.6 %all-to-all-start = ((bf16[32,32,288]{2,1,0:T(8,128)(2,1)}), bf16[32,32,288]{2,1,0:T(8,128)(2,1)}, u32[]{:S(2)}, u32[]{:S(2)}) async-start(bf16[32,32,288]{2,1,0:T(8,128)(2,1)} %bitcast.56), calls=%async_computation | async-start | bytes 1572864 | tf_op jit(solution)/shard_map/all_to_all | solution.py:253
  25.8 1.3 fusion.18
  27.1 2.2 fusion.34
  30.3 8.1 %all-to-all-done = bf16[32,32,288]{2,1,0:T(8,128)(2,1)} async-done(((bf16[32,32,288]{2,1,0:T(8,128)(2,1)}), bf16[32,32,288]{2,1,0:T(8,128)(2,1)}, u32[]{:S(2)}, u32[]{:S(2)}) %all-to-all-start) | async-done | bytes 589856 | tf_op jit(solution)/shard_map/all_to_all | solution.py:253
  39.2 3.5 %all-to-all-start.2 = ((bf16[8,128,288]{1,2,0:T(8,128)(2,1)}), bf16[8,128,288]{1,2,0:T(8,128)(2,1)S(1)}, u32[]{:S(2)}, u32[]{:S(2)}) async-start(bf16[8,128,288]{1,2,0:T(8,128)(2,1)} %broadcast_in_dim.19), calls=%async_computation.2 | async-start | bytes 1179648 | tf_op jit(solution)/shard_map/all_to_all | solution.py:246
  43.4 3.8 %multiply_reduce_fusion = (f32[128]{0:T(128)S(1)}, f32[128,768]{1,0:T(8,128)}) fusion(bf16[2560,768]{1,0:T(8,128)(2,1)} %param.21, bf16[128,2560]{1,0:T(8,128)(2,1)} %param.19, f32[2560]{0:T(1024)S(1)} %convert_element_type.71, f32[128]{0:T(128)} %copy-done.18), kind=kOutput, calls=%fused_computation.39 | convolution fusion | flops 504823680 | bytes 4992000 | tf_op jit(solution)/shard_map/dot_general | solution.py:225
  47.2 1.8 tile.8
  49.0 9.3 %all-to-all-done.2 = bf16[8,128,288]{1,2,0:T(8,128)(2,1)S(1)} async-done(((bf16[8,128,288]{1,2,0:T(8,128)(2,1)}), bf16[8,128,288]{1,2,0:T(8,128)(2,1)S(1)}, u32[]{:S(2)}, u32[]{:S(2)}) %all-to-all-start.2) | async-done | bytes 589856 | tf_op jit(solution)/shard_map/all_to_all | solution.py:246
  58.3 4.6 %all-to-all-start.1 = ((bf16[32,128,288]{1,2,0:T(8,128)(2,1)}), bf16[32,128,288]{1,2,0:T(8,128)(2,1)}, u32[]{:S(2)}, u32[]{:S(2)}) async-start(bf16[32,128,288]{1,2,0:T(8,128)(2,1)} %bitcast.54), calls=%async_computation.1 | async-start | bytes 4718592 | tf_op jit(solution)/shard_map/all_to_all | solution.py:259
  63.0 2.4 convolution_convert_fusion
  65.5 1.3 copy.43
  68.1 1.1 copy.48
  70.3 1.1 copy.49
  73.7 1.6 broadcast_in_dim_reshape.4.lim_row_ref
  75.2 2.2 copy.54
  77.4 1.7 pad_add_fusion.lims_ref
  79.2 1.7 pad_maximum_fusion.1.q_ref
  80.8 1.2 copy.51
  82.0 23.3 %shard_map.194 = (f32[2560,1]{1,0:T(8,128)}, f32[2560,1]{1,0:T(8,128)}, f32[2560,256]{1,0:T(8,128)}) custom-call(s32[2]{0:T(128)} %pad_add_fusion.lims_ref, s32[2560,1]{1,0:T(8,128)} %broadcast_in_dim_reshape.4.lim_row_ref, bf16[2560,288]{1,0:T(8,128)(2,1)} %pad_maximum_fusion.1.q_ref, bf16[1024,288]{1,0:T(8,128)(2,1)} %bitcast.64, ...), custom_call_target="tpu_custom_call" | custom-call | flops 5704253440 | bytes 3964928 | tf_op jit(solution)/shard_map/pallas_call | solution.py:140
  105.3 4.0 %all-to-all-done.1 = bf16[32,128,288]{1,2,0:T(8,128)(2,1)} async-done(((bf16[32,128,288]{1,2,0:T(8,128)(2,1)}), bf16[32,128,288]{1,2,0:T(8,128)(2,1)}, u32[]{:S(2)}, u32[]{:S(2)}) %all-to-all-start.1) | async-done | bytes 2359328 | tf_op jit(solution)/shard_map/all_to_all | solution.py:259
  109.3 4.5 %copy.50 = bf16[32,128,288]{2,1,0:T(8,128)(2,1)} copy(bf16[32,128,288]{1,2,0:T(8,128)(2,1)} %all-to-all-done.1) | data formatting | bytes 4718592 | tf_op jit(solution)/shard_map/all_to_all | solution.py:259
  113.8 41.7 %shard_map.195 = bf16[2560,256]{1,0:T(8,128)(2,1)} custom-call(s32[2]{0:T(128)} %pad_add_fusion.lims_ref, s32[2560,1]{1,0:T(8,128)} %broadcast_in_dim_reshape.4.lim_row_ref, bf16[2560,288]{1,0:T(8,128)(2,1)} %pad_maximum_fusion.1.q_ref, bf16[4096,288]{1,0:T(8,128)(2,1)} %bitcast.57, f32[2560,1]{1,0:T(8,128)} %get-tuple-element.9.refs_1_, ...), custom_call_target="tpu_custom_call" | custom-call | flops 11408506880 | bytes 5144576 | tf_op jit(solution)/shard_map/pallas_call | solution.py:140
  155.5 2.3 reshape.188
  158.9 3.9 %fusion.12 = bf16[128,2560]{1,0:T(8,128)(2,1)S(1)} fusion(bf16[128,1280]{0,1:T(8,128)(2,1)S(1)} %bitcast.63, bf16[1280,2560]{1,0:T(8,128)(2,1)} %param.28, bf16[128,2560]{1,0:T(8,128)(2,1)S(1)} %copy-done.4), kind=kOutput, calls=%fused_computation.13 | convolution fusion | flops 839843840 | bytes 8192000 | tf_op jit(solution)/shard_map/dot_general | solution.py:289
  164.2 31.8 %all_to_all.25 = bf16[4,128,1280]{2,1,0:T(8,128)(2,1)S(1)} all-to-all(bf16[4,128,1280]{2,1,0:T(8,128)(2,1)S(1)} %broadcast_in_dim.20), channel_id=1, replica_groups=mesh['grp'=4,'tq'=8,'tr'=4] {'grp'}, dimensions={0} | all-to-all | bytes 2621440 | tf_op jit(solution)/shard_map/all_to_all | solution.py:302
  196.0 6.4 %fusion.4 = f32[512,800]{0,1:T(8,128)} fusion(bf16[3,2560,800]{2,1,0:T(8,128)(2,1)} %all-gather.3.cloned.1.call-done, bf16[512,1280]{1,0:T(8,128)(2,1)S(1)} %bitcast.61, bf16[512,1280]{1,0:T(8,128)(2,1)} %all-gather.5.cloned.1.call-done), kind=kOutput, calls=%fused_computation.6 | convolution fusion | flops 2102394880 | bytes 8847360 | tf_op jit(solution)/shard_map/dot_general | solution.py:315
  202.4 10.9 %fusion.9 = bf16[512,2560]{1,0:T(8,128)(2,1)} fusion(bf16[3,2560,800]{2,1,0:T(8,128)(2,1)} %all-gather.3.cloned.1.call-done, f32[512,800]{0,1:T(8,128)} %fusion.4, bf16[512,1280]{1,0:T(8,128)(2,1)S(1)} %bitcast.62, bf16[512,1280]{1,0:T(8,128)(2,1)S(1)} %copy-done.19), kind=kOutput, calls=%fused_computation.11 | convolution fusion | flops 4203315200 | bytes 16056320 | tf_op jit(solution)/shard_map/dot_general | solution.py:318
  213.3 2.9 %fusion.45 = (bf16[512,1280]{1,0:T(8,128)(2,1)}, bf16[512,1280]{1,0:T(8,128)(2,1)S(1)}) fusion(bf16[512,2560]{1,0:T(8,128)(2,1)} %fusion.9), kind=kLoop, calls=%fused_computation.76 | loop fusion | bytes 5242880 | tf_op jit(solution)/shard_map/slice | solution.py:325
  216.3 31.0 %all_to_all.26 = bf16[4,128,1280]{2,1,0:T(8,128)(2,1)S(1)} all-to-all(bf16[4,128,1280]{2,1,0:T(8,128)(2,1)S(1)} %bitcast.55), channel_id=1, replica_groups=mesh['grp'=4,'tq'=8,'tr'=4] {'grp'}, dimensions={0} | all-to-all | bytes 2621440 | tf_op jit(solution)/shard_map/all_to_all | solution.py:327
  248.3 1.1 convert_element_type.87
  249.4 2.3 fusion.24
  (99 shorter events, 15.3 us)
Async XLA Ops:
  7.2 55.8 %copy-start = (bf16[768,1920]{1,0:T(8,128)(2,1)S(1)}, bf16[768,1920]{1,0:T(8,128)(2,1)}, u32[]{:S(2)}) copy-start(bf16[768,1920]{1,0:T(8,128)(2,1)} %param.23) | copy-start | bytes 8847364
  7.2 2.2 copy-start.2
  7.2 2.9 %copy-start.11 = (bf16[8,32,288]{2,1,0:T(8,128)(2,1)S(1)}, bf16[8,32,288]{2,1,0:T(8,128)(2,1)}, u32[]{:S(2)}) copy-start(bf16[8,32,288]{2,1,0:T(8,128)(2,1)} %param.34) | copy-start | bytes 442372
  7.2 155.6 %all-gather.3.cloned.1.call-start = ((), (), s32[]{:S(2)}) async-start(), calls=%async_computation.6 | async-start | bytes 14192640 | tf_op jit(solution)/shard_map/all_gather | solution.py:290
  9.3 12.9 %copy-start.20 = (s32[16]{0:T(128)S(1)}, s32[16]{0:T(128)}, u32[]{:S(2)}) copy-start(s32[16]{0:T(128)} %param.35) | copy-start | bytes 196
  9.4 13.4 %copy-start.14 = (bf16[2560]{0:T(1024)(128)(2,1)S(1)}, bf16[2560]{0:T(1024)(128)(2,1)}, u32[]{:S(2)}) copy-start(bf16[2560]{0:T(1024)(128)(2,1)} %param.20) | copy-start | bytes 15364
  9.4 14.1 %copy-start.21 = (s32[8]{0:T(128)S(1)}, s32[8]{0:T(128)}, u32[]{:S(2)}) copy-start(s32[8]{0:T(128)} %param.36) | copy-start | bytes 100
  11.7 26.6 %all-to-all-start = ((bf16[32,32,288]{2,1,0:T(8,128)(2,1)}), bf16[32,32,288]{2,1,0:T(8,128)(2,1)}, u32[]{:S(2)}, u32[]{:S(2)}) async-start(bf16[32,32,288]{2,1,0:T(8,128)(2,1)} %bitcast.56), calls=%async_computation | async-start | bytes 1572864 | tf_op jit(solution)/shard_map/all_to_all | solution.py:253
  22.8 6.6 %copy-start.22 = (bf16[256]{0:T(256)(128)(2,1)S(1)}, bf16[256]{0:T(256)(128)(2,1)}, u32[]{:S(2)}) copy-start(bf16[256]{0:T(256)(128)(2,1)} %param.25) | copy-start | bytes 1540
  27.1 2.3 copy-start.18
  29.3 13.5 %copy-start.17 = (bf16[768]{0:T(1024)(128)(2,1)S(1)}, bf16[768]{0:T(1024)(128)(2,1)}, u32[]{:S(2)}) copy-start(bf16[768]{0:T(1024)(128)(2,1)} %param.22) | copy-start | bytes 4612
  30.3 9.0 %copy-start.9 = (bf16[128,288]{0,1:T(8,128)(2,1)}, bf16[128,288]{0,1:T(8,128)(2,1)S(1)}, u32[]{:S(2)}) copy-start(bf16[128,288]{0,1:T(8,128)(2,1)S(1)} %pad_maximum_fusion.9) | copy-start | bytes 221188
  39.2 19.1 %all-to-all-start.2 = ((bf16[8,128,288]{1,2,0:T(8,128)(2,1)}), bf16[8,128,288]{1,2,0:T(8,128)(2,1)S(1)}, u32[]{:S(2)}, u32[]{:S(2)}) async-start(bf16[8,128,288]{1,2,0:T(8,128)(2,1)} %broadcast_in_dim.19), calls=%async_computation.2 | async-start | bytes 1179648 | tf_op jit(solution)/shard_map/all_to_all | solution.py:246
  43.4 3.8 %copy-start.10 = (bf16[4,128,288]{1,2,0:T(8,128)(2,1)S(1)}, bf16[4,128,288]{1,2,0:T(8,128)(2,1)}, u32[]{:S(2)}) copy-start(bf16[4,128,288]{1,2,0:T(8,128)(2,1)} %param.33) | copy-start | bytes 884740
  58.3 51.0 %all-to-all-start.1 = ((bf16[32,128,288]{1,2,0:T(8,128)(2,1)}), bf16[32,128,288]{1,2,0:T(8,128)(2,1)}, u32[]{:S(2)}, u32[]{:S(2)}) async-start(bf16[32,128,288]{1,2,0:T(8,128)(2,1)} %bitcast.54), calls=%async_computation.1 | async-start | bytes 4718592 | tf_op jit(solution)/shard_map/all_to_all | solution.py:259
  62.9 133.1 %all-gather.5.cloned.1.call-start = ((), (), s32[]{:S(2)}) async-start(), calls=%async_computation.7 | async-start | bytes 1638400 | tf_op jit(solution)/shard_map/all_gather | solution.py:301
  63.0 3.8 %copy-start.12 = (f32[128,16]{0,1:T(8,128)S(1)}, f32[128,16]{0,1:T(8,128)}, u32[]{:S(2)}) copy-start(f32[128,16]{0,1:T(8,128)} %get-tuple-element.22) | copy-start | bytes 24580
  63.0 3.8 %copy-start.13 = (f32[128,16]{0,1:T(8,128)S(1)}, f32[128,16]{0,1:T(8,128)}, u32[]{:S(2)}) copy-start(f32[128,16]{0,1:T(8,128)} %get-tuple-element.23) | copy-start | bytes 24580
  67.2 4.2 %copy-start.7 = (bf16[256,1280]{1,0:T(8,128)(2,1)S(1)}, bf16[256,1280]{1,0:T(8,128)(2,1)}, u32[]{:S(2)}) copy-start(bf16[256,1280]{1,0:T(8,128)(2,1)} %param.26) | copy-start | bytes 1966084
  73.0 0.6 copy-start.16
  73.5 3.9 %copy-start.15 = (bf16[2560]{0:T(1024)(128)(2,1)S(1)}, bf16[2560]{0:T(1024)(128)(2,1)}, u32[]{:S(2)}) copy-start(bf16[2560]{0:T(1024)(128)(2,1)} %param.29) | copy-start | bytes 15364
  73.5 5.6 %copy-start.5 = (bf16[2560,16]{1,0:T(8,128)(2,1)S(1)}, bf16[2560,16]{1,0:T(8,128)(2,1)}, u32[]{:S(2)}) copy-start(bf16[2560,16]{1,0:T(8,128)(2,1)} %copy.48) | copy-start | bytes 245764
  73.5 5.6 %copy-start.6 = (bf16[2560,16]{1,0:T(8,128)(2,1)S(1)}, bf16[2560,16]{1,0:T(8,128)(2,1)}, u32[]{:S(2)}) copy-start(bf16[2560,16]{1,0:T(8,128)(2,1)} %copy.49) | copy-start | bytes 245764
  155.5 2.3 copy-start.8
  157.8 1.1 copy-start.4
  162.8 1.3 copy-start.3
  164.1 84.2 %reduce-scatter.2.cloned.1.call-start = ((), (), s32[]{:S(2)}) async-start(), calls=%async_computation.8 | async-start | bytes 1638400 | tf_op jit(solution)/shard_map/reduce_scatter | solution.py:324
  196.0 6.4 %copy-start.19 = (bf16[512,1280]{1,0:T(8,128)(2,1)S(1)}, bf16[512,1280]{1,0:T(8,128)(2,1)}, u32[]{:S(2)}) copy-start(bf16[512,1280]{1,0:T(8,128)(2,1)} %all-gather.5.cloned.1.call-done) | copy-start | bytes 3932164
  247.3 4.4 %copy-start.1 = (bf16[768,1920]{1,0:T(8,128)(2,1)S(1)}, bf16[768,1920]{1,0:T(8,128)(2,1)}, u32[]{:S(2)}) copy-start(bf16[768,1920]{1,0:T(8,128)(2,1)} %param.23) | copy-start | bytes 8847364
Sparse Core Ops, SparseCore 0:
  10.4 98.1 all-gather.2
  164.2 31.4 all-gather.4
  216.4 31.2 reduce-scatter.1

commit v8 on v7

--- a/solution.py
+++ b/solution.py
@@ -243,38 +243,47 @@
     ).astype(jnp.bfloat16)
     latent_width = new_latents.shape[1]
     span_blocks = lax.axis_size("tq")
-    span_rows = lax.all_to_all(
-        jnp.broadcast_to(new_latents, (span_blocks,) + new_latents.shape), "tq", 0, 0, tiled=True
-    ).reshape(-1, latent_width)
+
     span_lower = jnp.zeros((tok_dev,), jnp.int32)
     span_limit = within + 1
     group_prompts = prompt_of[group_index * group_requests + jnp.arange(group_requests)]
     prompt_send = jnp.take(prompt_latents, group_prompts, axis=0)
-    prompt_rows = lax.all_to_all(
-        jnp.tile(prompt_send, (span_blocks, 1, 1)), ("tq", "tr"), 0, 0, tiled=True
+    cache_rows = lax.all_to_all(
+        jnp.tile(cache_latents, (span_blocks, 1, 1)), ("tq", "tr"), 0, 0, tiled=True
     ).reshape(-1, latent_width)
-    cache_send, _ = lax.optimization_barrier(
-        (jnp.tile(cache_latents, (span_blocks, 1, 1)), prompt_rows)
-    )
-    cache_rows = lax.all_to_all(cache_send, ("tq", "tr"), 0, 0, tiled=True).reshape(
-        -1, latent_width
+    tok_slots = span_blocks * group_requests
+    mates = (jnp.arange(tok_slots) % group_requests == local_request)[:, None, None]
+    span_send = jnp.where(
+        mates, jnp.broadcast_to(new_latents, (tok_slots,) + new_latents.shape), 0
+    ).astype(new_latents.dtype)
+    late_send, _ = lax.optimization_barrier(
+        (jnp.concatenate([jnp.tile(prompt_send, (span_blocks, 1, 1)), span_send], axis=1), cache_rows)
+    )
+    late_rows = lax.all_to_all(late_send, ("tq", "tr"), 0, 0, tiled=True)
+    prompt_piece = prompt_send.shape[1]
+    prompt_rows = late_rows[:, :prompt_piece].reshape(-1, latent_width)
+    span_rows = (
+        late_rows[:, prompt_piece:]
+        .reshape(span_blocks, group_requests, tok_dev, latent_width)
+        .take(local_request, axis=1)
+        .reshape(-1, latent_width)
     )
     query_rows = queries.reshape(tok_dev * HEADS, latent_width)
     score_scale = 1.0 / (NOPE + ROPE) ** 0.5
     lims = jnp.stack([prompt_live, cache_live]).astype(jnp.int32)
     lim_rows = jnp.repeat(span_limit, HEADS)[:, None]
     early_state = flash_part(
+        lims, lim_rows, query_rows, (("cache", cache_rows),), None, False, score_scale, KVR
+    )
+    latent_out = flash_part(
         lims,
         lim_rows,
         query_rows,
         (("span", span_rows), ("prompt", prompt_rows)),
-        None,
-        False,
+        early_state,
+        True,
         score_scale,
         KVR,
-    )
-    latent_out = flash_part(
-        lims, lim_rows, query_rows, (("cache", cache_rows),), early_state, True, score_scale, KVR
     ).reshape(tok_dev, HEADS, KVR)
     heads_out = (
         jnp.einsum(

time: 259 us -> 272 us (1.050)
  waiting for transfers between devices: 21.4 us -> 34.4 us
  matrix products: 30.7 us -> 27.7 us
  local copies, waits for them, and re-layouts: 30.1 us -> 33 us
    all_to_all x3 -> x2, waiting for transfers between devices: 21.4 us -> 34.4 us  [the longest x1 20.9 us: body(): lax.all_to_all(jnp.tile(cache_latents, (span_blocks, 1, 1)), ('tq', 'tr')...]
    slice x0 -> x2, local copies, waits for them, and re-layouts: none -> 4.53 us  [the longest x1 2.4 us: body(): late_rows[:, prompt_piece:]]
    all_to_all x3 -> x2, starting transfers between devices: 16.7 us -> 15 us  [the longest x1 8.74 us: body(): lax.all_to_all(jnp.tile(cache_latents, (span_blocks, 1, 1)), ('tq', 'tr')...]
    all_to_all x2 -> x1, local copies, waits for them, and re-layouts: 5.65 us -> 4.52 us  [body(): lax.all_to_all(jnp.tile(cache_latents, (span_blocks, 1, 1)), ('tq', 'tr')...]
  transfers between devices with their start and end apart: 6 -> 5, of which waited for: 3 -> 2; matrix products, arithmetic and copies ran while one was open for 18% -> 18% of each run, Pallas kernels for 25% -> 24%
where the time goes in v8:
time: 272 us; the launch traced here: 271 us
  Pallas kernels  64.9 us (24%)
  blocking collectives  62.6 us (23%)
  waiting for transfers between devices  34.4 us (13%)
  local copies, waits for them, and re-layouts  33 us (12%)
  matrix products  27.7 us (10%)
  between operations  17.4 us (6%)
  other arithmetic  16.2 us (6%)
  starting transfers between devices  15.3 us (6%)
    pallas_call x2, Pallas kernels, flash_part(): pl.pallas_call(kernel, grid_spec=pltpu.PrefetchScalarGridSpec(num_scalar_...  64.9 us
    all_to_all x1, blocking collectives, body(): lax.all_to_all(jnp.broadcast_to(post_norm[:, half_width:], (group_count,...  31.5 us
    all_to_all x1, blocking collectives, body(): lax.all_to_all(partial_out[:, half_width:].reshape(group_count, tok_dev,...  31 us
    all_to_all x1, waiting for transfers between devices, body(): lax.all_to_all(jnp.tile(cache_latents, (span_blocks, 1, 1)), ('tq', 'tr')...  20.9 us
    all_to_all x1, waiting for transfers between devices, body(): late_rows = lax.all_to_all(late_send, ('tq', 'tr'), 0, 0, tiled=True)  13.5 us
    dot_general x1, matrix products, body(): lax.dot_general(hidden, down_full, (((1,), (1,)), ((), ())), preferred_el...  10.9 us
    all_to_all x1, starting transfers between devices, body(): lax.all_to_all(jnp.tile(cache_latents, (span_blocks, 1, 1)), ('tq', 'tr')...  8.74 us
    dot_general x1, matrix products, body(): jnp.dot(rows_all, gate_full, preferred_element_type=jnp.float32)  6.39 us
  transfers between devices with their start and end apart: 5, of which 2 were waited for; matrix products, arithmetic and copies ran while one was open for 18% of the time, Pallas kernels for 24%

profile of v8, /device:TPU:8, one launch (start us, length us, event | category | flops | bytes accessed | tf_op | source)
XLA Modules:
  0.0 271.4 jit_solution(5561672192356411381)
XLA Ops:
  7.2 2.0 pad_maximum_fusion.9
  9.3 2.8 %tile.20 = bf16[8,4,128,288]{2,3,1,0:T(8,128)(2,1)} broadcast(bf16[4,128,288]{1,2,0:T(8,128)(2,1)} %param.33), dimensions={1,2,3} | broadcast | bytes 2654208 | tf_op jit(solution)/shard_map/tile | solution.py:252
  12.1 8.7 %all-to-all-start = ((bf16[32,128,288]{1,2,0:T(8,128)(2,1)}), bf16[32,128,288]{1,2,0:T(8,128)(2,1)}, u32[]{:S(2)}, u32[]{:S(2)}) async-start(bf16[32,128,288]{1,2,0:T(8,128)(2,1)} %bitcast.57), calls=%async_computation | async-start | bytes 4718592 | tf_op jit(solution)/shard_map/all_to_all | solution.py:251
  26.1 1.3 fusion.18
  27.4 2.2 fusion.34
  31.9 2.5 pad_maximum_fusion
  34.4 1.3 copy-done.6
  35.7 1.5 multiply_reduce_fusion
  37.2 20.9 %all-to-all-done = bf16[32,128,288]{1,2,0:T(8,128)(2,1)} async-done(((bf16[32,128,288]{1,2,0:T(8,128)(2,1)}), bf16[32,128,288]{1,2,0:T(8,128)(2,1)}, u32[]{:S(2)}, u32[]{:S(2)}) %all-to-all-start) | async-done | bytes 2359328 | tf_op jit(solution)/shard_map/all_to_all | solution.py:251
  58.1 4.5 %copy.53 = bf16[32,128,288]{2,1,0:T(8,128)(2,1)} copy(bf16[32,128,288]{1,2,0:T(8,128)(2,1)} %all-to-all-done) | data formatting | bytes 4718592 | tf_op jit(solution)/shard_map/all_to_all | solution.py:251
  62.6 6.2 %all-to-all-start.1 = ((bf16[32,160,288]{2,1,0:T(8,128)(2,1)}), bf16[32,160,288]{2,1,0:T(8,128)(2,1)}, u32[]{:S(2)}, u32[]{:S(2)}) async-start(bf16[32,160,288]{2,1,0:T(8,128)(2,1)} %pad_maximum_fusion), calls=%async_computation.1 | async-start | bytes 7864320 | tf_op jit(solution)/shard_map/all_to_all | solution.py:262
  69.1 1.6 convolution_convert_fusion
  72.3 1.1 copy.50
  74.6 1.1 copy.51
  77.7 1.5 broadcast_in_dim_reshape.4.lim_row_ref
  79.2 2.2 copy.57
  81.4 1.9 pad_add_fusion.lims_ref
  83.3 1.7 pad_maximum_fusion.2.q_ref
  85.0 41.1 %shard_map.194 = (f32[2560,1]{1,0:T(8,128)}, f32[2560,1]{1,0:T(8,128)}, f32[2560,256]{1,0:T(8,128)}) custom-call(s32[2]{0:T(128)} %pad_add_fusion.lims_ref, s32[2560,1]{1,0:T(8,128)} %broadcast_in_dim_reshape.4.lim_row_ref, bf16[2560,288]{1,0:T(8,128)(2,1)} %pad_maximum_fusion.2.q_ref, bf16[4096,288]{1,0:T(8,128)(2,1)} %bitcast.60), custom_call_target="tpu_custom_call" | custom-call | flops 11408506880 | bytes 5144576 | tf_op jit(solution)/shard_map/pallas_call | solution.py:140
  126.1 13.5 %all-to-all-done.1 = bf16[32,160,288]{2,1,0:T(8,128)(2,1)} async-done(((bf16[32,160,288]{2,1,0:T(8,128)(2,1)}), bf16[32,160,288]{2,1,0:T(8,128)(2,1)}, u32[]{:S(2)}, u32[]{:S(2)}) %all-to-all-start.1) | async-done | bytes 2949152 | tf_op jit(solution)/shard_map/all_to_all | solution.py:262
  139.6 2.4 slice.77
  142.0 2.1 slice.78
  145.1 23.8 %shard_map.195 = bf16[2560,256]{1,0:T(8,128)(2,1)} custom-call(s32[2]{0:T(128)} %pad_add_fusion.lims_ref, s32[2560,1]{1,0:T(8,128)} %broadcast_in_dim_reshape.4.lim_row_ref, bf16[2560,288]{1,0:T(8,128)(2,1)} %pad_maximum_fusion.2.q_ref, bf16[1024,288]{1,0:T(8,128)(2,1)} %bitcast.69, bf16[1024,288]{1,0:T(8,128)(2,1)} %bitcast.68, ...), custom_call_target="tpu_custom_call" | custom-call | flops 5704253440 | bytes 3964928 | tf_op jit(solution)/shard_map/pallas_call | solution.py:140
  168.9 2.3 reshape.204
  172.2 3.9 %fusion.12 = bf16[128,2560]{1,0:T(8,128)(2,1)S(1)} fusion(bf16[128,1280]{0,1:T(8,128)(2,1)S(1)} %bitcast.67, bf16[1280,2560]{1,0:T(8,128)(2,1)} %param.28, bf16[128,2560]{1,0:T(8,128)(2,1)S(1)} %copy-done.5), kind=kOutput, calls=%fused_computation.14 | convolution fusion | flops 839843840 | bytes 8192000 | tf_op jit(solution)/shard_map/dot_general | solution.py:298
  177.6 31.5 %all_to_all.20 = bf16[4,128,1280]{2,1,0:T(8,128)(2,1)S(1)} all-to-all(bf16[4,128,1280]{2,1,0:T(8,128)(2,1)S(1)} %broadcast_in_dim.67), channel_id=1, replica_groups=mesh['grp'=4,'tq'=8,'tr'=4] {'grp'}, dimensions={0} | all-to-all | bytes 2621440 | tf_op jit(solution)/shard_map/all_to_all | solution.py:311
  209.1 6.4 %fusion.4 = f32[512,800]{0,1:T(8,128)} fusion(bf16[3,2560,800]{2,1,0:T(8,128)(2,1)} %all-gather.3.cloned.1.call-done, bf16[512,1280]{1,0:T(8,128)(2,1)S(1)} %bitcast.65, bf16[512,1280]{1,0:T(8,128)(2,1)} %all-gather.5.cloned.1.call-done), kind=kOutput, calls=%fused_computation.6 | convolution fusion | flops 2102394880 | bytes 8847360 | tf_op jit(solution)/shard_map/dot_general | solution.py:324
  215.5 10.9 %fusion.9 = bf16[512,2560]{1,0:T(8,128)(2,1)} fusion(bf16[3,2560,800]{2,1,0:T(8,128)(2,1)} %all-gather.3.cloned.1.call-done, f32[512,800]{0,1:T(8,128)} %fusion.4, bf16[512,1280]{1,0:T(8,128)(2,1)S(1)} %bitcast.66, bf16[512,1280]{1,0:T(8,128)(2,1)S(1)} %copy-done.16), kind=kOutput, calls=%fused_computation.11 | convolution fusion | flops 4203315200 | bytes 16056320 | tf_op jit(solution)/shard_map/dot_general | solution.py:327
  226.4 3.0 %fusion.46 = (bf16[512,1280]{1,0:T(8,128)(2,1)}, bf16[512,1280]{1,0:T(8,128)(2,1)S(1)}) fusion(bf16[512,2560]{1,0:T(8,128)(2,1)} %fusion.9), kind=kLoop, calls=%fused_computation.81 | loop fusion | bytes 5242880 | tf_op jit(solution)/shard_map/slice | solution.py:334
  229.4 31.0 %all_to_all.21 = bf16[4,128,1280]{2,1,0:T(8,128)(2,1)S(1)} all-to-all(bf16[4,128,1280]{2,1,0:T(8,128)(2,1)S(1)} %bitcast.58), channel_id=1, replica_groups=mesh['grp'=4,'tq'=8,'tr'=4] {'grp'}, dimensions={0} | all-to-all | bytes 2621440 | tf_op jit(solution)/shard_map/all_to_all | solution.py:336
  261.5 1.1 convert_element_type.89
  262.6 2.3 fusion.24
  (96 shorter events, 13.6 us)
Async XLA Ops:
  7.2 61.9 %copy-start = (bf16[768,1920]{1,0:T(8,128)(2,1)S(1)}, bf16[768,1920]{1,0:T(8,128)(2,1)}, u32[]{:S(2)}) copy-start(bf16[768,1920]{1,0:T(8,128)(2,1)} %param.23) | copy-start | bytes 8847364
  7.2 169.0 %all-gather.3.cloned.1.call-start = ((), (), s32[]{:S(2)}) async-start(), calls=%async_computation.5 | async-start | bytes 14192640 | tf_op jit(solution)/shard_map/all_gather | solution.py:299
  12.1 8.8 %copy-start.2 = (s32[16]{0:T(128)S(1)}, s32[16]{0:T(128)}, u32[]{:S(2)}) copy-start(s32[16]{0:T(128)} %param.37) | copy-start | bytes 196
  12.1 10.7 %copy-start.17 = (s32[16]{0:T(128)S(1)}, s32[16]{0:T(128)}, u32[]{:S(2)}) copy-start(s32[16]{0:T(128)} %param.35) | copy-start | bytes 196
  12.1 11.3 %copy-start.13 = (bf16[2560]{0:T(1024)(128)(2,1)S(1)}, bf16[2560]{0:T(1024)(128)(2,1)}, u32[]{:S(2)}) copy-start(bf16[2560]{0:T(1024)(128)(2,1)} %param.20) | copy-start | bytes 15364
  12.1 11.3 %copy-start.15 = (bf16[768]{0:T(1024)(128)(2,1)S(1)}, bf16[768]{0:T(1024)(128)(2,1)}, u32[]{:S(2)}) copy-start(bf16[768]{0:T(1024)(128)(2,1)} %param.22) | copy-start | bytes 4612
  12.1 11.3 %copy-start.18 = (bf16[256]{0:T(256)(128)(2,1)S(1)}, bf16[256]{0:T(256)(128)(2,1)}, u32[]{:S(2)}) copy-start(bf16[256]{0:T(256)(128)(2,1)} %param.25) | copy-start | bytes 1540
  12.1 12.0 %copy-start.19 = (s32[8]{0:T(128)S(1)}, s32[8]{0:T(128)}, u32[]{:S(2)}) copy-start(s32[8]{0:T(128)} %param.36) | copy-start | bytes 100
  12.1 46.0 %all-to-all-start = ((bf16[32,128,288]{1,2,0:T(8,128)(2,1)}), bf16[32,128,288]{1,2,0:T(8,128)(2,1)}, u32[]{:S(2)}, u32[]{:S(2)}) async-start(bf16[32,128,288]{1,2,0:T(8,128)(2,1)} %bitcast.57), calls=%async_computation | async-start | bytes 4718592 | tf_op jit(solution)/shard_map/all_to_all | solution.py:251
  27.4 3.4 %copy-start.12 = (bf16[8,32,288]{2,1,0:T(8,128)(2,1)S(1)}, bf16[8,32,288]{2,1,0:T(8,128)(2,1)}, u32[]{:S(2)}) copy-start(bf16[8,32,288]{2,1,0:T(8,128)(2,1)} %param.34) | copy-start | bytes 442372
  29.9 1.9 copy-start.11
  31.9 2.5 copy-start.4
  31.9 3.8 %copy-start.6 = (bf16[2560,768]{1,0:T(8,128)(2,1)S(1)}, bf16[2560,768]{1,0:T(8,128)(2,1)}, u32[]{:S(2)}) copy-start(bf16[2560,768]{1,0:T(8,128)(2,1)} %param.21) | copy-start | bytes 11796484
  62.6 77.0 %all-to-all-start.1 = ((bf16[32,160,288]{2,1,0:T(8,128)(2,1)}), bf16[32,160,288]{2,1,0:T(8,128)(2,1)}, u32[]{:S(2)}, u32[]{:S(2)}) async-start(bf16[32,160,288]{2,1,0:T(8,128)(2,1)} %pad_maximum_fusion), calls=%async_computation.1 | async-start | bytes 7864320 | tf_op jit(solution)/shard_map/all_to_all | solution.py:262
  68.8 140.3 %all-gather.5.cloned.1.call-start = ((), (), s32[]{:S(2)}) async-start(), calls=%async_computation.6 | async-start | bytes 1638400 | tf_op jit(solution)/shard_map/all_gather | solution.py:310
  71.4 4.3 %copy-start.9 = (bf16[256,1280]{1,0:T(8,128)(2,1)S(1)}, bf16[256,1280]{1,0:T(8,128)(2,1)}, u32[]{:S(2)}) copy-start(bf16[256,1280]{1,0:T(8,128)(2,1)} %param.26) | copy-start | bytes 1966084
  77.6 3.8 %copy-start.14 = (bf16[2560]{0:T(1024)(128)(2,1)S(1)}, bf16[2560]{0:T(1024)(128)(2,1)}, u32[]{:S(2)}) copy-start(bf16[2560]{0:T(1024)(128)(2,1)} %param.29) | copy-start | bytes 15364
  77.6 5.7 %copy-start.7 = (bf16[2560,16]{1,0:T(8,128)(2,1)S(1)}, bf16[2560,16]{1,0:T(8,128)(2,1)}, u32[]{:S(2)}) copy-start(bf16[2560,16]{1,0:T(8,128)(2,1)} %copy.50) | copy-start | bytes 245764
  77.6 5.7 %copy-start.8 = (bf16[2560,16]{1,0:T(8,128)(2,1)S(1)}, bf16[2560,16]{1,0:T(8,128)(2,1)}, u32[]{:S(2)}) copy-start(bf16[2560,16]{1,0:T(8,128)(2,1)} %copy.51) | copy-start | bytes 245764
  168.9 2.3 copy-start.10
  171.1 1.1 copy-start.5
  176.1 1.3 copy-start.3
  177.5 84.0 %reduce-scatter.2.cloned.1.call-start = ((), (), s32[]{:S(2)}) async-start(), calls=%async_computation.7 | async-start | bytes 1638400 | tf_op jit(solution)/shard_map/reduce_scatter | solution.py:333
  209.1 6.4 %copy-start.16 = (bf16[512,1280]{1,0:T(8,128)(2,1)S(1)}, bf16[512,1280]{1,0:T(8,128)(2,1)}, u32[]{:S(2)}) copy-start(bf16[512,1280]{1,0:T(8,128)(2,1)} %all-gather.5.cloned.1.call-done) | copy-start | bytes 3932164
  260.4 4.4 %copy-start.1 = (bf16[768,1920]{1,0:T(8,128)(2,1)S(1)}, bf16[768,1920]{1,0:T(8,128)(2,1)}, u32[]{:S(2)}) copy-start(bf16[768,1920]{1,0:T(8,128)(2,1)} %param.23) | copy-start | bytes 8847364
Sparse Core Ops, SparseCore 0:
  10.4 127.7 all-gather.2
  177.6 31.2 all-gather.4
  229.5 31.2 reduce-scatter.1

commit v9 on v7

--- a/solution.py
+++ b/solution.py
@@ -250,13 +250,13 @@
     span_limit = within + 1
     group_prompts = prompt_of[group_index * group_requests + jnp.arange(group_requests)]
     prompt_send = jnp.take(prompt_latents, group_prompts, axis=0)
-    prompt_rows = lax.all_to_all(
-        jnp.tile(prompt_send, (span_blocks, 1, 1)), ("tq", "tr"), 0, 0, tiled=True
+    cache_rows = lax.all_to_all(
+        jnp.tile(cache_latents, (span_blocks, 1, 1)), ("tq", "tr"), 0, 0, tiled=True
     ).reshape(-1, latent_width)
-    cache_send, _ = lax.optimization_barrier(
-        (jnp.tile(cache_latents, (span_blocks, 1, 1)), prompt_rows)
-    )
-    cache_rows = lax.all_to_all(cache_send, ("tq", "tr"), 0, 0, tiled=True).reshape(
+    prompt_send, _ = lax.optimization_barrier(
+        (jnp.tile(prompt_send, (span_blocks, 1, 1)), cache_rows)
+    )
+    prompt_rows = lax.all_to_all(prompt_send, ("tq", "tr"), 0, 0, tiled=True).reshape(
         -1, latent_width
     )
     query_rows = queries.reshape(tok_dev * HEADS, latent_width)
@@ -264,17 +264,17 @@
     lims = jnp.stack([prompt_live, cache_live]).astype(jnp.int32)
     lim_rows = jnp.repeat(span_limit, HEADS)[:, None]
     early_state = flash_part(
+        lims, lim_rows, query_rows, (("cache", cache_rows),), None, False, score_scale, KVR
+    )
+    latent_out = flash_part(
         lims,
         lim_rows,
         query_rows,
         (("span", span_rows), ("prompt", prompt_rows)),
-        None,
-        False,
+        early_state,
+        True,
         score_scale,
         KVR,
-    )
-    latent_out = flash_part(
-        lims, lim_rows, query_rows, (("cache", cache_rows),), early_state, True, score_scale, KVR
     ).reshape(tok_dev, HEADS, KVR)
     heads_out = (
         jnp.einsum(

time: 259 us -> 290 us (1.12)
  waiting for transfers between devices: 21.4 us -> 44 us
  local copies, waits for them, and re-layouts: 30.1 us -> 35.5 us
    all_to_all x2, waiting for transfers between devices: 12.1 us -> 33.3 us  [the longest x1 33.3 us: body(): lax.all_to_all(jnp.tile(cache_latents, (span_blocks, 1, 1)), ('tq', 'tr')...]
    all_to_all x1, starting transfers between devices: 3.54 us -> 7.13 us  [body(): lax.all_to_all(jnp.broadcast_to(new_latents, (span_blocks,) + new_latents...]
  transfers between devices with their start and end apart: 6 -> 6, of which waited for: 3 -> 4; matrix products, arithmetic and copies ran while one was open for 18% -> 18% of each run, Pallas kernels for 25% -> 22%
where the time goes in v9:
time: 290 us; the launch traced here: 287 us
  Pallas kernels  64.6 us (22%)
  blocking collectives  61.5 us (21%)
  waiting for transfers between devices  44 us (15%)
  local copies, waits for them, and re-layouts  35.5 us (12%)
  matrix products  30.8 us (11%)
  starting transfers between devices  17.9 us (6%)
  between operations  17.3 us (6%)
  other arithmetic  15.8 us (5%)
    pallas_call x2, Pallas kernels, flash_part(): pl.pallas_call(kernel, grid_spec=pltpu.PrefetchScalarGridSpec(num_scalar_...  64.6 us
    all_to_all x1, waiting for transfers between devices, body(): lax.all_to_all(jnp.tile(cache_latents, (span_blocks, 1, 1)), ('tq', 'tr')...  33.3 us
    all_to_all x1, blocking collectives, body(): lax.all_to_all(partial_out[:, half_width:].reshape(group_count, tok_dev,...  30.8 us
    all_to_all x1, blocking collectives, body(): lax.all_to_all(jnp.broadcast_to(post_norm[:, half_width:], (group_count,...  30.7 us
    dot_general x1, matrix products, body(): lax.dot_general(hidden, down_full, (((1,), (1,)), ((), ())), preferred_el...  10.9 us
    all_to_all x1, waiting for transfers between devices, body(): lax.all_to_all(jnp.broadcast_to(new_latents, (span_blocks,) + new_latents...  8.2 us
    all_to_all x1, starting transfers between devices, body(): lax.all_to_all(jnp.broadcast_to(new_latents, (span_blocks,) + new_latents...  7.13 us
    dot_general x1, matrix products, body(): jnp.dot(rows_all, gate_full, preferred_element_type=jnp.float32)  6.39 us
  transfers between devices with their start and end apart: 6, of which 4 were waited for; matrix products, arithmetic and copies ran while one was open for 18% of the time, Pallas kernels for 22%

profile of v9, /device:TPU:8, one launch (start us, length us, event | category | flops | bytes accessed | tf_op | source)
XLA Modules:
  0.0 287.5 jit_solution(17086964490451633102)
XLA Ops:
  7.2 2.1 pad_maximum_fusion.8
  9.3 1.2 dynamic_slice.9
  11.9 1.3 dynamic_slice.11
  15.1 1.3 dynamic_slice.10
  18.2 1.3 fusion.18
  19.5 2.2 fusion.34
  24.2 7.1 %all-to-all-start = ((bf16[8,128,288]{1,2,0:T(8,128)(2,1)}), bf16[8,128,288]{1,2,0:T(8,128)(2,1)S(1)}, u32[]{:S(2)}, u32[]{:S(2)}) async-start(bf16[8,128,288]{1,2,0:T(8,128)(2,1)} %broadcast_in_dim.14), calls=%async_computation | async-start | bytes 1179648 | tf_op jit(solution)/shard_map/all_to_all | solution.py:246
  31.9 3.9 %multiply_reduce_fusion = (f32[128]{0:T(128)S(1)}, f32[128,768]{1,0:T(8,128)}) fusion(bf16[2560,768]{1,0:T(8,128)(2,1)} %param.21, bf16[128,2560]{1,0:T(8,128)(2,1)} %param.19, f32[2560]{0:T(1024)S(1)} %convert_element_type.71, f32[128]{0:T(128)} %copy-done.16), kind=kOutput, calls=%fused_computation.39 | convolution fusion | flops 504823680 | bytes 4992000 | tf_op jit(solution)/shard_map/dot_general | solution.py:225
  36.3 8.2 %all-to-all-done = bf16[8,128,288]{1,2,0:T(8,128)(2,1)S(1)} async-done(((bf16[8,128,288]{1,2,0:T(8,128)(2,1)}), bf16[8,128,288]{1,2,0:T(8,128)(2,1)S(1)}, u32[]{:S(2)}, u32[]{:S(2)}) %all-to-all-start) | async-done | bytes 589856 | tf_op jit(solution)/shard_map/all_to_all | solution.py:246
  44.5 2.7 tile.20
  47.3 5.5 %all-to-all-start.1 = ((bf16[32,128,288]{1,2,0:T(8,128)(2,1)}), bf16[32,128,288]{1,2,0:T(8,128)(2,1)}, u32[]{:S(2)}, u32[]{:S(2)}) async-start(bf16[32,128,288]{1,2,0:T(8,128)(2,1)} %bitcast.54), calls=%async_computation.1 | async-start | bytes 4718592 | tf_op jit(solution)/shard_map/all_to_all | solution.py:253
  52.8 2.4 convolution_convert_fusion
  55.2 1.3 copy.43
  63.4 1.5 broadcast_in_dim_reshape.4.lim_row_ref
  65.6 2.2 copy.54
  67.8 1.5 gather_fusion.1
  69.3 1.9 pad_add_fusion.lims_ref
  71.3 1.7 pad_maximum_fusion.1.q_ref
  74.2 33.3 %all-to-all-done.1 = bf16[32,128,288]{1,2,0:T(8,128)(2,1)} async-done(((bf16[32,128,288]{1,2,0:T(8,128)(2,1)}), bf16[32,128,288]{1,2,0:T(8,128)(2,1)}, u32[]{:S(2)}, u32[]{:S(2)}) %all-to-all-start.1) | async-done | bytes 2359328 | tf_op jit(solution)/shard_map/all_to_all | solution.py:253
  107.5 4.5 %copy.51 = bf16[32,128,288]{2,1,0:T(8,128)(2,1)} copy(bf16[32,128,288]{1,2,0:T(8,128)(2,1)} %all-to-all-done.1) | data formatting | bytes 4718592 | tf_op jit(solution)/shard_map/all_to_all | solution.py:253
  112.9 5.0 %all-to-all-start.2 = ((bf16[32,32,288]{2,1,0:T(8,128)(2,1)}), bf16[32,32,288]{2,1,0:T(8,128)(2,1)S(1)}, u32[]{:S(2)}, u32[]{:S(2)}) async-start(bf16[32,32,288]{2,1,0:T(8,128)(2,1)} %bitcast.9), calls=%async_computation.2 | async-start | bytes 1572864 | tf_op jit(solution)/shard_map/all_to_all | solution.py:259
  118.2 41.1 %shard_map.194 = (f32[2560,1]{1,0:T(8,128)}, f32[2560,1]{1,0:T(8,128)}, f32[2560,256]{1,0:T(8,128)}) custom-call(s32[2]{0:T(128)} %pad_add_fusion.lims_ref, s32[2560,1]{1,0:T(8,128)} %broadcast_in_dim_reshape.4.lim_row_ref, bf16[2560,288]{1,0:T(8,128)(2,1)} %pad_maximum_fusion.1.q_ref, bf16[4096,288]{1,0:T(8,128)(2,1)} %bitcast.56), custom_call_target="tpu_custom_call" | custom-call | flops 11408506880 | bytes 5144576 | tf_op jit(solution)/shard_map/pallas_call | solution.py:140
  160.2 23.5 %shard_map.195 = bf16[2560,256]{1,0:T(8,128)(2,1)} custom-call(s32[2]{0:T(128)} %pad_add_fusion.lims_ref, s32[2560,1]{1,0:T(8,128)} %broadcast_in_dim_reshape.4.lim_row_ref, bf16[2560,288]{1,0:T(8,128)(2,1)} %pad_maximum_fusion.1.q_ref, bf16[1024,288]{1,0:T(8,128)(2,1)} %bitcast.64, bf16[1024,288]{1,0:T(8,128)(2,1)} %bitcast.63, ...), custom_call_target="tpu_custom_call" | custom-call | flops 5704253440 | bytes 3964928 | tf_op jit(solution)/shard_map/pallas_call | solution.py:140
  183.7 2.3 reshape.188
  187.1 3.9 %fusion.12 = bf16[128,2560]{1,0:T(8,128)(2,1)S(1)} fusion(bf16[128,1280]{0,1:T(8,128)(2,1)S(1)} %bitcast.62, bf16[1280,2560]{1,0:T(8,128)(2,1)} %param.28, bf16[128,2560]{1,0:T(8,128)(2,1)S(1)} %copy-done.4), kind=kOutput, calls=%fused_computation.13 | convolution fusion | flops 839843840 | bytes 8192000 | tf_op jit(solution)/shard_map/dot_general | solution.py:289
  192.5 30.7 %all_to_all.25 = bf16[4,128,1280]{2,1,0:T(8,128)(2,1)S(1)} all-to-all(bf16[4,128,1280]{2,1,0:T(8,128)(2,1)S(1)} %broadcast_in_dim.20), channel_id=1, replica_groups=mesh['grp'=4,'tq'=8,'tr'=4] {'grp'}, dimensions={0} | all-to-all | bytes 2621440 | tf_op jit(solution)/shard_map/all_to_all | solution.py:302
  223.2 2.1 all-gather.5.cloned.1.call-done
  225.3 6.4 %fusion.4 = f32[512,800]{0,1:T(8,128)} fusion(bf16[3,2560,800]{2,1,0:T(8,128)(2,1)} %all-gather.3.cloned.1.call-done, bf16[512,1280]{1,0:T(8,128)(2,1)S(1)} %bitcast.60, bf16[512,1280]{1,0:T(8,128)(2,1)} %all-gather.5.cloned.1.call-done), kind=kOutput, calls=%fused_computation.6 | convolution fusion | flops 2102394880 | bytes 8847360 | tf_op jit(solution)/shard_map/dot_general | solution.py:315
  231.7 10.9 %fusion.9 = bf16[512,2560]{1,0:T(8,128)(2,1)} fusion(bf16[3,2560,800]{2,1,0:T(8,128)(2,1)} %all-gather.3.cloned.1.call-done, f32[512,800]{0,1:T(8,128)} %fusion.4, bf16[512,1280]{1,0:T(8,128)(2,1)S(1)} %bitcast.61, bf16[512,1280]{1,0:T(8,128)(2,1)S(1)} %copy-done.17), kind=kOutput, calls=%fused_computation.11 | convolution fusion | flops 4203315200 | bytes 16056320 | tf_op jit(solution)/shard_map/dot_general | solution.py:318
  242.6 3.0 %fusion.45 = (bf16[512,1280]{1,0:T(8,128)(2,1)}, bf16[512,1280]{1,0:T(8,128)(2,1)S(1)}) fusion(bf16[512,2560]{1,0:T(8,128)(2,1)} %fusion.9), kind=kLoop, calls=%fused_computation.76 | loop fusion | bytes 5242880 | tf_op jit(solution)/shard_map/slice | solution.py:325
  245.6 30.8 %all_to_all.26 = bf16[4,128,1280]{2,1,0:T(8,128)(2,1)S(1)} all-to-all(bf16[4,128,1280]{2,1,0:T(8,128)(2,1)S(1)} %bitcast.55), channel_id=1, replica_groups=mesh['grp'=4,'tq'=8,'tr'=4] {'grp'}, dimensions={0} | all-to-all | bytes 2621440 | tf_op jit(solution)/shard_map/all_to_all | solution.py:327
  278.7 2.3 fusion.24
  (89 shorter events, 21.2 us)
Async XLA Ops:
  7.2 45.6 %copy-start = (bf16[768,1920]{1,0:T(8,128)(2,1)S(1)}, bf16[768,1920]{1,0:T(8,128)(2,1)}, u32[]{:S(2)}) copy-start(bf16[768,1920]{1,0:T(8,128)(2,1)} %param.23) | copy-start | bytes 8847364
  7.2 183.9 %all-gather.3.cloned.1.call-start = ((), (), s32[]{:S(2)}) async-start(), calls=%async_computation.6 | async-start | bytes 14192640 | tf_op jit(solution)/shard_map/all_gather | solution.py:290
  19.5 4.6 %copy-start.16 = (f32[128]{0:T(128)}, f32[128]{0:T(128)S(1)}, u32[]{:S(2)}) copy-start(f32[128]{0:T(128)S(1)} %add_rsqrt_fusion.3) | copy-start | bytes 1540
  21.7 9.6 %copy-start.15 = (bf16[768]{0:T(1024)(128)(2,1)S(1)}, bf16[768]{0:T(1024)(128)(2,1)}, u32[]{:S(2)}) copy-start(bf16[768]{0:T(1024)(128)(2,1)} %param.22) | copy-start | bytes 4612
  22.6 0.6 copy-start.10
  24.2 20.4 %all-to-all-start = ((bf16[8,128,288]{1,2,0:T(8,128)(2,1)}), bf16[8,128,288]{1,2,0:T(8,128)(2,1)S(1)}, u32[]{:S(2)}, u32[]{:S(2)}) async-start(bf16[8,128,288]{1,2,0:T(8,128)(2,1)} %broadcast_in_dim.14), calls=%async_computation | async-start | bytes 1179648 | tf_op jit(solution)/shard_map/all_to_all | solution.py:246
  47.3 60.2 %all-to-all-start.1 = ((bf16[32,128,288]{1,2,0:T(8,128)(2,1)}), bf16[32,128,288]{1,2,0:T(8,128)(2,1)}, u32[]{:S(2)}, u32[]{:S(2)}) async-start(bf16[32,128,288]{1,2,0:T(8,128)(2,1)} %bitcast.54), calls=%async_computation.1 | async-start | bytes 4718592 | tf_op jit(solution)/shard_map/all_to_all | solution.py:253
  52.8 3.8 %copy-start.11 = (f32[128,16]{0,1:T(8,128)S(1)}, f32[128,16]{0,1:T(8,128)}, u32[]{:S(2)}) copy-start(f32[128,16]{0,1:T(8,128)} %get-tuple-element.22) | copy-start | bytes 24580
  52.8 3.8 %copy-start.12 = (f32[128,16]{0,1:T(8,128)S(1)}, f32[128,16]{0,1:T(8,128)}, u32[]{:S(2)}) copy-start(f32[128,16]{0,1:T(8,128)} %get-tuple-element.23) | copy-start | bytes 24580
  56.9 4.2 %copy-start.8 = (bf16[256,1280]{1,0:T(8,128)(2,1)S(1)}, bf16[256,1280]{1,0:T(8,128)(2,1)}, u32[]{:S(2)}) copy-start(bf16[256,1280]{1,0:T(8,128)(2,1)} %param.26) | copy-start | bytes 1966084
  62.7 0.6 copy-start.14
  62.7 2.2 copy-start.2
  63.3 4.4 %copy-start.13 = (bf16[2560]{0:T(1024)(128)(2,1)S(1)}, bf16[2560]{0:T(1024)(128)(2,1)}, u32[]{:S(2)}) copy-start(bf16[2560]{0:T(1024)(128)(2,1)} %param.29) | copy-start | bytes 15364
  63.4 7.8 %copy-start.5 = (bf16[2560,16]{1,0:T(8,128)(2,1)S(1)}, bf16[2560,16]{1,0:T(8,128)(2,1)}, u32[]{:S(2)}) copy-start(bf16[2560,16]{1,0:T(8,128)(2,1)} %copy.48) | copy-start | bytes 245764
  63.4 7.8 %copy-start.6 = (bf16[2560,16]{1,0:T(8,128)(2,1)S(1)}, bf16[2560,16]{1,0:T(8,128)(2,1)}, u32[]{:S(2)}) copy-start(bf16[2560,16]{1,0:T(8,128)(2,1)} %copy.49) | copy-start | bytes 245764
  112.9 46.3 %all-to-all-start.2 = ((bf16[32,32,288]{2,1,0:T(8,128)(2,1)}), bf16[32,32,288]{2,1,0:T(8,128)(2,1)S(1)}, u32[]{:S(2)}, u32[]{:S(2)}) async-start(bf16[32,32,288]{2,1,0:T(8,128)(2,1)} %bitcast.9), calls=%async_computation.2 | async-start | bytes 1572864 | tf_op jit(solution)/shard_map/all_to_all | solution.py:259
  118.0 107.4 %all-gather.5.cloned.1.call-start = ((), (), s32[]{:S(2)}) async-start(), calls=%async_computation.7 | async-start | bytes 1638400 | tf_op jit(solution)/shard_map/all_gather | solution.py:301
  159.3 0.9 copy-start.7
  183.7 2.3 copy-start.9
  186.0 1.1 copy-start.4
  191.0 1.3 copy-start.3
  192.3 85.3 %reduce-scatter.2.cloned.1.call-start = ((), (), s32[]{:S(2)}) async-start(), calls=%async_computation.8 | async-start | bytes 1638400 | tf_op jit(solution)/shard_map/reduce_scatter | solution.py:324
  225.3 6.4 %copy-start.17 = (bf16[512,1280]{1,0:T(8,128)(2,1)S(1)}, bf16[512,1280]{1,0:T(8,128)(2,1)}, u32[]{:S(2)}) copy-start(bf16[512,1280]{1,0:T(8,128)(2,1)} %all-gather.5.cloned.1.call-done) | copy-start | bytes 3932164
  276.4 4.5 %copy-start.1 = (bf16[768,1920]{1,0:T(8,128)(2,1)S(1)}, bf16[768,1920]{1,0:T(8,128)(2,1)}, u32[]{:S(2)}) copy-start(bf16[768,1920]{1,0:T(8,128)(2,1)} %param.23) | copy-start | bytes 8847364
Sparse Core Ops, SparseCore 0:
  10.4 96.4 all-gather.2
  192.4 32.8 all-gather.4
  245.7 31.9 reduce-scatter.1
